TPU v7x, 256 devices: a whole 4x4x8 slice. The times are simulated.
256 devices in a mesh: dp: 32 (over z, x), tensor: 8 (over y, core).
Axes of the slice: x: 4, y: 4, z: 8, core: 2. Of those that a mesh axis runs over, the one named last changes fastest.
Arguments:
- gradients: float32 [32, 2368, 1024], P('dp', None, 'tensor'), may hold values from -96 to 96
- weights: float32 [2368, 1024], P(None, 'tensor'), may hold values from -64 to 64
- first_moment: float32 [2368, 1024], P(None, 'tensor'), may hold values from -64 to 64
- second_moment: float32 [2368, 1024], P(None, 'tensor'), may hold values from 0.05 to 2
Outputs:
- weights_new: float32 [2368, 1024], P(None, 'tensor')
- first_new: float32 [2368, 1024], P(None, 'tensor')
- second_new: float32 [2368, 1024], P(None, 'tensor')
- copies: bfloat16 [2368, 1024], replicated
- ratios: float32 [4], replicated
All inputs are finite; a program needn't handle non-finite values.
Results may differ from a plain program's by a relative error of at most 0.0004.
Values may be sent and summed in bfloat16 or wider, within the bound.
No kernel may reach another device: no remote copies, remote signals or barrier semaphores. Data moves between devices by JAX's collectives and lax.ppermute only.
A program may use at most 64 MiB of HBM per device.

v0:
```python
import jax
import jax.numpy as jnp
from jax import lax
from jax.sharding import PartitionSpec as P

D = 1024
HID = 1342


beta_one = 0.9
beta_two = 0.999
correct_one = 1.0 - 0.9**20
correct_two = 1.0 - 0.999**20
epsilon = 1e-06
learn_rate = 0.01
decay_rate = 0.01


def group_table(row_count):
    row_ids = lax.broadcasted_iota(jnp.int32, (row_count, 4), 0)
    which = lax.broadcasted_iota(jnp.int32, (row_count, 4), 1)
    group = jnp.where(row_ids < D, 0, jnp.where(row_ids < D + HID, 1, row_ids - D - HID + 2))
    return (group == which).astype(jnp.float32)


def group_squares(values, seg_table):
    row_sums = jnp.sum(values * values, axis=1)
    return jnp.dot(row_sums, seg_table, precision=lax.Precision.HIGHEST)


def adam_part(grad, weights, first_moment, second_moment, seg_table):
    first_new = beta_one * first_moment + (1.0 - beta_one) * grad
    second_new = beta_two * second_moment + (1.0 - beta_two) * grad * grad
    decay = decay_rate * (seg_table[:, 0] + seg_table[:, 1])
    update = (
        first_new / correct_one / (jnp.sqrt(second_new / correct_two) + epsilon)
        + decay[:, None] * weights
    )
    return (first_new, second_new, update)


def apply_ratios(weights, update, seg_table, weight_total, step_total):
    ratios = jnp.sqrt(weight_total) / jnp.sqrt(step_total)
    row_ratio = jnp.dot(seg_table, ratios, precision=lax.Precision.HIGHEST)
    return (weights - learn_rate * row_ratio[:, None] * update, ratios)


def shards(gradients, weights, first_moment, second_moment):
    local_grad = gradients[0]
    row_count = weights.shape[0]
    seg_table = group_table(row_count)
    grad = lax.psum(local_grad, "dp") / lax.axis_size("dp")
    first_new, second_new, update = adam_part(grad, weights, first_moment, second_moment, seg_table)
    step_local = group_squares(update, seg_table)
    weight_total, step_total = lax.psum((group_squares(weights, seg_table), step_local), "tensor")
    weights_new, ratios = apply_ratios(weights, update, seg_table, weight_total, step_total)
    copies = lax.all_gather(weights_new.astype(jnp.bfloat16), "tensor", axis=1, tiled=True)
    return (weights_new, first_new, second_new, copies, ratios)


def solution(mesh):
    return jax.shard_map(
        shards,
        mesh=mesh,
        in_specs=(P("dp", None, "tensor"), P(None, "tensor"), P(None, "tensor"), P(None, "tensor")),
        out_specs=(P(None, "tensor"), P(None, "tensor"), P(None, "tensor"), P(), P()),
        check_vma=False,
    )
```

profile of v0, /device:TPU:1, one launch (start us, length us, event | category | flops | bytes accessed | tf_op | source)
XLA Modules:
  0.0 233.5 jit_solution(6003623145983622729)
XLA Ops:
  7.2 0.0 copy-start
  7.2 0.0 all-reduce.3.cloned.1.call-start
  7.2 0.7 all-reduce.3.cloned.1.call-update
  7.9 0.0 all-gather.2.cloned.1.call-start
  8.1 153.3 %all-reduce.3.cloned.1.call-done = f32[2368,128]{1,0:T(8,128)} async-done(((f32[2368,128]{1,0:T(8,128)}), f32[2368,128]{1,0:T(8,128)}) %all-reduce.3.cloned.1.call-update) | async-done | bytes 1212432 | tf_op jit(solution)/shard_map/psum | solution.py:52
  161.4 0.0 copy-done
  161.4 4.3 %multiply_reduce_fusion = (f32[2368]{0:T(1024)S(1)}, f32[2368,128]{1,0:T(8,128)S(1)}, f32[2368,128]{1,0:T(8,128)}, f32[2368,128]{1,0:T(8,128)}, f32[2368]{0:T(1024)S(1)}) fusion(f32[2368,128]{1,0:T(8,128)S(1)} %copy-done, f32[2368]{0:T(1024)S(1)} %fusion.1, f32[2368,128]{1,0:T(8,128)} %all-reduce.3.cloned.1.call-done, f32[2368,128]{1,0:T(8,128)} %param.6, ...), kind=kLoop, calls=%fused_computation.1 | loop fusion | flops 5451136 | bytes 8515328 | tf_op jit(solution)/shard_map/reduce_sum | solution.py:27
  165.7 0.1 convolution_bitcast_fusion
  165.9 0.2 convolution_bitcast_fusion.1
  166.1 17.5 %all-reduce = (f32[4]{0:T(128)S(1)}, f32[4]{0:T(128)S(1)}) all-reduce(f32[4]{0:T(128)S(1)} %convolution_bitcast_fusion, f32[4]{0:T(128)S(1)} %convolution_bitcast_fusion.1), channel_id=1, replica_groups=mesh['dp'=32,'tensor'=8] {'tensor'}, use_global_device_ids=true, to_apply=%region_4.5 | all-reduce | flops 8 | bytes 64 | tf_op jit(solution)/shard_map/psum | solution.py:55
  183.6 0.0 copy-start.1
  183.6 0.2 convolution_reduce_fusion
  183.8 1.6 fusion.3
  185.4 0.0 copy-done.1
  185.4 0.0 all-gather.2.cloned.1.call-update
  185.4 36.1 %all-gather.2.cloned.1.call-done = bf16[2368,1024]{1,0:T(8,128)(2,1)} async-done(((bf16[2368,128]{1,0:T(8,128)(2,1)}), bf16[2368,1024]{1,0:T(8,128)(2,1)}) %all-gather.2.cloned.1.call-update) | async-done | bytes 4849680 | tf_op jit(solution)/shard_map/all_gather | solution.py:57
  221.5 5.1 %copy.12 = bf16[2368,1024]{1,0:T(8,128)(2,1)} copy(bf16[2368,1024]{1,0:T(8,128)(2,1)} %all-gather.2.cloned.1.call-done) | data formatting | bytes 9699328
  (8 shorter events, 0.1 us)
Async XLA Ops:
  7.2 154.2 %copy-start = (f32[2368,128]{1,0:T(8,128)S(1)}, f32[2368,128]{1,0:T(8,128)}, u32[]{:S(2)}) copy-start(f32[2368,128]{1,0:T(8,128)} %param.5) | copy-start | bytes 3637252
  7.2 154.2 %all-reduce.3.cloned.1.call-start = ((), (), s32[]{:S(2)}) async-start(), calls=%async_computation | async-start | bytes 2424832 | tf_op jit(solution)/shard_map/psum | solution.py:52
  7.9 213.6 %all-gather.2.cloned.1.call-start = ((), (), s32[]{:S(2)}) async-start(), calls=%async_computation.1 | async-start | bytes 5455872 | tf_op jit(solution)/shard_map/all_gather | solution.py:57
  183.6 1.8 copy-start.1
Sparse Core Ops, SparseCore 0:
  11.4 149.9 all-reduce.2
  185.6 35.8 all-gather.1
where the time goes:
time: 234 us; the launch traced here: 233 us
  waiting for transfers between devices  190 us (81%)
  blocking collectives  17.5 us (7%)
  between operations  14.1 us (6%)
  other arithmetic  6.02 us (3%)
  local copies, waits for them, and re-layouts  5.15 us (2%)
    psum x1, waiting for transfers between devices, shards(): grad = lax.psum(local_grad, 'dp') / lax.axis_size('dp')  153 us
    all_gather x1, waiting for transfers between devices, shards(): lax.all_gather(weights_new.astype(jnp.bfloat16), 'tensor', axis=1, tiled=...  36.1 us
    psum x1, blocking collectives, shards(): lax.psum((group_squares(weights, seg_table), step_local), 'tensor')  17.5 us
    unnamed x5, local copies, waits for them, and re-layouts  5.13 us
  transfers between devices with their start and end apart: 2, of which 2 were waited for; matrix products, arithmetic and copies ran while one was open for 0% of the time, Pallas kernels for 0%

commit v1 on v0

--- a/solution.py
+++ b/solution.py
@@ -1,6 +1,8 @@
 import jax
 import jax.numpy as jnp
+import numpy as np
 from jax import lax
+from jax.sharding import Mesh
 from jax.sharding import PartitionSpec as P
 
 D = 1024
@@ -14,6 +16,9 @@
 epsilon = 1e-06
 learn_rate = 0.01
 decay_rate = 0.01
+
+DP = ("z", "x")
+TN = ("y", "core")
 
 
 def group_table(row_count):
@@ -45,24 +50,62 @@
     return (weights - learn_rate * row_ratio[:, None] * update, ratios)
 
 
-def shards(gradients, weights, first_moment, second_moment):
-    local_grad = gradients[0]
-    row_count = weights.shape[0]
-    seg_table = group_table(row_count)
-    grad = lax.psum(local_grad, "dp") / lax.axis_size("dp")
-    first_new, second_new, update = adam_part(grad, weights, first_moment, second_moment, seg_table)
-    step_local = group_squares(update, seg_table)
-    weight_total, step_total = lax.psum((group_squares(weights, seg_table), step_local), "tensor")
-    weights_new, ratios = apply_ratios(weights, update, seg_table, weight_total, step_total)
-    copies = lax.all_gather(weights_new.astype(jnp.bfloat16), "tensor", axis=1, tiled=True)
-    return (weights_new, first_new, second_new, copies, ratios)
+def dp_sum(x, nz, nx):
+    rows, cols = x.shape
+    unit = 8 * nz * nx
+    padded = -(-rows // unit) * unit
+    y = jnp.pad(x, ((0, padded - rows), (0, 0)))
+    y = lax.all_to_all(y.reshape(nx, padded // nx, cols), "x", 0, 0, tiled=False).sum(0)
+    y = lax.all_to_all(y.reshape(nz, padded // (nx * nz), cols), "z", 0, 0, tiled=False).sum(0)
+    y = lax.all_to_all(jnp.broadcast_to(y[None], (nz,) + y.shape), "z", 0, 0, tiled=False)
+    y = y.reshape(padded // nx, cols)
+    y = lax.all_to_all(jnp.broadcast_to(y[None], (nx,) + y.shape), "x", 0, 0, tiled=False)
+    return y.reshape(padded, cols)[:rows]
+
+
+def tensor_sum(v, ny, ncore):
+    for axis, size in (("core", ncore), ("y", ny)):
+        step = 1
+        while step < size:
+            v = v + lax.ppermute(v, axis, [(i, i ^ step) for i in range(size)])
+            step *= 2
+    return v
+
+
+def make_shards(nz, nx, ny, ncore):
+    def shards(gradients, weights, first_moment, second_moment):
+        local_grad = gradients[0]
+        row_count = weights.shape[0]
+        seg_table = group_table(row_count)
+        grad = dp_sum(local_grad, nz, nx) / (nz * nx)
+        first_new, second_new, update = adam_part(grad, weights, first_moment, second_moment, seg_table)
+        both = jnp.concatenate([group_squares(weights, seg_table), group_squares(update, seg_table)])
+        both = tensor_sum(both, ny, ncore)
+        weight_total, step_total = both[:4], both[4:]
+        weights_new, ratios = apply_ratios(weights, update, seg_table, weight_total, step_total)
+        copies = lax.all_gather(weights_new.astype(jnp.bfloat16), TN, axis=1, tiled=True)
+        return (weights_new, first_new, second_new, copies, ratios)
+
+    return shards
+
+
+def physical_mesh(mesh):
+    devices = mesh.devices
+    dp_devices = devices[:, 0]
+    nx = len({d.coords[0] for d in dp_devices})
+    nz = dp_devices.size // nx
+    tn_devices = devices[0, :]
+    ncore = len({d.core_on_chip for d in tn_devices})
+    ny = tn_devices.size // ncore
+    return Mesh(devices.reshape(nz, nx, ny, ncore), ("z", "x", "y", "core")), (nz, nx, ny, ncore)
 
 
 def solution(mesh):
+    mesh2, sizes = physical_mesh(mesh)
     return jax.shard_map(
-        shards,
-        mesh=mesh,
-        in_specs=(P("dp", None, "tensor"), P(None, "tensor"), P(None, "tensor"), P(None, "tensor")),
-        out_specs=(P(None, "tensor"), P(None, "tensor"), P(None, "tensor"), P(), P()),
+        make_shards(*sizes),
+        mesh=mesh2,
+        in_specs=(P(DP, None, TN), P(None, TN), P(None, TN), P(None, TN)),
+        out_specs=(P(None, TN), P(None, TN), P(None, TN), P(), P()),
         check_vma=False,
     )

time: 234 us -> 149 us (0.64)
  waiting for transfers between devices: 190 us -> 54.1 us
  blocking collectives: 17.5 us -> 53.1 us
  starting transfers between devices: 0.08 us -> 13.5 us
  local copies, waits for them, and re-layouts: 5.15 us -> 7.68 us
    psum x1 -> x0, waiting for transfers between devices: 153 us -> none  [shards(): grad = lax.psum(local_grad, 'dp') / lax.axis_size('dp')]
    all_to_all x0 -> x3, blocking collectives: none -> 53.1 us  [the longest x1 21.6 us: dp_sum(): lax.all_to_all(y.reshape(nx, padded // nx, cols), 'x', 0, 0, tiled=False)]
    psum x1 -> x0, blocking collectives: 17.5 us -> none  [shards(): lax.psum((group_squares(weights, seg_table), step_local), 'tensor')]
    all_to_all x0 -> x1, waiting for transfers between devices: none -> 13.2 us  [dp_sum(): lax.all_to_all(jnp.broadcast_to(y[None], (nx,) + y.shape), 'x', 0, 0, til...]
    ppermute x0 -> x3, starting transfers between devices: none -> 9.76 us  [tensor_sum(): v = v + lax.ppermute(v, axis, [(i, i ^ step) for i in range(size)])]
    all_to_all x0 -> x1, starting transfers between devices: none -> 3.67 us  [dp_sum(): lax.all_to_all(jnp.broadcast_to(y[None], (nx,) + y.shape), 'x', 0, 0, til...]
    ppermute x0 -> x3, waiting for transfers between devices: none -> 2.95 us  [tensor_sum(): v = v + lax.ppermute(v, axis, [(i, i ^ step) for i in range(size)])]
  transfers between devices with their start and end apart: 2 -> 5, of which waited for: 2 -> 5; matrix products, arithmetic and copies ran while one was open for 0% -> 0% of each run, Pallas kernels for 0% -> 0%
where the time goes in v1:
time: 149 us
  waiting for transfers between devices  54.1 us (36%)
  blocking collectives  53.1 us (36%)
  between operations  14.1 us (9%)
  starting transfers between devices  13.5 us (9%)
  local copies, waits for them, and re-layouts  7.68 us (5%)
  other arithmetic  6.06 us (4%)
    all_gather x1, waiting for transfers between devices, shards(): lax.all_gather(weights_new.astype(jnp.bfloat16), TN, axis=1, tiled=True)  38 us
    all_to_all x1, blocking collectives, dp_sum(): lax.all_to_all(y.reshape(nx, padded // nx, cols), 'x', 0, 0, tiled=False)  21.6 us
    all_to_all x1, blocking collectives, dp_sum(): lax.all_to_all(y.reshape(nz, padded // (nx * nz), cols), 'z', 0, 0, tiled...  18.7 us
    all_to_all x1, waiting for transfers between devices, dp_sum(): lax.all_to_all(jnp.broadcast_to(y[None], (nx,) + y.shape), 'x', 0, 0, til...  13.2 us
    all_to_all x1, blocking collectives, dp_sum(): lax.all_to_all(jnp.broadcast_to(y[None], (nz,) + y.shape), 'z', 0, 0, til...  12.8 us
    ppermute x3, starting transfers between devices, tensor_sum(): v = v + lax.ppermute(v, axis, [(i, i ^ step) for i in range(size)])  9.76 us
    unnamed x5, local copies, waits for them, and re-layouts  5.13 us
    reduce_sum x1, other arithmetic, group_squares(): row_sums = jnp.sum(values * values, axis=1)  3.96 us
  transfers between devices with their start and end apart: 5, of which 5 were waited for; matrix products, arithmetic and copies ran while one was open for 0% of the time, Pallas kernels for 0%

profile of v1, /device:TPU:1, one launch (start us, length us, event | category | flops | bytes accessed | tf_op | source)
XLA Modules:
  0.0 149.0 jit_solution(8851995358770724701)
XLA Ops:
  7.2 1.4 pad.4
  8.5 21.6 %all_to_all.20 = f32[4,640,128]{2,1,0:T(8,128)S(1)} all-to-all(f32[4,640,128]{2,1,0:T(8,128)S(1)} %bitcast.17), channel_id=1, replica_groups=mesh['z'=8,'x'=4,'y'=4,'core'=2] {'x'}, dimensions={0} | all-to-all | bytes 2621440 | tf_op jit(solution)/shard_map/all_to_all | solution.py:58
  30.2 0.1 reduce_sum.37
  30.3 18.7 %all_to_all.21 = f32[8,80,128]{2,1,0:T(8,128)S(1)} all-to-all(f32[8,80,128]{2,1,0:T(8,128)S(1)} %bitcast.19), channel_id=1, replica_groups=mesh['z'=8,'x'=4,'y'=4,'core'=2] {'z'}, dimensions={0} | all-to-all | bytes 655360 | tf_op jit(solution)/shard_map/all_to_all | solution.py:59
  49.0 12.8 %all_to_all.22 = f32[8,80,128]{2,1,0:T(8,128)S(1)} all-to-all(f32[8,80,128]{2,1,0:T(8,128)S(1)} %broadcast_in_dim.24), channel_id=1, replica_groups=mesh['z'=8,'x'=4,'y'=4,'core'=2] {'z'}, dimensions={0} | all-to-all | bytes 655360 | tf_op jit(solution)/shard_map/all_to_all | solution.py:60
  61.8 1.1 broadcast_in_dim.26
  62.9 0.0 copy-start
  62.9 3.7 %all-to-all-start.3 = ((f32[4,640,128]{2,1,0:T(8,128)}), f32[4,640,128]{2,1,0:T(8,128)S(1)}, u32[]{:S(2)}, u32[]{:S(2)}) async-start(f32[4,640,128]{2,1,0:T(8,128)} %broadcast_in_dim.26), calls=%async_computation.3 | async-start | bytes 2621440 | tf_op jit(solution)/shard_map/all_to_all | solution.py:62
  66.6 0.0 all-gather.2.cloned.1.call-start
  66.8 13.2 %all-to-all-done.3 = f32[4,640,128]{2,1,0:T(8,128)S(1)} async-done(((f32[4,640,128]{2,1,0:T(8,128)}), f32[4,640,128]{2,1,0:T(8,128)S(1)}, u32[]{:S(2)}, u32[]{:S(2)}) %all-to-all-start.3) | async-done | bytes 1310752 | tf_op jit(solution)/shard_map/all_to_all | solution.py:62
  79.9 0.0 copy-done
  79.9 4.0 %multiply_reduce_fusion = (f32[2368]{0:T(1024)S(1)}, f32[2368,128]{1,0:T(8,128)S(1)}, f32[2368,128]{1,0:T(8,128)}, f32[2368,128]{1,0:T(8,128)}, f32[2368]{0:T(1024)S(1)}) fusion(f32[2368,128]{1,0:T(8,128)S(1)} %copy-done, f32[2368]{0:T(1024)S(1)} %fusion.1, f32[2560,128]{1,0:T(8,128)S(1)} %bitcast.18, f32[2368,128]{1,0:T(8,128)} %param.6, f32[2368,128]{1,0:T(8,128)} %param.7), kind=kLoop, calls=%fused_computation.1 | loop fusion | flops 5451136 | bytes 8515328 | tf_op jit(solution)/shard_map/reduce_sum | solution.py:32
  83.9 0.1 convolution_bitcast_fusion
  84.1 0.2 convolution_bitcast_fusion.1
  84.3 0.1 pad_maximum_fusion
  84.4 5.5 %collective-permute-start = (f32[8]{0:T(128)S(1)}, f32[8]{0:T(128)S(1)}, u32[]{:S(2)}, u32[]{:S(2)}) collective-permute-start(f32[8]{0:T(128)S(1)} %pad_maximum_fusion), channel_id=1, source_target_pairs={{0,1},{1,0},{2,3},{3,2},{4,5},{5,4},{6,7},{7,6},{8,9},{9,8},{10,11... | collective-permute-start | bytes 104 | tf_op jit(solution)/shard_map/ppermute | solution.py:70
  89.9 0.8 collective-permute-done
  90.7 0.1 fusion.10
  90.8 1.3 collective-permute-start.1
  92.1 1.1 collective-permute-done.1
  93.3 2.9 %collective-permute-start.2 = (f32[8]{0:T(128)S(1)}, f32[8]{0:T(128)S(1)}, u32[]{:S(2)}, u32[]{:S(2)}) collective-permute-start(f32[8]{0:T(128)S(1)} %add.59), channel_id=1, source_target_pairs={{0,4},{2,6},{4,0},{6,2},{1,5},{3,7},{5,1},{7,3},{8,12},{10,14},{12... | collective-permute-start | bytes 104 | tf_op jit(solution)/shard_map/ppermute | solution.py:70
  96.2 1.0 collective-permute-done.2
  97.2 0.1 rsqrt_multiply_fusion
  97.3 0.0 copy-start.1
  97.3 0.2 convolution_reduce_fusion
  97.5 1.6 %fusion.3 = (bf16[2368,128]{1,0:T(8,128)(2,1)}, f32[2368,128]{1,0:T(8,128)}) fusion(f32[2368,128]{1,0:T(8,128)S(1)} %copy-done, f32[2368,128]{1,0:T(8,128)S(1)} %get-tuple-element.8, f32[2368]{0:T(1024)S(1)} %broadcast_multiply_fusion), kind=kLoop, calls=%fused_computation.20 | loop fusion | flops 909312 | bytes 4252928 | tf_op jit(solution)/shard_map/convert_element_type | solution.py:86
  99.1 0.0 copy-done.1
  99.1 0.0 all-gather.2.cloned.1.call-update
  99.1 38.0 %all-gather.2.cloned.1.call-done = bf16[2368,1024]{1,0:T(8,128)(2,1)} async-done(((bf16[2368,128]{1,0:T(8,128)(2,1)}), bf16[2368,1024]{1,0:T(8,128)(2,1)}) %all-gather.2.cloned.1.call-update) | async-done | bytes 4849680 | tf_op jit(solution)/shard_map/all_gather | solution.py:86
  137.1 5.1 %copy.10 = bf16[2368,1024]{1,0:T(8,128)(2,1)} copy(bf16[2368,1024]{1,0:T(8,128)(2,1)} %all-gather.2.cloned.1.call-done) | data formatting | bytes 9699328
  (11 shorter events, 0.2 us)
Async XLA Ops:
  62.9 17.0 %copy-start = (f32[2368,128]{1,0:T(8,128)S(1)}, f32[2368,128]{1,0:T(8,128)}, u32[]{:S(2)}) copy-start(f32[2368,128]{1,0:T(8,128)} %param.5) | copy-start | bytes 3637252
  62.9 17.0 %all-to-all-start.3 = ((f32[4,640,128]{2,1,0:T(8,128)}), f32[4,640,128]{2,1,0:T(8,128)S(1)}, u32[]{:S(2)}, u32[]{:S(2)}) async-start(f32[4,640,128]{2,1,0:T(8,128)} %broadcast_in_dim.26), calls=%async_computation.3 | async-start | bytes 2621440 | tf_op jit(solution)/shard_map/all_to_all | solution.py:62
  66.6 70.5 %all-gather.2.cloned.1.call-start = ((), (), s32[]{:S(2)}) async-start(), calls=%async_computation.4 | async-start | bytes 5455872 | tf_op jit(solution)/shard_map/all_gather | solution.py:86
  84.4 6.4 %collective-permute-start = (f32[8]{0:T(128)S(1)}, f32[8]{0:T(128)S(1)}, u32[]{:S(2)}, u32[]{:S(2)}) collective-permute-start(f32[8]{0:T(128)S(1)} %pad_maximum_fusion), channel_id=1, source_target_pairs={{0,1},{1,0},{2,3},{3,2},{4,5},{5,4},{6,7},{7,6},{8,9},{9,8},{10,11... | collective-permute-start | bytes 104 | tf_op jit(solution)/shard_map/ppermute | solution.py:70
  90.8 2.4 %collective-permute-start.1 = (f32[8]{0:T(128)S(1)}, f32[8]{0:T(128)S(1)}, u32[]{:S(2)}, u32[]{:S(2)}) collective-permute-start(f32[8]{0:T(128)S(1)} %fusion.10), channel_id=1, source_target_pairs={{0,2},{2,0},{4,6},{6,4},{1,3},{3,1},{5,7},{7,5},{8,10},{10,8},{12,... | collective-permute-start | bytes 104 | tf_op jit(solution)/shard_map/ppermute | solution.py:70
  93.3 3.9 %collective-permute-start.2 = (f32[8]{0:T(128)S(1)}, f32[8]{0:T(128)S(1)}, u32[]{:S(2)}, u32[]{:S(2)}) collective-permute-start(f32[8]{0:T(128)S(1)} %add.59), channel_id=1, source_target_pairs={{0,4},{2,6},{4,0},{6,2},{1,5},{3,7},{5,1},{7,3},{8,12},{10,14},{12... | collective-permute-start | bytes 104 | tf_op jit(solution)/shard_map/ppermute | solution.py:70
  97.3 1.8 %copy-start.1 = (f32[4]{0:T(128)}, f32[4]{0:T(128)S(1)}, u32[]{:S(2)}) copy-start(f32[4]{0:T(128)S(1)} %rsqrt_multiply_fusion) | copy-start | bytes 52
Sparse Core Ops, SparseCore 0:
  99.2 37.7 all-gather.1

commit v2 on v1

--- a/solution.py
+++ b/solution.py
@@ -72,6 +72,21 @@
     return v
 
 
+def tensor_gather(b, ny):
+    y = lax.axis_index("y")
+    core = lax.axis_index("core")
+    swap = [(0, 1), (1, 0)]
+    mine = [b] + [lax.ppermute(b, "y", [(i, (i - s) % ny) for i in range(ny)]) for s in range(1, ny)]
+    other = [lax.ppermute(m, "core", swap) for m in mine]
+    pairs = [
+        jnp.where(core == 0, jnp.concatenate([m, o], 1), jnp.concatenate([o, m], 1))
+        for m, o in zip(mine, other)
+    ]
+    q = jnp.concatenate(pairs + pairs, 1)
+    width = 2 * b.shape[1]
+    return lax.dynamic_slice_in_dim(q, ((ny - y) % ny) * width, ny * width, 1)
+
+
 def make_shards(nz, nx, ny, ncore):
     def shards(gradients, weights, first_moment, second_moment):
         local_grad = gradients[0]
@@ -83,7 +98,10 @@
         both = tensor_sum(both, ny, ncore)
         weight_total, step_total = both[:4], both[4:]
         weights_new, ratios = apply_ratios(weights, update, seg_table, weight_total, step_total)
-        copies = lax.all_gather(weights_new.astype(jnp.bfloat16), TN, axis=1, tiled=True)
+        if ncore == 2:
+            copies = tensor_gather(weights_new.astype(jnp.bfloat16), ny)
+        else:
+            copies = lax.all_gather(weights_new.astype(jnp.bfloat16), TN, axis=1, tiled=True)
         return (weights_new, first_new, second_new, copies, ratios)
 
     return shards

time: 149 us -> 135 us (0.906)
  waiting for transfers between devices: 54.1 us -> 26.3 us
  starting transfers between devices: 13.5 us -> 36.6 us
  between operations: 14.1 us -> 0.81 us
  other arithmetic: 6.06 us -> 11.9 us
  local copies, waits for them, and re-layouts: 7.68 us -> 5.57 us
    all_gather x1 -> x0, waiting for transfers between devices: 38 us -> none  [shards(): lax.all_gather(weights_new.astype(jnp.bfloat16), TN, axis=1, tiled=True)]
    ppermute x0 -> x7, starting transfers between devices: none -> 23.2 us  [the longest x4 19.4 us: tensor_gather(): other = [lax.ppermute(m, 'core', swap) for m in mine]]
    ppermute x0 -> x7, waiting for transfers between devices: none -> 10.1 us  [the longest x3 10.1 us: tensor_gather(): lax.ppermute(b, 'y', [(i, (i - s) % ny) for i in range(ny)])]
    unnamed x0 -> x7, other arithmetic: none -> 5.55 us
    unnamed x5 -> x4, local copies, waits for them, and re-layouts: 5.13 us -> 0.01 us
    dynamic_slice x0 -> x1, local copies, waits for them, and re-layouts: none -> 3.02 us  [tensor_gather(): return lax.dynamic_slice_in_dim(q, (ny - y) % ny * width, ny * width, 1)]
  transfers between devices with their start and end apart: 5 -> 11, of which waited for: 5 -> 6; matrix products, arithmetic and copies ran while one was open for 0% -> 2% of each run, Pallas kernels for 0% -> 0%
where the time goes in v2:
time: 135 us
  blocking collectives  53.1 us (39%)
  starting transfers between devices  36.6 us (27%)
  waiting for transfers between devices  26.3 us (19%)
  other arithmetic  11.9 us (9%)
  local copies, waits for them, and re-layouts  5.57 us (4%)
    all_to_all x1, blocking collectives, dp_sum(): lax.all_to_all(y.reshape(nx, padded // nx, cols), 'x', 0, 0, tiled=False)  21.6 us
    ppermute x4, starting transfers between devices, tensor_gather(): other = [lax.ppermute(m, 'core', swap) for m in mine]  19.4 us
    all_to_all x1, blocking collectives, dp_sum(): lax.all_to_all(y.reshape(nz, padded // (nx * nz), cols), 'z', 0, 0, tiled...  18.7 us
    all_to_all x1, waiting for transfers between devices, dp_sum(): lax.all_to_all(jnp.broadcast_to(y[None], (nx,) + y.shape), 'x', 0, 0, til...  13.2 us
    all_to_all x1, blocking collectives, dp_sum(): lax.all_to_all(jnp.broadcast_to(y[None], (nz,) + y.shape), 'z', 0, 0, til...  12.8 us
    ppermute x3, waiting for transfers between devices, tensor_gather(): lax.ppermute(b, 'y', [(i, (i - s) % ny) for i in range(ny)])  10.1 us
    ppermute x3, starting transfers between devices, tensor_sum(): v = v + lax.ppermute(v, axis, [(i, i ^ step) for i in range(size)])  9.76 us
    unnamed x7, other arithmetic  5.55 us
  transfers between devices with their start and end apart: 11, of which 6 were waited for; matrix products, arithmetic and copies ran while one was open for 2% of the time, Pallas kernels for 0%

profile of v2, /device:TPU:1, one launch (start us, length us, event | category | flops | bytes accessed | tf_op | source)
XLA Modules:
  0.0 134.8 jit_solution(8249720474707047484)
XLA Ops:
  0.6 1.4 %pad.4 = f32[2560,128]{1,0:T(8,128)S(1)} pad(f32[2368,128]{1,0:T(8,128)} %bitcast.21, f32[]{:T(128)} %constant.50.clone.1), padding=0_192x0_0 | pad | bytes 2523140 | tf_op jit(solution)/shard_map/jit(_pad)/pad | solution.py:57
  2.0 21.6 %all_to_all.20 = f32[4,640,128]{2,1,0:T(8,128)S(1)} all-to-all(f32[4,640,128]{2,1,0:T(8,128)S(1)} %bitcast.17), channel_id=1, replica_groups=mesh['z'=8,'x'=4,'y'=4,'core'=2] {'x'}, dimensions={0} | all-to-all | bytes 2621440 | tf_op jit(solution)/shard_map/all_to_all | solution.py:58
  23.6 0.1 reduce_sum.37
  23.7 18.7 %all_to_all.21 = f32[8,80,128]{2,1,0:T(8,128)S(1)} all-to-all(f32[8,80,128]{2,1,0:T(8,128)S(1)} %bitcast.19), channel_id=1, replica_groups=mesh['z'=8,'x'=4,'y'=4,'core'=2] {'z'}, dimensions={0} | all-to-all | bytes 655360 | tf_op jit(solution)/shard_map/all_to_all | solution.py:59
  42.4 12.8 %all_to_all.22 = f32[8,80,128]{2,1,0:T(8,128)S(1)} all-to-all(f32[8,80,128]{2,1,0:T(8,128)S(1)} %broadcast_in_dim.24), channel_id=1, replica_groups=mesh['z'=8,'x'=4,'y'=4,'core'=2] {'z'}, dimensions={0} | all-to-all | bytes 655360 | tf_op jit(solution)/shard_map/all_to_all | solution.py:60
  55.3 1.1 broadcast_in_dim.26
  56.4 0.0 copy-start
  56.4 3.7 %all-to-all-start.3 = ((f32[4,640,128]{2,1,0:T(8,128)}), f32[4,640,128]{2,1,0:T(8,128)S(1)}, u32[]{:S(2)}, u32[]{:S(2)}) async-start(f32[4,640,128]{2,1,0:T(8,128)} %broadcast_in_dim.26), calls=%async_computation.3 | async-start | bytes 2621440 | tf_op jit(solution)/shard_map/all_to_all | solution.py:62
  60.2 13.2 %all-to-all-done.3 = f32[4,640,128]{2,1,0:T(8,128)S(1)} async-done(((f32[4,640,128]{2,1,0:T(8,128)}), f32[4,640,128]{2,1,0:T(8,128)S(1)}, u32[]{:S(2)}, u32[]{:S(2)}) %all-to-all-start.3) | async-done | bytes 1310752 | tf_op jit(solution)/shard_map/all_to_all | solution.py:62
  73.4 0.0 copy-done
  73.4 4.0 %multiply_reduce_fusion = (f32[2368]{0:T(1024)S(1)}, f32[2368,128]{1,0:T(8,128)S(1)}, f32[2368,128]{1,0:T(8,128)}, f32[2368,128]{1,0:T(8,128)}, f32[2368]{0:T(1024)S(1)}) fusion(f32[2368,128]{1,0:T(8,128)S(1)} %copy-done, f32[2368]{0:T(1024)S(1)} %fusion.9, f32[2560,128]{1,0:T(8,128)S(1)} %bitcast.18, f32[2368,128]{1,0:T(8,128)} %param.6, f32[2368,128]{1,0:T(8,128)} %param.7), kind=kLoop, calls=%fused_computation.5 | loop fusion | flops 5451136 | bytes 8515328 | tf_op jit(solution)/shard_map/reduce_sum | solution.py:32
  77.4 0.1 convolution_bitcast_fusion
  77.5 0.2 convolution_bitcast_fusion.1
  77.7 0.1 pad_maximum_fusion
  77.9 5.5 %collective-permute-start = (f32[8]{0:T(128)S(1)}, f32[8]{0:T(128)S(1)}, u32[]{:S(2)}, u32[]{:S(2)}) collective-permute-start(f32[8]{0:T(128)S(1)} %pad_maximum_fusion), channel_id=1, source_target_pairs={{0,1},{1,0},{2,3},{3,2},{4,5},{5,4},{6,7},{7,6},{8,9},{9,8},{10,11... | collective-permute-start | bytes 104 | tf_op jit(solution)/shard_map/ppermute | solution.py:70
  83.4 0.8 collective-permute-done
  84.2 0.1 fusion.18
  84.3 1.3 collective-permute-start.1
  85.6 1.1 collective-permute-done.1
  86.7 2.9 %collective-permute-start.2 = (f32[8]{0:T(128)S(1)}, f32[8]{0:T(128)S(1)}, u32[]{:S(2)}, u32[]{:S(2)}) collective-permute-start(f32[8]{0:T(128)S(1)} %add.66), channel_id=1, source_target_pairs={{0,4},{2,6},{4,0},{6,2},{1,5},{3,7},{5,1},{7,3},{8,12},{10,14},{12... | collective-permute-start | bytes 104 | tf_op jit(solution)/shard_map/ppermute | solution.py:70
  89.6 1.0 collective-permute-done.2
  90.7 0.1 rsqrt_multiply_fusion
  90.7 0.2 convolution_reduce_fusion
  90.9 1.4 %fusion.11 = (bf16[2368,128]{1,0:T(8,128)(2,1)S(1)}, f32[2368,128]{1,0:T(8,128)}) fusion(f32[2368,128]{1,0:T(8,128)S(1)} %copy-done, f32[2368,128]{1,0:T(8,128)S(1)} %get-tuple-element.8, f32[2368]{0:T(1024)S(1)} %broadcast_multiply_fusion), kind=kLoop, calls=%fused_computation.33 | loop fusion | flops 909312 | bytes 4252928 | tf_op jit(solution)/shard_map/convert_element_type | solution.py:102
  92.4 0.0 copy-done.1
  92.4 2.7 %collective-permute-start.4 = (bf16[2368,128]{1,0:T(8,128)(2,1)S(1)}, bf16[2368,128]{1,0:T(8,128)(2,1)S(1)}, u32[]{:S(2)}, u32[]{:S(2)}) collective-permute-start(bf16[2368,128]{1,0:T(8,128)(2,1)S(1)} %get-tuple-element.5), channel_id=1, source_target_pairs={{0,6},{2,0},{4,2},{6,4},{1,7},{3,1},{5,3},{7,5},{8,14},{10,8},{12,... | collective-permute-start | bytes 1818632 | tf_op jit(solution)/shard_map/ppermute | solution.py:79
  95.1 0.3 collective-permute-start.6
  95.4 0.7 collective-permute-start.8
  96.1 3.5 %collective-permute-start.3 = (bf16[2368,128]{1,0:T(8,128)(2,1)S(1)}, bf16[2368,128]{1,0:T(8,128)(2,1)S(1)}, u32[]{:S(2)}, u32[]{:S(2)}) collective-permute-start(bf16[2368,128]{1,0:T(8,128)(2,1)S(1)} %get-tuple-element.5), channel_id=1, source_target_pairs={{0,1},{1,0},{2,3},{3,2},{4,5},{5,4},{6,7},{7,6},{8,9},{9,8},{10,11... | collective-permute-start | bytes 1818632 | tf_op jit(solution)/shard_map/ppermute | solution.py:80
  99.6 6.9 %collective-permute-done.4 = bf16[2368,128]{1,0:T(8,128)(2,1)S(1)} collective-permute-done((bf16[2368,128]{1,0:T(8,128)(2,1)S(1)}, bf16[2368,128]{1,0:T(8,128)(2,1)S(1)}, u32[]{:S(2)}, u32[]{:S(2)}) %collective-permute-start.4) | collective-permute-done | bytes 606240 | tf_op jit(solution)/shard_map/ppermute | solution.py:79
  106.5 15.4 %collective-permute-start.5 = (bf16[2368,128]{1,0:T(8,128)(2,1)S(1)}, bf16[2368,128]{1,0:T(8,128)(2,1)}, u32[]{:S(2)}, u32[]{:S(2)}) collective-permute-start(bf16[2368,128]{1,0:T(8,128)(2,1)S(1)} %collective-permute-done.4), channel_id=1, source_target_pairs={{0,1},{1,0},{2,3},{3,2},{4,5},{5,4},{6,7},{7,6},{8,9},{9,8},{10,11... | collective-permute-start | bytes 1818632 | tf_op jit(solution)/shard_map/ppermute | solution.py:80
  122.0 0.0 collective-permute-done.6
  122.0 0.0 collective-permute-start.7
  122.0 3.2 %collective-permute-done.8 = bf16[2368,128]{1,0:T(8,128)(2,1)S(1)} collective-permute-done((bf16[2368,128]{1,0:T(8,128)(2,1)S(1)}, bf16[2368,128]{1,0:T(8,128)(2,1)S(1)}, u32[]{:S(2)}, u32[]{:S(2)}) %collective-permute-start.8) | collective-permute-done | bytes 606240 | tf_op jit(solution)/shard_map/ppermute | solution.py:79
  125.2 0.5 collective-permute-start.9
  125.7 0.0 collective-permute-done.3
  125.7 0.4 fusion.6
  126.1 0.0 collective-permute-done.5
  126.1 1.6 %fusion.4 = bf16[2368,2048]{1,0:T(8,128)(2,1)S(1)} fusion(bf16[2368,2048]{1,0:T(8,128)(2,1)S(1)} %fusion.6, bf16[2368,128]{1,0:T(8,128)(2,1)S(1)} %collective-permute-done.4, bf16[2368,128]{1,0:T(8,128)(2,1)} %collective-permute-done.5, pred[]{:T(512)S(6)} %eq.18), kind=kLoop, calls=%fused_computation.17 | loop fusion | flops 5455872 | bytes 2424833
  127.7 0.0 collective-permute-done.7
  127.7 0.5 fusion.2
  128.2 0.0 collective-permute-done.9
  128.2 0.5 fusion
  128.7 0.5 fusion.7
  129.2 1.6 %fusion.5 = bf16[2368,2048]{1,0:T(8,128)(2,1)S(1)} fusion(bf16[2368,2048]{1,0:T(8,128)(2,1)S(1)} %fusion.7, bf16[2368,128]{1,0:T(8,128)(2,1)S(1)} %collective-permute-done.4, bf16[2368,128]{1,0:T(8,128)(2,1)} %collective-permute-done.5, pred[]{:T(512)S(6)} %eq.18), kind=kLoop, calls=%fused_computation.18 | loop fusion | flops 5455872 | bytes 2424833
  130.8 0.5 fusion.3
  131.3 0.5 fusion.1
  131.8 3.0 %constant_dynamic-slice_fusion = bf16[2368,1024]{1,0:T(8,128)(2,1)} fusion(bf16[2368,2048]{1,0:T(8,128)(2,1)S(1)} %fusion.1, s32[]{:T(128)S(6)} %select_n.57), kind=kLoop, calls=%fused_computation.32 | loop fusion | bytes 9699332 | tf_op jit(solution)/shard_map/dynamic_slice | solution.py:87
  (12 shorter events, 0.2 us)
Async XLA Ops:
  56.4 17.0 %copy-start = (f32[2368,128]{1,0:T(8,128)S(1)}, f32[2368,128]{1,0:T(8,128)}, u32[]{:S(2)}) copy-start(f32[2368,128]{1,0:T(8,128)} %param.5) | copy-start | bytes 3637252
  56.4 17.0 %all-to-all-start.3 = ((f32[4,640,128]{2,1,0:T(8,128)}), f32[4,640,128]{2,1,0:T(8,128)S(1)}, u32[]{:S(2)}, u32[]{:S(2)}) async-start(f32[4,640,128]{2,1,0:T(8,128)} %broadcast_in_dim.26), calls=%async_computation.3 | async-start | bytes 2621440 | tf_op jit(solution)/shard_map/all_to_all | solution.py:62
  77.9 6.4 %collective-permute-start = (f32[8]{0:T(128)S(1)}, f32[8]{0:T(128)S(1)}, u32[]{:S(2)}, u32[]{:S(2)}) collective-permute-start(f32[8]{0:T(128)S(1)} %pad_maximum_fusion), channel_id=1, source_target_pairs={{0,1},{1,0},{2,3},{3,2},{4,5},{5,4},{6,7},{7,6},{8,9},{9,8},{10,11... | collective-permute-start | bytes 104 | tf_op jit(solution)/shard_map/ppermute | solution.py:70
  84.3 2.4 %collective-permute-start.1 = (f32[8]{0:T(128)S(1)}, f32[8]{0:T(128)S(1)}, u32[]{:S(2)}, u32[]{:S(2)}) collective-permute-start(f32[8]{0:T(128)S(1)} %fusion.18), channel_id=1, source_target_pairs={{0,2},{2,0},{4,6},{6,4},{1,3},{3,1},{5,7},{7,5},{8,10},{10,8},{12,... | collective-permute-start | bytes 104 | tf_op jit(solution)/shard_map/ppermute | solution.py:70
  86.7 3.9 %collective-permute-start.2 = (f32[8]{0:T(128)S(1)}, f32[8]{0:T(128)S(1)}, u32[]{:S(2)}, u32[]{:S(2)}) collective-permute-start(f32[8]{0:T(128)S(1)} %add.66), channel_id=1, source_target_pairs={{0,4},{2,6},{4,0},{6,2},{1,5},{3,7},{5,1},{7,3},{8,12},{10,14},{12... | collective-permute-start | bytes 104 | tf_op jit(solution)/shard_map/ppermute | solution.py:70
  90.7 1.6 %copy-start.1 = (f32[4]{0:T(128)}, f32[4]{0:T(128)S(1)}, u32[]{:S(2)}) copy-start(f32[4]{0:T(128)S(1)} %rsqrt_multiply_fusion) | copy-start | bytes 52
  92.4 14.2 %collective-permute-start.4 = (bf16[2368,128]{1,0:T(8,128)(2,1)S(1)}, bf16[2368,128]{1,0:T(8,128)(2,1)S(1)}, u32[]{:S(2)}, u32[]{:S(2)}) collective-permute-start(bf16[2368,128]{1,0:T(8,128)(2,1)S(1)} %get-tuple-element.5), channel_id=1, source_target_pairs={{0,6},{2,0},{4,2},{6,4},{1,7},{3,1},{5,3},{7,5},{8,14},{10,8},{12,... | collective-permute-start | bytes 1818632 | tf_op jit(solution)/shard_map/ppermute | solution.py:79
  95.1 26.9 %collective-permute-start.6 = (bf16[2368,128]{1,0:T(8,128)(2,1)S(1)}, bf16[2368,128]{1,0:T(8,128)(2,1)S(1)}, u32[]{:S(2)}, u32[]{:S(2)}) collective-permute-start(bf16[2368,128]{1,0:T(8,128)(2,1)S(1)} %get-tuple-element.5), channel_id=1, source_target_pairs={{0,4},{2,6},{4,0},{6,2},{1,5},{3,7},{5,1},{7,3},{8,12},{10,14},{12... | collective-permute-start | bytes 1818632 | tf_op jit(solution)/shard_map/ppermute | solution.py:79
  95.4 29.7 %collective-permute-start.8 = (bf16[2368,128]{1,0:T(8,128)(2,1)S(1)}, bf16[2368,128]{1,0:T(8,128)(2,1)S(1)}, u32[]{:S(2)}, u32[]{:S(2)}) collective-permute-start(bf16[2368,128]{1,0:T(8,128)(2,1)S(1)} %get-tuple-element.5), channel_id=1, source_target_pairs={{0,2},{2,4},{4,6},{6,0},{1,3},{3,5},{5,7},{7,1},{8,10},{10,12},{12... | collective-permute-start | bytes 1818632 | tf_op jit(solution)/shard_map/ppermute | solution.py:79
  96.1 29.6 %collective-permute-start.3 = (bf16[2368,128]{1,0:T(8,128)(2,1)S(1)}, bf16[2368,128]{1,0:T(8,128)(2,1)S(1)}, u32[]{:S(2)}, u32[]{:S(2)}) collective-permute-start(bf16[2368,128]{1,0:T(8,128)(2,1)S(1)} %get-tuple-element.5), channel_id=1, source_target_pairs={{0,1},{1,0},{2,3},{3,2},{4,5},{5,4},{6,7},{7,6},{8,9},{9,8},{10,11... | collective-permute-start | bytes 1818632 | tf_op jit(solution)/shard_map/ppermute | solution.py:80
  106.5 19.6 %collective-permute-start.5 = (bf16[2368,128]{1,0:T(8,128)(2,1)S(1)}, bf16[2368,128]{1,0:T(8,128)(2,1)}, u32[]{:S(2)}, u32[]{:S(2)}) collective-permute-start(bf16[2368,128]{1,0:T(8,128)(2,1)S(1)} %collective-permute-done.4), channel_id=1, source_target_pairs={{0,1},{1,0},{2,3},{3,2},{4,5},{5,4},{6,7},{7,6},{8,9},{9,8},{10,11... | collective-permute-start | bytes 1818632 | tf_op jit(solution)/shard_map/ppermute | solution.py:80
  122.0 5.8 %collective-permute-start.7 = (bf16[2368,128]{1,0:T(8,128)(2,1)S(1)}, bf16[2368,128]{1,0:T(8,128)(2,1)S(1)}, u32[]{:S(2)}, u32[]{:S(2)}) collective-permute-start(bf16[2368,128]{1,0:T(8,128)(2,1)S(1)} %collective-permute-done.6), channel_id=1, source_target_pairs={{0,1},{1,0},{2,3},{3,2},{4,5},{5,4},{6,7},{7,6},{8,9},{9,8},{10,11... | collective-permute-start | bytes 1818632 | tf_op jit(solution)/shard_map/ppermute | solution.py:80
  125.2 3.0 %collective-permute-start.9 = (bf16[2368,128]{1,0:T(8,128)(2,1)S(1)}, bf16[2368,128]{1,0:T(8,128)(2,1)S(1)}, u32[]{:S(2)}, u32[]{:S(2)}) collective-permute-start(bf16[2368,128]{1,0:T(8,128)(2,1)S(1)} %collective-permute-done.8), channel_id=1, source_target_pairs={{0,1},{1,0},{2,3},{3,2},{4,5},{5,4},{6,7},{7,6},{8,9},{9,8},{10,11... | collective-permute-start | bytes 1818632 | tf_op jit(solution)/shard_map/ppermute | solution.py:80

commit v3 on v2

--- a/solution.py
+++ b/solution.py
@@ -52,24 +52,32 @@
 
 def dp_sum(x, nz, nx):
     rows, cols = x.shape
-    unit = 8 * nz * nx
-    padded = -(-rows // unit) * unit
-    y = jnp.pad(x, ((0, padded - rows), (0, 0)))
-    y = lax.all_to_all(y.reshape(nx, padded // nx, cols), "x", 0, 0, tiled=False).sum(0)
-    y = lax.all_to_all(y.reshape(nz, padded // (nx * nz), cols), "z", 0, 0, tiled=False).sum(0)
+    part = rows // nx
+    padded = -(-part // (8 * nz)) * (8 * nz)
+    y = lax.all_to_all(x.reshape(nx, part, cols), "x", 0, 0, tiled=False).sum(0)
+    y = jnp.pad(y, ((0, padded - part), (0, 0)))
+    y = lax.all_to_all(y.reshape(nz, padded // nz, cols), "z", 0, 0, tiled=False).sum(0)
     y = lax.all_to_all(jnp.broadcast_to(y[None], (nz,) + y.shape), "z", 0, 0, tiled=False)
-    y = y.reshape(padded // nx, cols)
+    y = y.reshape(padded, cols)[:part]
     y = lax.all_to_all(jnp.broadcast_to(y[None], (nx,) + y.shape), "x", 0, 0, tiled=False)
-    return y.reshape(padded, cols)[:rows]
+    return y.reshape(rows, cols)
 
 
 def tensor_sum(v, ny, ncore):
-    for axis, size in (("core", ncore), ("y", ny)):
-        step = 1
-        while step < size:
-            v = v + lax.ppermute(v, axis, [(i, i ^ step) for i in range(size)])
-            step *= 2
-    return v
+    if ncore == 2:
+        v = v + lax.ppermute(v, "core", [(0, 1), (1, 0)])
+    else:
+        v = lax.psum(v, "core")
+    y = lax.axis_index("y")
+    slots = jnp.zeros((ny,) + v.shape, v.dtype)
+    slots = lax.dynamic_update_index_in_dim(slots, v, y, 0)
+    for s in range(1, ny):
+        got = lax.ppermute(v, "y", [(i, (i - s) % ny) for i in range(ny)])
+        slots = lax.dynamic_update_index_in_dim(slots, got, (y + s) % ny, 0)
+    total = slots[0]
+    for k in range(1, ny):
+        total = total + slots[k]
+    return total
 
 
 def tensor_gather(b, ny):

time: 135 us -> 130 us (0.963)
  waiting for transfers between devices: 26.3 us -> 24.3 us
  other arithmetic: 11.9 us -> 10.3 us
  blocking collectives: 53.1 us -> 51.6 us
    reduce_sum x1, other arithmetic: 3.96 us -> 1.26 us  [group_squares(): row_sums = jnp.sum(values * values, axis=1)]
    unnamed x4 -> x10, local copies, waits for them, and re-layouts: 0.01 us -> 1.97 us
    all_to_all x1, waiting for transfers between devices: 13.2 us -> 11.7 us  [dp_sum(): lax.all_to_all(jnp.broadcast_to(y[None], (nx,) + y.shape), 'x', 0, 0, til...]
    ppermute x3 -> x4, starting transfers between devices: 9.76 us -> 10.9 us  [the longest x1 5.88 us: tensor_sum(): v = v + lax.ppermute(v, 'core', [(0, 1), (1, 0)])]
    ppermute x3 -> x4, waiting for transfers between devices: 2.95 us -> 2.14 us  [the longest x3 1.32 us: tensor_sum(): got = lax.ppermute(v, 'y', [(i, (i - s) % ny) for i in range(ny)])]
  transfers between devices with their start and end apart: 11 -> 12, of which waited for: 6 -> 5; matrix products, arithmetic and copies ran while one was open for 2% -> 3% of each run, Pallas kernels for 0% -> 0%
where the time goes in v3:
time: 130 us
  blocking collectives  51.6 us (40%)
  starting transfers between devices  36 us (28%)
  waiting for transfers between devices  24.3 us (19%)
  other arithmetic  10.3 us (8%)
  local copies, waits for them, and re-layouts  6.31 us (5%)
    all_to_all x1, blocking collectives, dp_sum(): y = lax.all_to_all(x.reshape(nx, part, cols), 'x', 0, 0, tiled=False).sum(0)  19.9 us
    all_to_all x1, blocking collectives, dp_sum(): lax.all_to_all(y.reshape(nz, padded // nz, cols), 'z', 0, 0, tiled=False)  19.2 us
    ppermute x4, starting transfers between devices, tensor_gather(): other = [lax.ppermute(m, 'core', swap) for m in mine]  18.8 us
    all_to_all x1, blocking collectives, dp_sum(): lax.all_to_all(jnp.broadcast_to(y[None], (nz,) + y.shape), 'z', 0, 0, til...  12.5 us
    all_to_all x1, waiting for transfers between devices, dp_sum(): lax.all_to_all(jnp.broadcast_to(y[None], (nx,) + y.shape), 'x', 0, 0, til...  11.7 us
    ppermute x3, waiting for transfers between devices, tensor_gather(): lax.ppermute(b, 'y', [(i, (i - s) % ny) for i in range(ny)])  10.4 us
    ppermute x1, starting transfers between devices, tensor_sum(): v = v + lax.ppermute(v, 'core', [(0, 1), (1, 0)])  5.88 us
    unnamed x7, other arithmetic  5.55 us
  transfers between devices with their start and end apart: 12, of which 5 were waited for; matrix products, arithmetic and copies ran while one was open for 3% of the time, Pallas kernels for 0%

profile of v3, /device:TPU:1, one launch (start us, length us, event | category | flops | bytes accessed | tf_op | source)
XLA Modules:
  0.0 130.0 jit_solution(17930108319675904036)
XLA Ops:
  0.6 19.9 %all_to_all.20 = f32[4,592,128]{2,1,0:T(8,128)S(1)} all-to-all(f32[4,592,128]{2,1,0:T(8,128)} %bitcast.27), channel_id=1, replica_groups=mesh['z'=8,'x'=4,'y'=4,'core'=2] {'x'}, dimensions={0} | all-to-all | bytes 2424832 | tf_op jit(solution)/shard_map/all_to_all | solution.py:57
  20.6 0.1 reduce_sum.37
  20.7 19.2 %all_to_all.21 = f32[8,80,128]{2,1,0:T(8,128)S(1)} all-to-all(f32[8,80,128]{2,1,0:T(8,128)S(1)} %bitcast.25), channel_id=1, replica_groups=mesh['z'=8,'x'=4,'y'=4,'core'=2] {'z'}, dimensions={0} | all-to-all | bytes 655360 | tf_op jit(solution)/shard_map/all_to_all | solution.py:59
  39.9 12.5 %all_to_all.22 = f32[8,80,128]{2,1,0:T(8,128)S(1)} all-to-all(f32[8,80,128]{2,1,0:T(8,128)S(1)} %broadcast_in_dim.40), channel_id=1, replica_groups=mesh['z'=8,'x'=4,'y'=4,'core'=2] {'z'}, dimensions={0} | all-to-all | bytes 655360 | tf_op jit(solution)/shard_map/all_to_all | solution.py:60
  52.5 1.1 broadcast_in_dim.41
  53.6 3.5 %all-to-all-start.3 = ((f32[4,592,128]{2,1,0:T(8,128)}), f32[4,592,128]{2,1,0:T(8,128)S(1)}, u32[]{:S(2)}, u32[]{:S(2)}) async-start(f32[4,592,128]{2,1,0:T(8,128)} %broadcast_in_dim.41), calls=%async_computation.3 | async-start | bytes 2424832 | tf_op jit(solution)/shard_map/all_to_all | solution.py:62
  57.3 0.0 copy-start.3
  57.3 11.7 %all-to-all-done.3 = f32[4,592,128]{2,1,0:T(8,128)S(1)} async-done(((f32[4,592,128]{2,1,0:T(8,128)}), f32[4,592,128]{2,1,0:T(8,128)S(1)}, u32[]{:S(2)}, u32[]{:S(2)}) %all-to-all-start.3) | async-done | bytes 1212448 | tf_op jit(solution)/shard_map/all_to_all | solution.py:62
  69.0 0.2 broadcast_multiply_fusion
  69.2 1.1 copy-done.4
  70.3 0.4 bitcast_add_fusion
  70.7 0.0 copy-start
  70.7 0.0 copy-start.1
  70.7 0.9 copy-done.2
  71.6 1.3 multiply_reduce_fusion
  72.9 0.1 convolution_bitcast_fusion
  73.0 0.2 convolution_bitcast_fusion.1
  73.2 0.1 pad_maximum_fusion
  73.4 5.9 %collective-permute-start = (f32[8]{0:T(128)S(1)}, f32[8]{0:T(128)S(1)}, u32[]{:S(2)}, u32[]{:S(2)}) collective-permute-start(f32[8]{0:T(128)S(1)} %pad_maximum_fusion), channel_id=1, source_target_pairs={{0,1},{1,0},{2,3},{3,2},{4,5},{5,4},{6,7},{7,6},{8,9},{9,8},{10,11... | collective-permute-start | bytes 104 | tf_op jit(solution)/shard_map/ppermute | solution.py:68
  79.2 0.8 collective-permute-done
  80.1 0.1 fusion.19
  80.1 1.3 %collective-permute-start.3 = (f32[8]{0:T(128)S(1)}, f32[8]{0:T(128)S(1)}, u32[]{:S(2)}, u32[]{:S(2)}) collective-permute-start(f32[8]{0:T(128)S(1)} %fusion.19), channel_id=1, source_target_pairs={{0,2},{2,4},{4,6},{6,0},{1,3},{3,5},{5,7},{7,1},{8,10},{10,12},{12... | collective-permute-start | bytes 104 | tf_op jit(solution)/shard_map/ppermute | solution.py:75
  81.4 2.6 %collective-permute-start.2 = (f32[8]{0:T(128)S(1)}, f32[8]{0:T(128)S(1)}, u32[]{:S(2)}, u32[]{:S(2)}) collective-permute-start(f32[8]{0:T(128)S(1)} %fusion.19), channel_id=1, source_target_pairs={{0,4},{2,6},{4,0},{6,2},{1,5},{3,7},{5,1},{7,3},{8,12},{10,14},{12... | collective-permute-start | bytes 104 | tf_op jit(solution)/shard_map/ppermute | solution.py:75
  84.1 1.1 collective-permute-start.1
  85.2 1.3 %collective-permute-done.1 = f32[8]{0:T(128)S(1)} collective-permute-done((f32[8]{0:T(128)S(1)}, f32[8]{0:T(128)S(1)}, u32[]{:S(2)}, u32[]{:S(2)}) %collective-permute-start.1) | collective-permute-done | bytes 64 | tf_op jit(solution)/shard_map/ppermute | solution.py:75
  86.5 0.0 collective-permute-done.2
  86.6 0.0 collective-permute-done.3
  86.6 0.3 convolution_reduce_fusion
  86.9 1.4 %fusion.11 = (bf16[2368,128]{1,0:T(8,128)(2,1)S(1)}, f32[2368,128]{1,0:T(8,128)}) fusion(f32[2368,128]{1,0:T(8,128)S(1)} %copy-done.2, f32[2368,128]{1,0:T(8,128)S(1)} %get-tuple-element.8, f32[2368]{0:T(1024)S(1)} %broadcast_multiply_fusion.1), kind=kLoop, calls=%fused_computation.36 | loop fusion | flops 909312 | bytes 4252928 | tf_op jit(solution)/shard_map/convert_element_type | solution.py:110
  88.3 2.3 %collective-permute-start.5 = (bf16[2368,128]{1,0:T(8,128)(2,1)S(1)}, bf16[2368,128]{1,0:T(8,128)(2,1)S(1)}, u32[]{:S(2)}, u32[]{:S(2)}) collective-permute-start(bf16[2368,128]{1,0:T(8,128)(2,1)S(1)} %get-tuple-element.5), channel_id=1, source_target_pairs={{0,6},{2,0},{4,2},{6,4},{1,7},{3,1},{5,3},{7,5},{8,14},{10,8},{12,... | collective-permute-start | bytes 1818632 | tf_op jit(solution)/shard_map/ppermute | solution.py:87
  90.6 0.0 collective-permute-start.7
  90.6 0.6 collective-permute-start.9
  91.2 2.6 %collective-permute-start.4 = (bf16[2368,128]{1,0:T(8,128)(2,1)S(1)}, bf16[2368,128]{1,0:T(8,128)(2,1)S(1)}, u32[]{:S(2)}, u32[]{:S(2)}) collective-permute-start(bf16[2368,128]{1,0:T(8,128)(2,1)S(1)} %get-tuple-element.5), channel_id=1, source_target_pairs={{0,1},{1,0},{2,3},{3,2},{4,5},{5,4},{6,7},{7,6},{8,9},{9,8},{10,11... | collective-permute-start | bytes 1818632 | tf_op jit(solution)/shard_map/ppermute | solution.py:88
  93.8 8.4 %collective-permute-done.5 = bf16[2368,128]{1,0:T(8,128)(2,1)S(1)} collective-permute-done((bf16[2368,128]{1,0:T(8,128)(2,1)S(1)}, bf16[2368,128]{1,0:T(8,128)(2,1)S(1)}, u32[]{:S(2)}, u32[]{:S(2)}) %collective-permute-start.5) | collective-permute-done | bytes 606240 | tf_op jit(solution)/shard_map/ppermute | solution.py:87
  102.1 15.3 %collective-permute-start.6 = (bf16[2368,128]{1,0:T(8,128)(2,1)S(1)}, bf16[2368,128]{1,0:T(8,128)(2,1)}, u32[]{:S(2)}, u32[]{:S(2)}) collective-permute-start(bf16[2368,128]{1,0:T(8,128)(2,1)S(1)} %collective-permute-done.5), channel_id=1, source_target_pairs={{0,1},{1,0},{2,3},{3,2},{4,5},{5,4},{6,7},{7,6},{8,9},{9,8},{10,11... | collective-permute-start | bytes 1818632 | tf_op jit(solution)/shard_map/ppermute | solution.py:88
  117.5 0.6 fusion.18
  118.1 0.0 collective-permute-start.8
  118.1 2.0 %collective-permute-done.9 = bf16[2368,128]{1,0:T(8,128)(2,1)S(1)} collective-permute-done((bf16[2368,128]{1,0:T(8,128)(2,1)S(1)}, bf16[2368,128]{1,0:T(8,128)(2,1)S(1)}, u32[]{:S(2)}, u32[]{:S(2)}) %collective-permute-start.9) | collective-permute-done | bytes 606240 | tf_op jit(solution)/shard_map/ppermute | solution.py:87
  120.1 0.8 collective-permute-start.10
  120.9 0.4 fusion.6
  121.3 1.6 %fusion.4 = bf16[2368,2048]{1,0:T(8,128)(2,1)S(1)} fusion(bf16[2368,2048]{1,0:T(8,128)(2,1)S(1)} %fusion.6, bf16[2368,128]{1,0:T(8,128)(2,1)S(1)} %collective-permute-done.5, bf16[2368,128]{1,0:T(8,128)(2,1)} %collective-permute-done.6, pred[]{:T(512)S(6)} %eq.21), kind=kLoop, calls=%fused_computation.19 | loop fusion | flops 5455872 | bytes 2424833
  122.9 0.5 fusion.2
  123.4 0.5 fusion
  123.9 0.5 fusion.7
  124.4 1.6 %fusion.5 = bf16[2368,2048]{1,0:T(8,128)(2,1)S(1)} fusion(bf16[2368,2048]{1,0:T(8,128)(2,1)S(1)} %fusion.7, bf16[2368,128]{1,0:T(8,128)(2,1)S(1)} %collective-permute-done.5, bf16[2368,128]{1,0:T(8,128)(2,1)} %collective-permute-done.6, pred[]{:T(512)S(6)} %eq.21), kind=kLoop, calls=%fused_computation.20 | loop fusion | flops 5455872 | bytes 2424833
  126.0 0.5 fusion.3
  126.5 0.5 fusion.1
  127.0 3.0 %constant_dynamic-slice_fusion = bf16[2368,1024]{1,0:T(8,128)(2,1)} fusion(bf16[2368,2048]{1,0:T(8,128)(2,1)S(1)} %fusion.1, s32[]{:T(128)S(6)} %select_n.89), kind=kLoop, calls=%fused_computation.35 | loop fusion | bytes 9699332 | tf_op jit(solution)/shard_map/dynamic_slice | solution.py:95
  (27 shorter events, 0.4 us)
Async XLA Ops:
  53.6 15.5 %all-to-all-start.3 = ((f32[4,592,128]{2,1,0:T(8,128)}), f32[4,592,128]{2,1,0:T(8,128)S(1)}, u32[]{:S(2)}, u32[]{:S(2)}) async-start(f32[4,592,128]{2,1,0:T(8,128)} %broadcast_in_dim.41), calls=%async_computation.3 | async-start | bytes 2424832 | tf_op jit(solution)/shard_map/all_to_all | solution.py:62
  57.3 12.0 %copy-start.3 = (f32[2368,128]{1,0:T(8,128)S(1)}, f32[2368,128]{1,0:T(8,128)}, u32[]{:S(2)}) copy-start(f32[2368,128]{1,0:T(8,128)} %param.7) | copy-start | bytes 3637252
  69.0 1.3 copy-start.4
  70.3 1.3 copy-start.2
  70.7 2.2 %copy-start = (f32[2368,128]{1,0:T(8,128)}, f32[2368,128]{1,0:T(8,128)S(1)}, u32[]{:S(2)}) copy-start(f32[2368,128]{1,0:T(8,128)S(1)} %get-tuple-element.16) | copy-start | bytes 3637252
  70.7 2.2 %copy-start.1 = (f32[2368,128]{1,0:T(8,128)}, f32[2368,128]{1,0:T(8,128)S(1)}, u32[]{:S(2)}) copy-start(f32[2368,128]{1,0:T(8,128)S(1)} %get-tuple-element.17) | copy-start | bytes 3637252
  73.4 6.7 %collective-permute-start = (f32[8]{0:T(128)S(1)}, f32[8]{0:T(128)S(1)}, u32[]{:S(2)}, u32[]{:S(2)}) collective-permute-start(f32[8]{0:T(128)S(1)} %pad_maximum_fusion), channel_id=1, source_target_pairs={{0,1},{1,0},{2,3},{3,2},{4,5},{5,4},{6,7},{7,6},{8,9},{9,8},{10,11... | collective-permute-start | bytes 104 | tf_op jit(solution)/shard_map/ppermute | solution.py:68
  80.1 6.4 %collective-permute-start.3 = (f32[8]{0:T(128)S(1)}, f32[8]{0:T(128)S(1)}, u32[]{:S(2)}, u32[]{:S(2)}) collective-permute-start(f32[8]{0:T(128)S(1)} %fusion.19), channel_id=1, source_target_pairs={{0,2},{2,4},{4,6},{6,0},{1,3},{3,5},{5,7},{7,1},{8,10},{10,12},{12... | collective-permute-start | bytes 104 | tf_op jit(solution)/shard_map/ppermute | solution.py:75
  81.4 5.1 %collective-permute-start.2 = (f32[8]{0:T(128)S(1)}, f32[8]{0:T(128)S(1)}, u32[]{:S(2)}, u32[]{:S(2)}) collective-permute-start(f32[8]{0:T(128)S(1)} %fusion.19), channel_id=1, source_target_pairs={{0,4},{2,6},{4,0},{6,2},{1,5},{3,7},{5,1},{7,3},{8,12},{10,14},{12... | collective-permute-start | bytes 104 | tf_op jit(solution)/shard_map/ppermute | solution.py:75
  84.1 2.4 %collective-permute-start.1 = (f32[8]{0:T(128)S(1)}, f32[8]{0:T(128)S(1)}, u32[]{:S(2)}, u32[]{:S(2)}) collective-permute-start(f32[8]{0:T(128)S(1)} %fusion.19), channel_id=1, source_target_pairs={{0,6},{2,0},{4,2},{6,4},{1,7},{3,1},{5,3},{7,5},{8,14},{10,8},{12,... | collective-permute-start | bytes 104 | tf_op jit(solution)/shard_map/ppermute | solution.py:75
  88.3 13.8 %collective-permute-start.5 = (bf16[2368,128]{1,0:T(8,128)(2,1)S(1)}, bf16[2368,128]{1,0:T(8,128)(2,1)S(1)}, u32[]{:S(2)}, u32[]{:S(2)}) collective-permute-start(bf16[2368,128]{1,0:T(8,128)(2,1)S(1)} %get-tuple-element.5), channel_id=1, source_target_pairs={{0,6},{2,0},{4,2},{6,4},{1,7},{3,1},{5,3},{7,5},{8,14},{10,8},{12,... | collective-permute-start | bytes 1818632 | tf_op jit(solution)/shard_map/ppermute | solution.py:87
  90.6 27.5 %collective-permute-start.7 = (bf16[2368,128]{1,0:T(8,128)(2,1)S(1)}, bf16[2368,128]{1,0:T(8,128)(2,1)S(1)}, u32[]{:S(2)}, u32[]{:S(2)}) collective-permute-start(bf16[2368,128]{1,0:T(8,128)(2,1)S(1)} %get-tuple-element.5), channel_id=1, source_target_pairs={{0,4},{2,6},{4,0},{6,2},{1,5},{3,7},{5,1},{7,3},{8,12},{10,14},{12... | collective-permute-start | bytes 1818632 | tf_op jit(solution)/shard_map/ppermute | solution.py:87
  90.6 29.5 %collective-permute-start.9 = (bf16[2368,128]{1,0:T(8,128)(2,1)S(1)}, bf16[2368,128]{1,0:T(8,128)(2,1)S(1)}, u32[]{:S(2)}, u32[]{:S(2)}) collective-permute-start(bf16[2368,128]{1,0:T(8,128)(2,1)S(1)} %get-tuple-element.5), channel_id=1, source_target_pairs={{0,2},{2,4},{4,6},{6,0},{1,3},{3,5},{5,7},{7,1},{8,10},{10,12},{12... | collective-permute-start | bytes 1818632 | tf_op jit(solution)/shard_map/ppermute | solution.py:87
  91.2 29.7 %collective-permute-start.4 = (bf16[2368,128]{1,0:T(8,128)(2,1)S(1)}, bf16[2368,128]{1,0:T(8,128)(2,1)S(1)}, u32[]{:S(2)}, u32[]{:S(2)}) collective-permute-start(bf16[2368,128]{1,0:T(8,128)(2,1)S(1)} %get-tuple-element.5), channel_id=1, source_target_pairs={{0,1},{1,0},{2,3},{3,2},{4,5},{5,4},{6,7},{7,6},{8,9},{9,8},{10,11... | collective-permute-start | bytes 1818632 | tf_op jit(solution)/shard_map/ppermute | solution.py:88
  102.1 19.1 %collective-permute-start.6 = (bf16[2368,128]{1,0:T(8,128)(2,1)S(1)}, bf16[2368,128]{1,0:T(8,128)(2,1)}, u32[]{:S(2)}, u32[]{:S(2)}) collective-permute-start(bf16[2368,128]{1,0:T(8,128)(2,1)S(1)} %collective-permute-done.5), channel_id=1, source_target_pairs={{0,1},{1,0},{2,3},{3,2},{4,5},{5,4},{6,7},{7,6},{8,9},{9,8},{10,11... | collective-permute-start | bytes 1818632 | tf_op jit(solution)/shard_map/ppermute | solution.py:88
  118.1 4.9 %collective-permute-start.8 = (bf16[2368,128]{1,0:T(8,128)(2,1)S(1)}, bf16[2368,128]{1,0:T(8,128)(2,1)S(1)}, u32[]{:S(2)}, u32[]{:S(2)}) collective-permute-start(bf16[2368,128]{1,0:T(8,128)(2,1)S(1)} %collective-permute-done.7), channel_id=1, source_target_pairs={{0,1},{1,0},{2,3},{3,2},{4,5},{5,4},{6,7},{7,6},{8,9},{9,8},{10,11... | collective-permute-start | bytes 1818632 | tf_op jit(solution)/shard_map/ppermute | solution.py:88
  120.1 3.3 %collective-permute-start.10 = (bf16[2368,128]{1,0:T(8,128)(2,1)S(1)}, bf16[2368,128]{1,0:T(8,128)(2,1)S(1)}, u32[]{:S(2)}, u32[]{:S(2)}) collective-permute-start(bf16[2368,128]{1,0:T(8,128)(2,1)S(1)} %collective-permute-done.9), channel_id=1, source_target_pairs={{0,1},{1,0},{2,3},{3,2},{4,5},{5,4},{6,7},{7,6},{8,9},{9,8},{10,11... | collective-permute-start | bytes 1818632 | tf_op jit(solution)/shard_map/ppermute | solution.py:88

commit v4 on v3

--- a/solution.py
+++ b/solution.py
@@ -84,15 +84,15 @@
     y = lax.axis_index("y")
     core = lax.axis_index("core")
     swap = [(0, 1), (1, 0)]
-    mine = [b] + [lax.ppermute(b, "y", [(i, (i - s) % ny) for i in range(ny)]) for s in range(1, ny)]
-    other = [lax.ppermute(m, "core", swap) for m in mine]
-    pairs = [
-        jnp.where(core == 0, jnp.concatenate([m, o], 1), jnp.concatenate([o, m], 1))
-        for m, o in zip(mine, other)
-    ]
-    q = jnp.concatenate(pairs + pairs, 1)
-    width = 2 * b.shape[1]
-    return lax.dynamic_slice_in_dim(q, ((ny - y) % ny) * width, ny * width, 1)
+    width = b.shape[1]
+    out = jnp.zeros((b.shape[0], 2 * ny * width), b.dtype)
+    for s in range(ny):
+        mine = b if s == 0 else lax.ppermute(b, "y", [(i, (i - s) % ny) for i in range(ny)])
+        other = lax.ppermute(mine, "core", swap)
+        chip = (y + s) % ny
+        out = lax.dynamic_update_slice_in_dim(out, mine, (2 * chip + core) * width, 1)
+        out = lax.dynamic_update_slice_in_dim(out, other, (2 * chip + 1 - core) * width, 1)
+    return out
 
 
 def make_shards(nz, nx, ny, ncore):

time: 130 us -> 130 us (level)
  starting transfers between devices: 36 us -> 26.2 us
  waiting for transfers between devices: 24.3 us -> 32.8 us
  local copies, waits for them, and re-layouts: 6.31 us -> 12.8 us
  other arithmetic: 10.3 us -> 5.06 us
    ppermute x4, starting transfers between devices: 18.8 us -> 10.8 us  [tensor_gather(): other = lax.ppermute(mine, 'core', swap)]
    ppermute x3, waiting for transfers between devices: 10.4 us -> 17.4 us  [tensor_gather(): lax.ppermute(b, 'y', [(i, (i - s) % ny) for i in range(ny)])]
    dynamic_update_slice x0 -> x7, local copies, waits for them, and re-layouts: none -> 6.01 us  [the longest x4 3.44 us: tensor_gather(): lax.dynamic_update_slice_in_dim(out, other, (2 * chip + 1 - core) * width...]
    unnamed x7 -> x0, other arithmetic: 5.55 us -> none
    dynamic_slice x1 -> x0, local copies, waits for them, and re-layouts: 3.02 us -> none  [tensor_gather(): return lax.dynamic_slice_in_dim(q, (ny - y) % ny * width, ny * width, 1)]
    broadcast_in_dim x0 -> x1, local copies, waits for them, and re-layouts: none -> 2.85 us  [tensor_gather(): out = jnp.zeros((b.shape[0], 2 * ny * width), b.dtype)]
    dynamic_update_slice x0 -> x1, other arithmetic: none -> 1.6 us  [tensor_gather(): lax.dynamic_update_slice_in_dim(out, mine, (2 * chip + core) * width, 1)]
    ppermute x3, waiting for transfers between devices: 1.32 us -> 2.83 us  [tensor_sum(): got = lax.ppermute(v, 'y', [(i, (i - s) % ny) for i in range(ny)])]
  transfers between devices with their start and end apart: 12 -> 12, of which waited for: 5 -> 5; matrix products, arithmetic and copies ran while one was open for 3% -> 5% of each run, Pallas kernels for 0% -> 0%
where the time goes in v4:
time: 130 us
  blocking collectives  51.6 us (40%)
  waiting for transfers between devices  32.8 us (25%)
  starting transfers between devices  26.2 us (20%)
  local copies, waits for them, and re-layouts  12.8 us (10%)
  other arithmetic  5.06 us (4%)
    all_to_all x1, blocking collectives, dp_sum(): y = lax.all_to_all(x.reshape(nx, part, cols), 'x', 0, 0, tiled=False).sum(0)  19.9 us
    all_to_all x1, blocking collectives, dp_sum(): lax.all_to_all(y.reshape(nz, padded // nz, cols), 'z', 0, 0, tiled=False)  19.2 us
    ppermute x3, waiting for transfers between devices, tensor_gather(): lax.ppermute(b, 'y', [(i, (i - s) % ny) for i in range(ny)])  17.4 us
    all_to_all x1, blocking collectives, dp_sum(): lax.all_to_all(jnp.broadcast_to(y[None], (nz,) + y.shape), 'z', 0, 0, til...  12.5 us
    all_to_all x1, waiting for transfers between devices, dp_sum(): lax.all_to_all(jnp.broadcast_to(y[None], (nx,) + y.shape), 'x', 0, 0, til...  11.7 us
    ppermute x4, starting transfers between devices, tensor_gather(): other = lax.ppermute(mine, 'core', swap)  10.8 us
    ppermute x1, starting transfers between devices, tensor_sum(): v = v + lax.ppermute(v, 'core', [(0, 1), (1, 0)])  5.88 us
    ppermute x3, starting transfers between devices, tensor_sum(): got = lax.ppermute(v, 'y', [(i, (i - s) % ny) for i in range(ny)])  3.78 us
  transfers between devices with their start and end apart: 12, of which 5 were waited for; matrix products, arithmetic and copies ran while one was open for 5% of the time, Pallas kernels for 0%

profile of v4, /device:TPU:1, one launch (start us, length us, event | category | flops | bytes accessed | tf_op | source)
XLA Modules:
  0.0 130.0 jit_solution(13961228799887115865)
XLA Ops:
  0.6 19.9 %all_to_all.20 = f32[4,592,128]{2,1,0:T(8,128)S(1)} all-to-all(f32[4,592,128]{2,1,0:T(8,128)} %bitcast.27), channel_id=1, replica_groups=mesh['z'=8,'x'=4,'y'=4,'core'=2] {'x'}, dimensions={0} | all-to-all | bytes 2424832 | tf_op jit(solution)/shard_map/all_to_all | solution.py:57
  20.6 0.1 reduce_sum.37
  20.7 19.2 %all_to_all.21 = f32[8,80,128]{2,1,0:T(8,128)S(1)} all-to-all(f32[8,80,128]{2,1,0:T(8,128)S(1)} %bitcast.25), channel_id=1, replica_groups=mesh['z'=8,'x'=4,'y'=4,'core'=2] {'z'}, dimensions={0} | all-to-all | bytes 655360 | tf_op jit(solution)/shard_map/all_to_all | solution.py:59
  39.9 12.5 %all_to_all.22 = f32[8,80,128]{2,1,0:T(8,128)S(1)} all-to-all(f32[8,80,128]{2,1,0:T(8,128)S(1)} %broadcast_in_dim.43), channel_id=1, replica_groups=mesh['z'=8,'x'=4,'y'=4,'core'=2] {'z'}, dimensions={0} | all-to-all | bytes 655360 | tf_op jit(solution)/shard_map/all_to_all | solution.py:60
  52.5 1.1 broadcast_in_dim.44
  53.6 3.5 %all-to-all-start.3 = ((f32[4,592,128]{2,1,0:T(8,128)}), f32[4,592,128]{2,1,0:T(8,128)S(1)}, u32[]{:S(2)}, u32[]{:S(2)}) async-start(f32[4,592,128]{2,1,0:T(8,128)} %broadcast_in_dim.44), calls=%async_computation.3 | async-start | bytes 2424832 | tf_op jit(solution)/shard_map/all_to_all | solution.py:62
  57.3 11.7 %all-to-all-done.3 = f32[4,592,128]{2,1,0:T(8,128)S(1)} async-done(((f32[4,592,128]{2,1,0:T(8,128)}), f32[4,592,128]{2,1,0:T(8,128)S(1)}, u32[]{:S(2)}, u32[]{:S(2)}) %all-to-all-start.3) | async-done | bytes 1212448 | tf_op jit(solution)/shard_map/all_to_all | solution.py:62
  69.0 0.2 broadcast_multiply_fusion
  69.2 1.1 copy-done.5
  70.3 0.4 copy-done.6
  70.7 0.3 bitcast_add_fusion
  70.9 0.0 copy-start
  70.9 0.0 copy-start.1
  71.0 1.2 copy-done.2
  72.1 2.0 %multiply_reduce_fusion = (f32[2368]{0:T(1024)S(1)}, f32[2368,128]{1,0:T(8,128)}, f32[2368]{0:T(1024)S(1)}) fusion(f32[2368,128]{1,0:T(8,128)S(1)} %copy-done.2, f32[2368]{0:T(1024)S(1)} %fusion.1, f32[2368,128]{1,0:T(8,128)S(1)} %get-tuple-element.17, f32[2368,128]{1,0:T(8,128)S(1)} %get-tuple-element.18), kind=kLoop, calls=%fused_computation.3 | loop fusion | flops 3026304 | bytes 4878080 | tf_op jit(solution)/shard_map/reduce_sum | solution.py:32
  74.2 0.1 convolution_bitcast_fusion.1
  74.3 0.2 convolution_bitcast_fusion
  74.5 0.1 pad_maximum_fusion
  74.6 5.9 %collective-permute-start = (f32[8]{0:T(128)S(1)}, f32[8]{0:T(128)S(1)}, u32[]{:S(2)}, u32[]{:S(2)}) collective-permute-start(f32[8]{0:T(128)S(1)} %pad_maximum_fusion), channel_id=1, source_target_pairs={{0,1},{1,0},{2,3},{3,2},{4,5},{5,4},{6,7},{7,6},{8,9},{9,8},{10,11... | collective-permute-start | bytes 104 | tf_op jit(solution)/shard_map/ppermute | solution.py:68
  80.5 0.8 collective-permute-done
  81.3 0.1 fusion.10
  81.4 2.7 %collective-permute-start.1 = (f32[8]{0:T(128)S(1)}, f32[8]{0:T(128)S(1)}, u32[]{:S(2)}, u32[]{:S(2)}) collective-permute-start(f32[8]{0:T(128)S(1)} %fusion.10), channel_id=1, source_target_pairs={{0,6},{2,0},{4,2},{6,4},{1,7},{3,1},{5,3},{7,5},{8,14},{10,8},{12,... | collective-permute-start | bytes 104 | tf_op jit(solution)/shard_map/ppermute | solution.py:75
  84.1 0.3 collective-permute-start.2
  84.5 0.7 collective-permute-start.3
  85.3 2.8 %collective-permute-done.2 = f32[8]{0:T(128)S(1)} collective-permute-done((f32[8]{0:T(128)S(1)}, f32[8]{0:T(128)S(1)}, u32[]{:S(2)}, u32[]{:S(2)}) %collective-permute-start.2) | collective-permute-done | bytes 64 | tf_op jit(solution)/shard_map/ppermute | solution.py:75
  88.1 0.0 collective-permute-done.3
  88.2 0.3 convolution_reduce_fusion
  88.4 0.0 copy-start.3
  88.5 0.0 copy-start.4
  88.5 2.8 %broadcast_in_dim.49 = bf16[2368,1024]{1,0:T(8,128)(2,1)} broadcast(bf16[]{:T(256)} %constant.97.clone.1), dimensions={} | broadcast | bytes 4849666 | tf_op jit(solution)/shard_map/broadcast_in_dim | solution.py:88
  91.3 1.6 %constant_dynamic-update-slice_fusion.7 = (bf16[2368,1024]{1,0:T(8,128)(2,1)}, bf16[2368,128]{1,0:T(8,128)(2,1)S(1)}, f32[2368,128]{1,0:T(8,128)}) fusion(bf16[2368,1024]{1,0:T(8,128)(2,1)} %broadcast_in_dim.49, s32[]{:T(128)S(6)} %select_n.91, f32[2368,128]{1,0:T(8,128)S(1)} %copy-done.3, f32[2368,128]{1,0:T(8,128)S(1)} %copy-done.4, ...), kind=kLoop, calls=%fused_computation.26 | loop fusion | flops 909312 | bytes 4859140 | tf_op jit(solution)/shard_map/dynamic_update_slice | solution.py:93
  92.9 0.4 collective-permute-start.5
  93.4 1.0 collective-permute-start.7
  94.3 0.9 collective-permute-start.9
  95.2 2.9 %collective-permute-start.4 = (bf16[2368,128]{1,0:T(8,128)(2,1)S(1)}, bf16[2368,128]{1,0:T(8,128)(2,1)S(1)}, u32[]{:S(2)}, u32[]{:S(2)}) collective-permute-start(bf16[2368,128]{1,0:T(8,128)(2,1)S(1)} %get-tuple-element.6), channel_id=1, source_target_pairs={{0,1},{1,0},{2,3},{3,2},{4,5},{5,4},{6,7},{7,6},{8,9},{9,8},{10,11... | collective-permute-start | bytes 1818632 | tf_op jit(solution)/shard_map/ppermute | solution.py:91
  98.1 0.6 fusion.9
  98.7 7.4 %collective-permute-done.5 = bf16[2368,128]{1,0:T(8,128)(2,1)S(1)} collective-permute-done((bf16[2368,128]{1,0:T(8,128)(2,1)S(1)}, bf16[2368,128]{1,0:T(8,128)(2,1)S(1)}, u32[]{:S(2)}, u32[]{:S(2)}) %collective-permute-start.5) | collective-permute-done | bytes 606240 | tf_op jit(solution)/shard_map/ppermute | solution.py:90
  106.1 5.4 %collective-permute-start.6 = (bf16[2368,128]{1,0:T(8,128)(2,1)S(1)}, bf16[2368,128]{1,0:T(8,128)(2,1)S(1)}, u32[]{:S(2)}, u32[]{:S(2)}) collective-permute-start(bf16[2368,128]{1,0:T(8,128)(2,1)S(1)} %collective-permute-done.5), channel_id=1, source_target_pairs={{0,1},{1,0},{2,3},{3,2},{4,5},{5,4},{6,7},{7,6},{8,9},{9,8},{10,11... | collective-permute-start | bytes 1818632 | tf_op jit(solution)/shard_map/ppermute | solution.py:91
  111.5 2.0 %collective-permute-start.8 = (bf16[2368,128]{1,0:T(8,128)(2,1)S(1)}, bf16[2368,128]{1,0:T(8,128)(2,1)S(1)}, u32[]{:S(2)}, u32[]{:S(2)}) collective-permute-start(bf16[2368,128]{1,0:T(8,128)(2,1)S(1)} %collective-permute-done.7), channel_id=1, source_target_pairs={{0,1},{1,0},{2,3},{3,2},{4,5},{5,4},{6,7},{7,6},{8,9},{9,8},{10,11... | collective-permute-start | bytes 1818632 | tf_op jit(solution)/shard_map/ppermute | solution.py:91
  113.5 10.0 %collective-permute-done.9 = bf16[2368,128]{1,0:T(8,128)(2,1)S(1)} collective-permute-done((bf16[2368,128]{1,0:T(8,128)(2,1)S(1)}, bf16[2368,128]{1,0:T(8,128)(2,1)S(1)}, u32[]{:S(2)}, u32[]{:S(2)}) %collective-permute-start.9) | collective-permute-done | bytes 606240 | tf_op jit(solution)/shard_map/ppermute | solution.py:90
  123.5 0.5 collective-permute-start.10
  124.0 0.9 constant_dynamic-update-slice_fusion.6
  124.8 0.9 constant_dynamic-update-slice_fusion.5
  125.7 0.9 constant_dynamic-update-slice_fusion.4
  126.5 0.9 constant_dynamic-update-slice_fusion.3
  127.4 0.9 constant_dynamic-update-slice_fusion.2
  128.3 0.9 constant_dynamic-update-slice_fusion.1
  129.1 0.9 constant_dynamic-update-slice_fusion
  (30 shorter events, 0.4 us)
Async XLA Ops:
  53.6 15.5 %all-to-all-start.3 = ((f32[4,592,128]{2,1,0:T(8,128)}), f32[4,592,128]{2,1,0:T(8,128)S(1)}, u32[]{:S(2)}, u32[]{:S(2)}) async-start(f32[4,592,128]{2,1,0:T(8,128)} %broadcast_in_dim.44), calls=%async_computation.3 | async-start | bytes 2424832 | tf_op jit(solution)/shard_map/all_to_all | solution.py:62
  69.0 1.3 copy-start.5
  69.0 1.6 %copy-start.6 = (f32[2368,128]{1,0:T(8,128)S(1)}, f32[2368,128]{1,0:T(8,128)}, u32[]{:S(2)}) copy-start(f32[2368,128]{1,0:T(8,128)} %param.6) | copy-start | bytes 3637252
  70.7 1.5 %copy-start.2 = (f32[2368,128]{1,0:T(8,128)S(1)}, f32[2368,128]{1,0:T(8,128)}, u32[]{:S(2)}) copy-start(f32[2368,128]{1,0:T(8,128)} %param.5) | copy-start | bytes 3637252
  70.9 3.2 %copy-start = (f32[2368,128]{1,0:T(8,128)}, f32[2368,128]{1,0:T(8,128)S(1)}, u32[]{:S(2)}) copy-start(f32[2368,128]{1,0:T(8,128)S(1)} %get-tuple-element.17) | copy-start | bytes 3637252
  70.9 3.2 %copy-start.1 = (f32[2368,128]{1,0:T(8,128)}, f32[2368,128]{1,0:T(8,128)S(1)}, u32[]{:S(2)}) copy-start(f32[2368,128]{1,0:T(8,128)S(1)} %get-tuple-element.18) | copy-start | bytes 3637252
  74.6 6.7 %collective-permute-start = (f32[8]{0:T(128)S(1)}, f32[8]{0:T(128)S(1)}, u32[]{:S(2)}, u32[]{:S(2)}) collective-permute-start(f32[8]{0:T(128)S(1)} %pad_maximum_fusion), channel_id=1, source_target_pairs={{0,1},{1,0},{2,3},{3,2},{4,5},{5,4},{6,7},{7,6},{8,9},{9,8},{10,11... | collective-permute-start | bytes 104 | tf_op jit(solution)/shard_map/ppermute | solution.py:68
  81.4 3.8 %collective-permute-start.1 = (f32[8]{0:T(128)S(1)}, f32[8]{0:T(128)S(1)}, u32[]{:S(2)}, u32[]{:S(2)}) collective-permute-start(f32[8]{0:T(128)S(1)} %fusion.10), channel_id=1, source_target_pairs={{0,6},{2,0},{4,2},{6,4},{1,7},{3,1},{5,3},{7,5},{8,14},{10,8},{12,... | collective-permute-start | bytes 104 | tf_op jit(solution)/shard_map/ppermute | solution.py:75
  84.1 3.9 %collective-permute-start.2 = (f32[8]{0:T(128)S(1)}, f32[8]{0:T(128)S(1)}, u32[]{:S(2)}, u32[]{:S(2)}) collective-permute-start(f32[8]{0:T(128)S(1)} %fusion.10), channel_id=1, source_target_pairs={{0,4},{2,6},{4,0},{6,2},{1,5},{3,7},{5,1},{7,3},{8,12},{10,14},{12... | collective-permute-start | bytes 104 | tf_op jit(solution)/shard_map/ppermute | solution.py:75
  84.5 3.6 %collective-permute-start.3 = (f32[8]{0:T(128)S(1)}, f32[8]{0:T(128)S(1)}, u32[]{:S(2)}, u32[]{:S(2)}) collective-permute-start(f32[8]{0:T(128)S(1)} %fusion.10), channel_id=1, source_target_pairs={{0,2},{2,4},{4,6},{6,0},{1,3},{3,5},{5,7},{7,1},{8,10},{10,12},{12... | collective-permute-start | bytes 104 | tf_op jit(solution)/shard_map/ppermute | solution.py:75
  88.4 2.9 %copy-start.3 = (f32[2368,128]{1,0:T(8,128)S(1)}, f32[2368,128]{1,0:T(8,128)}, u32[]{:S(2)}) copy-start(f32[2368,128]{1,0:T(8,128)} %param.5) | copy-start | bytes 3637252
  88.5 2.9 %copy-start.4 = (f32[2368,128]{1,0:T(8,128)S(1)}, f32[2368,128]{1,0:T(8,128)}, u32[]{:S(2)}) copy-start(f32[2368,128]{1,0:T(8,128)} %get-tuple-element.9) | copy-start | bytes 3637252
  92.9 13.2 %collective-permute-start.5 = (bf16[2368,128]{1,0:T(8,128)(2,1)S(1)}, bf16[2368,128]{1,0:T(8,128)(2,1)S(1)}, u32[]{:S(2)}, u32[]{:S(2)}) collective-permute-start(bf16[2368,128]{1,0:T(8,128)(2,1)S(1)} %get-tuple-element.6), channel_id=1, source_target_pairs={{0,6},{2,0},{4,2},{6,4},{1,7},{3,1},{5,3},{7,5},{8,14},{10,8},{12,... | collective-permute-start | bytes 1818632 | tf_op jit(solution)/shard_map/ppermute | solution.py:90
  93.4 18.2 %collective-permute-start.7 = (bf16[2368,128]{1,0:T(8,128)(2,1)S(1)}, bf16[2368,128]{1,0:T(8,128)(2,1)S(1)}, u32[]{:S(2)}, u32[]{:S(2)}) collective-permute-start(bf16[2368,128]{1,0:T(8,128)(2,1)S(1)} %get-tuple-element.6), channel_id=1, source_target_pairs={{0,4},{2,6},{4,0},{6,2},{1,5},{3,7},{5,1},{7,3},{8,12},{10,14},{12... | collective-permute-start | bytes 1818632 | tf_op jit(solution)/shard_map/ppermute | solution.py:90
  94.3 29.1 %collective-permute-start.9 = (bf16[2368,128]{1,0:T(8,128)(2,1)S(1)}, bf16[2368,128]{1,0:T(8,128)(2,1)S(1)}, u32[]{:S(2)}, u32[]{:S(2)}) collective-permute-start(bf16[2368,128]{1,0:T(8,128)(2,1)S(1)} %get-tuple-element.6), channel_id=1, source_target_pairs={{0,2},{2,4},{4,6},{6,0},{1,3},{3,5},{5,7},{7,1},{8,10},{10,12},{12... | collective-permute-start | bytes 1818632 | tf_op jit(solution)/shard_map/ppermute | solution.py:90
  95.2 28.8 %collective-permute-start.4 = (bf16[2368,128]{1,0:T(8,128)(2,1)S(1)}, bf16[2368,128]{1,0:T(8,128)(2,1)S(1)}, u32[]{:S(2)}, u32[]{:S(2)}) collective-permute-start(bf16[2368,128]{1,0:T(8,128)(2,1)S(1)} %get-tuple-element.6), channel_id=1, source_target_pairs={{0,1},{1,0},{2,3},{3,2},{4,5},{5,4},{6,7},{7,6},{8,9},{9,8},{10,11... | collective-permute-start | bytes 1818632 | tf_op jit(solution)/shard_map/ppermute | solution.py:91
  106.1 19.6 %collective-permute-start.6 = (bf16[2368,128]{1,0:T(8,128)(2,1)S(1)}, bf16[2368,128]{1,0:T(8,128)(2,1)S(1)}, u32[]{:S(2)}, u32[]{:S(2)}) collective-permute-start(bf16[2368,128]{1,0:T(8,128)(2,1)S(1)} %collective-permute-done.5), channel_id=1, source_target_pairs={{0,1},{1,0},{2,3},{3,2},{4,5},{5,4},{6,7},{7,6},{8,9},{9,8},{10,11... | collective-permute-start | bytes 1818632 | tf_op jit(solution)/shard_map/ppermute | solution.py:91
  111.5 15.9 %collective-permute-start.8 = (bf16[2368,128]{1,0:T(8,128)(2,1)S(1)}, bf16[2368,128]{1,0:T(8,128)(2,1)S(1)}, u32[]{:S(2)}, u32[]{:S(2)}) collective-permute-start(bf16[2368,128]{1,0:T(8,128)(2,1)S(1)} %collective-permute-done.7), channel_id=1, source_target_pairs={{0,1},{1,0},{2,3},{3,2},{4,5},{5,4},{6,7},{7,6},{8,9},{9,8},{10,11... | collective-permute-start | bytes 1818632 | tf_op jit(solution)/shard_map/ppermute | solution.py:91
  123.5 5.7 %collective-permute-start.10 = (bf16[2368,128]{1,0:T(8,128)(2,1)S(1)}, bf16[2368,128]{1,0:T(8,128)(2,1)S(1)}, u32[]{:S(2)}, u32[]{:S(2)}) collective-permute-start(bf16[2368,128]{1,0:T(8,128)(2,1)S(1)} %collective-permute-done.9), channel_id=1, source_target_pairs={{0,1},{1,0},{2,3},{3,2},{4,5},{5,4},{6,7},{7,6},{8,9},{9,8},{10,11... | collective-permute-start | bytes 1818632 | tf_op jit(solution)/shard_map/ppermute | solution.py:91

commit v5 on v4

--- a/solution.py
+++ b/solution.py
@@ -84,14 +84,23 @@
     y = lax.axis_index("y")
     core = lax.axis_index("core")
     swap = [(0, 1), (1, 0)]
-    width = b.shape[1]
-    out = jnp.zeros((b.shape[0], 2 * ny * width), b.dtype)
-    for s in range(ny):
-        mine = b if s == 0 else lax.ppermute(b, "y", [(i, (i - s) % ny) for i in range(ny)])
+    rows, width = b.shape
+
+    def shift(v, s):
+        return lax.ppermute(v, "y", [(i, (i - s) % ny) for i in range(ny)])
+
+    if ny == 4 and rows % 16 == 0:
+        half = rows // 2
+        plus, minus = shift(b, 1), shift(b, -1)
+        pieces = [(b, 0, 0), (plus, 1, 0), (minus, 3, 0), (shift(plus[:half], 1), 2, 0), (shift(minus[half:], -1), 2, half)]
+    else:
+        pieces = [(b, 0, 0)] + [(shift(b, s), s, 0) for s in range(1, ny)]
+    out = jnp.zeros((rows, 2 * ny * width), b.dtype)
+    for mine, s, row in pieces:
         other = lax.ppermute(mine, "core", swap)
         chip = (y + s) % ny
-        out = lax.dynamic_update_slice_in_dim(out, mine, (2 * chip + core) * width, 1)
-        out = lax.dynamic_update_slice_in_dim(out, other, (2 * chip + 1 - core) * width, 1)
+        out = lax.dynamic_update_slice(out, mine, (row, (2 * chip + core) * width))
+        out = lax.dynamic_update_slice(out, other, (row, (2 * chip + 1 - core) * width))
     return out
 
 

time: 130 us -> 125 us (0.962)
  waiting for transfers between devices: 32.8 us -> 23.9 us
  starting transfers between devices: 26.2 us -> 28.6 us
    ppermute x3 -> x4, waiting for transfers between devices: 17.4 us -> 8.51 us  [shift(): return lax.ppermute(v, 'y', [(i, (i - s) % ny) for i in range(ny)])]
    ppermute x3 -> x4, starting transfers between devices: 2.27 us -> 3.56 us  [shift(): return lax.ppermute(v, 'y', [(i, (i - s) % ny) for i in range(ny)])]
    dynamic_update_slice x7 -> x9, local copies, waits for them, and re-layouts: 6.01 us -> 7.24 us  [the longest x5 4.05 us: tensor_gather(): lax.dynamic_update_slice(out, other, (row, (2 * chip + 1 - core) * width))]
    ppermute x4 -> x5, starting transfers between devices: 10.8 us -> 11.8 us  [tensor_gather(): other = lax.ppermute(mine, 'core', swap)]
  transfers between devices with their start and end apart: 12 -> 14, of which waited for: 5 -> 4; matrix products, arithmetic and copies ran while one was open for 5% -> 6% of each run, Pallas kernels for 0% -> 0%
where the time goes in v5:
time: 125 us
  blocking collectives  51.6 us (41%)
  starting transfers between devices  28.6 us (23%)
  waiting for transfers between devices  23.9 us (19%)
  local copies, waits for them, and re-layouts  14.1 us (11%)
  other arithmetic  5.06 us (4%)
    all_to_all x1, blocking collectives, dp_sum(): y = lax.all_to_all(x.reshape(nx, part, cols), 'x', 0, 0, tiled=False).sum(0)  19.9 us
    all_to_all x1, blocking collectives, dp_sum(): lax.all_to_all(y.reshape(nz, padded // nz, cols), 'z', 0, 0, tiled=False)  19.2 us
    all_to_all x1, blocking collectives, dp_sum(): lax.all_to_all(jnp.broadcast_to(y[None], (nz,) + y.shape), 'z', 0, 0, til...  12.5 us
    ppermute x5, starting transfers between devices, tensor_gather(): other = lax.ppermute(mine, 'core', swap)  11.8 us
    all_to_all x1, waiting for transfers between devices, dp_sum(): lax.all_to_all(jnp.broadcast_to(y[None], (nx,) + y.shape), 'x', 0, 0, til...  11.7 us
    ppermute x4, waiting for transfers between devices, shift(): return lax.ppermute(v, 'y', [(i, (i - s) % ny) for i in range(ny)])  8.51 us
    ppermute x1, starting transfers between devices, tensor_sum(): v = v + lax.ppermute(v, 'core', [(0, 1), (1, 0)])  5.88 us
    dynamic_update_slice x5, local copies, waits for them, and re-layouts, tensor_gather(): lax.dynamic_update_slice(out, other, (row, (2 * chip + 1 - core) * width))  4.05 us
  transfers between devices with their start and end apart: 14, of which 4 were waited for; matrix products, arithmetic and copies ran while one was open for 6% of the time, Pallas kernels for 0%

profile of v5, /device:TPU:1, one launch (start us, length us, event | category | flops | bytes accessed | tf_op | source)
XLA Modules:
  0.0 124.7 jit_solution(1352793305370808739)
XLA Ops:
  0.6 19.9 %all_to_all.20 = f32[4,592,128]{2,1,0:T(8,128)S(1)} all-to-all(f32[4,592,128]{2,1,0:T(8,128)} %bitcast.27), channel_id=1, replica_groups=mesh['z'=8,'x'=4,'y'=4,'core'=2] {'x'}, dimensions={0} | all-to-all | bytes 2424832 | tf_op jit(solution)/shard_map/all_to_all | solution.py:57
  20.6 0.1 reduce_sum.37
  20.7 19.2 %all_to_all.21 = f32[8,80,128]{2,1,0:T(8,128)S(1)} all-to-all(f32[8,80,128]{2,1,0:T(8,128)S(1)} %bitcast.25), channel_id=1, replica_groups=mesh['z'=8,'x'=4,'y'=4,'core'=2] {'z'}, dimensions={0} | all-to-all | bytes 655360 | tf_op jit(solution)/shard_map/all_to_all | solution.py:59
  39.9 12.5 %all_to_all.22 = f32[8,80,128]{2,1,0:T(8,128)S(1)} all-to-all(f32[8,80,128]{2,1,0:T(8,128)S(1)} %broadcast_in_dim.43), channel_id=1, replica_groups=mesh['z'=8,'x'=4,'y'=4,'core'=2] {'z'}, dimensions={0} | all-to-all | bytes 655360 | tf_op jit(solution)/shard_map/all_to_all | solution.py:60
  52.5 1.1 broadcast_in_dim.44
  53.6 3.5 %all-to-all-start.3 = ((f32[4,592,128]{2,1,0:T(8,128)}), f32[4,592,128]{2,1,0:T(8,128)S(1)}, u32[]{:S(2)}, u32[]{:S(2)}) async-start(f32[4,592,128]{2,1,0:T(8,128)} %broadcast_in_dim.44), calls=%async_computation.3 | async-start | bytes 2424832 | tf_op jit(solution)/shard_map/all_to_all | solution.py:62
  57.3 11.7 %all-to-all-done.3 = f32[4,592,128]{2,1,0:T(8,128)S(1)} async-done(((f32[4,592,128]{2,1,0:T(8,128)}), f32[4,592,128]{2,1,0:T(8,128)S(1)}, u32[]{:S(2)}, u32[]{:S(2)}) %all-to-all-start.3) | async-done | bytes 1212448 | tf_op jit(solution)/shard_map/all_to_all | solution.py:62
  69.0 0.2 broadcast_multiply_fusion
  69.2 1.1 copy-done.5
  70.3 0.4 copy-done.6
  70.7 0.3 bitcast_add_fusion
  70.9 0.0 copy-start.1
  71.0 1.2 copy-done.2
  72.1 2.0 %multiply_reduce_fusion = (f32[2368]{0:T(1024)S(1)}, f32[2368,128]{1,0:T(8,128)}, f32[2368]{0:T(1024)S(1)}) fusion(f32[2368,128]{1,0:T(8,128)S(1)} %copy-done.2, f32[2368]{0:T(1024)S(1)} %fusion.1, f32[2368,128]{1,0:T(8,128)S(1)} %get-tuple-element.17, f32[2368,128]{1,0:T(8,128)S(1)} %get-tuple-element.18), kind=kLoop, calls=%fused_computation.3 | loop fusion | flops 3026304 | bytes 4878080 | tf_op jit(solution)/shard_map/reduce_sum | solution.py:32
  74.2 0.1 convolution_bitcast_fusion.1
  74.3 0.2 convolution_bitcast_fusion
  74.5 0.1 pad_maximum_fusion
  74.6 5.9 %collective-permute-start = (f32[8]{0:T(128)S(1)}, f32[8]{0:T(128)S(1)}, u32[]{:S(2)}, u32[]{:S(2)}) collective-permute-start(f32[8]{0:T(128)S(1)} %pad_maximum_fusion), channel_id=1, source_target_pairs={{0,1},{1,0},{2,3},{3,2},{4,5},{5,4},{6,7},{7,6},{8,9},{9,8},{10,11... | collective-permute-start | bytes 104 | tf_op jit(solution)/shard_map/ppermute | solution.py:68
  80.5 0.8 collective-permute-done
  81.3 0.1 fusion.10
  81.4 2.7 %collective-permute-start.1 = (f32[8]{0:T(128)S(1)}, f32[8]{0:T(128)S(1)}, u32[]{:S(2)}, u32[]{:S(2)}) collective-permute-start(f32[8]{0:T(128)S(1)} %fusion.10), channel_id=1, source_target_pairs={{0,6},{2,0},{4,2},{6,4},{1,7},{3,1},{5,3},{7,5},{8,14},{10,8},{12,... | collective-permute-start | bytes 104 | tf_op jit(solution)/shard_map/ppermute | solution.py:75
  84.1 0.3 collective-permute-start.2
  84.5 0.7 collective-permute-start.3
  85.3 2.8 %collective-permute-done.2 = f32[8]{0:T(128)S(1)} collective-permute-done((f32[8]{0:T(128)S(1)}, f32[8]{0:T(128)S(1)}, u32[]{:S(2)}, u32[]{:S(2)}) %collective-permute-start.2) | collective-permute-done | bytes 64 | tf_op jit(solution)/shard_map/ppermute | solution.py:75
  88.1 0.0 collective-permute-done.3
  88.2 0.3 convolution_reduce_fusion
  88.5 2.8 %broadcast_in_dim.49 = bf16[2368,1024]{1,0:T(8,128)(2,1)} broadcast(bf16[]{:T(256)} %constant.100.clone.1), dimensions={} | broadcast | bytes 4849666 | tf_op jit(solution)/shard_map/broadcast_in_dim | solution.py:98
  91.3 1.6 %constant_dynamic-update-slice_fusion.7 = (bf16[2368,1024]{1,0:T(8,128)(2,1)}, bf16[2368,128]{1,0:T(8,128)(2,1)S(1)}, f32[2368,128]{1,0:T(8,128)}) fusion(bf16[2368,1024]{1,0:T(8,128)(2,1)} %broadcast_in_dim.49, s32[]{:T(128)S(6)} %select_n.95, f32[2368,128]{1,0:T(8,128)S(1)} %copy-done.3, f32[2368,128]{1,0:T(8,128)S(1)} %copy-done.4, ...), kind=kLoop, calls=%fused_computation.26 | loop fusion | flops 909312 | bytes 4859140 | tf_op jit(solution)/shard_map/dynamic_update_slice | solution.py:102
  92.9 0.4 collective-permute-start.5
  93.4 1.0 collective-permute-start.7
  94.4 2.6 %collective-permute-start.4 = (bf16[2368,128]{1,0:T(8,128)(2,1)S(1)}, bf16[2368,128]{1,0:T(8,128)(2,1)S(1)}, u32[]{:S(2)}, u32[]{:S(2)}) collective-permute-start(bf16[2368,128]{1,0:T(8,128)(2,1)S(1)} %get-tuple-element.6), channel_id=1, source_target_pairs={{0,1},{1,0},{2,3},{3,2},{4,5},{5,4},{6,7},{7,6},{8,9},{9,8},{10,11... | collective-permute-start | bytes 1818632 | tf_op jit(solution)/shard_map/ppermute | solution.py:100
  97.0 0.6 fusion.9
  97.6 8.5 %collective-permute-done.5 = bf16[2368,128]{1,0:T(8,128)(2,1)S(1)} collective-permute-done((bf16[2368,128]{1,0:T(8,128)(2,1)S(1)}, bf16[2368,128]{1,0:T(8,128)(2,1)S(1)}, u32[]{:S(2)}, u32[]{:S(2)}) %collective-permute-start.5) | collective-permute-done | bytes 606240 | tf_op jit(solution)/shard_map/ppermute | solution.py:90
  106.1 2.0 %collective-permute-start.9 = (bf16[1184,128]{1,0:T(8,128)(2,1)S(1)}, bf16[1184,128]{1,0:T(8,128)(2,1)S(1)}, u32[]{:S(2)}, u32[]{:S(2)}) collective-permute-start(bf16[1184,128]{1,0:T(8,128)(2,1)S(1)} %slice.49), channel_id=1, source_target_pairs={{0,6},{2,0},{4,2},{6,4},{1,7},{3,1},{5,3},{7,5},{8,14},{10,8},{12,... | collective-permute-start | bytes 909320 | tf_op jit(solution)/shard_map/ppermute | solution.py:90
  108.2 0.1 collective-permute-start.11
  108.3 3.0 %collective-permute-start.6 = (bf16[2368,128]{1,0:T(8,128)(2,1)S(1)}, bf16[2368,128]{1,0:T(8,128)(2,1)S(1)}, u32[]{:S(2)}, u32[]{:S(2)}) collective-permute-start(bf16[2368,128]{1,0:T(8,128)(2,1)S(1)} %collective-permute-done.5), channel_id=1, source_target_pairs={{0,1},{1,0},{2,3},{3,2},{4,5},{5,4},{6,7},{7,6},{8,9},{9,8},{10,11... | collective-permute-start | bytes 1818632 | tf_op jit(solution)/shard_map/ppermute | solution.py:100
  111.3 0.1 collective-permute-start.8
  111.4 0.9 constant_dynamic-update-slice_fusion.6
  112.2 0.9 constant_dynamic-update-slice_fusion.5
  113.1 2.8 %collective-permute-start.10 = (bf16[1184,128]{1,0:T(8,128)(2,1)S(1)}, bf16[1184,128]{1,0:T(8,128)(2,1)S(1)}, u32[]{:S(2)}, u32[]{:S(2)}) collective-permute-start(bf16[1184,128]{1,0:T(8,128)(2,1)S(1)} %collective-permute-done.9), channel_id=1, source_target_pairs={{0,1},{1,0},{2,3},{3,2},{4,5},{5,4},{6,7},{7,6},{8,9},{9,8},{10,11... | collective-permute-start | bytes 909320 | tf_op jit(solution)/shard_map/ppermute | solution.py:100
  115.9 3.2 %collective-permute-start.12 = (bf16[1184,128]{1,0:T(8,128)(2,1)S(1)}, bf16[1184,128]{1,0:T(8,128)(2,1)S(1)}, u32[]{:S(2)}, u32[]{:S(2)}) collective-permute-start(bf16[1184,128]{1,0:T(8,128)(2,1)S(1)} %collective-permute-done.11), channel_id=1, source_target_pairs={{0,1},{1,0},{2,3},{3,2},{4,5},{5,4},{6,7},{7,6},{8,9},{9,8},{10,11... | collective-permute-start | bytes 909320 | tf_op jit(solution)/shard_map/ppermute | solution.py:100
  119.2 0.9 constant_dynamic-update-slice_fusion.4
  120.0 0.9 constant_dynamic-update-slice_fusion.3
  120.9 0.9 constant_dynamic-update-slice_fusion.2
  121.8 0.7 constant_dynamic-update-slice_fusion.1
  122.5 0.7 constant_dynamic-update-slice_fusion
  123.2 0.7 constant_dynamic-update-slice_fusion.9
  124.0 0.7 constant_dynamic-update-slice_fusion.8
  (38 shorter events, 0.4 us)
Async XLA Ops:
  53.6 15.5 %all-to-all-start.3 = ((f32[4,592,128]{2,1,0:T(8,128)}), f32[4,592,128]{2,1,0:T(8,128)S(1)}, u32[]{:S(2)}, u32[]{:S(2)}) async-start(f32[4,592,128]{2,1,0:T(8,128)} %broadcast_in_dim.44), calls=%async_computation.3 | async-start | bytes 2424832 | tf_op jit(solution)/shard_map/all_to_all | solution.py:62
  69.0 1.3 %copy-start.5 = (f32[2368,128]{1,0:T(8,128)S(1)}, f32[2368,128]{1,0:T(8,128)}, u32[]{:S(2)}) copy-start(f32[2368,128]{1,0:T(8,128)} %param.7) | copy-start | bytes 3637252
  69.0 1.6 %copy-start.6 = (f32[2368,128]{1,0:T(8,128)S(1)}, f32[2368,128]{1,0:T(8,128)}, u32[]{:S(2)}) copy-start(f32[2368,128]{1,0:T(8,128)} %param.6) | copy-start | bytes 3637252
  70.7 1.5 %copy-start.2 = (f32[2368,128]{1,0:T(8,128)S(1)}, f32[2368,128]{1,0:T(8,128)}, u32[]{:S(2)}) copy-start(f32[2368,128]{1,0:T(8,128)} %param.5) | copy-start | bytes 3637252
  70.9 3.2 %copy-start = (f32[2368,128]{1,0:T(8,128)}, f32[2368,128]{1,0:T(8,128)S(1)}, u32[]{:S(2)}) copy-start(f32[2368,128]{1,0:T(8,128)S(1)} %get-tuple-element.17) | copy-start | bytes 3637252
  70.9 3.2 %copy-start.1 = (f32[2368,128]{1,0:T(8,128)}, f32[2368,128]{1,0:T(8,128)S(1)}, u32[]{:S(2)}) copy-start(f32[2368,128]{1,0:T(8,128)S(1)} %get-tuple-element.18) | copy-start | bytes 3637252
  74.6 6.7 %collective-permute-start = (f32[8]{0:T(128)S(1)}, f32[8]{0:T(128)S(1)}, u32[]{:S(2)}, u32[]{:S(2)}) collective-permute-start(f32[8]{0:T(128)S(1)} %pad_maximum_fusion), channel_id=1, source_target_pairs={{0,1},{1,0},{2,3},{3,2},{4,5},{5,4},{6,7},{7,6},{8,9},{9,8},{10,11... | collective-permute-start | bytes 104 | tf_op jit(solution)/shard_map/ppermute | solution.py:68
  81.4 3.8 %collective-permute-start.1 = (f32[8]{0:T(128)S(1)}, f32[8]{0:T(128)S(1)}, u32[]{:S(2)}, u32[]{:S(2)}) collective-permute-start(f32[8]{0:T(128)S(1)} %fusion.10), channel_id=1, source_target_pairs={{0,6},{2,0},{4,2},{6,4},{1,7},{3,1},{5,3},{7,5},{8,14},{10,8},{12,... | collective-permute-start | bytes 104 | tf_op jit(solution)/shard_map/ppermute | solution.py:75
  84.1 3.9 %collective-permute-start.2 = (f32[8]{0:T(128)S(1)}, f32[8]{0:T(128)S(1)}, u32[]{:S(2)}, u32[]{:S(2)}) collective-permute-start(f32[8]{0:T(128)S(1)} %fusion.10), channel_id=1, source_target_pairs={{0,4},{2,6},{4,0},{6,2},{1,5},{3,7},{5,1},{7,3},{8,12},{10,14},{12... | collective-permute-start | bytes 104 | tf_op jit(solution)/shard_map/ppermute | solution.py:75
  84.5 3.6 %collective-permute-start.3 = (f32[8]{0:T(128)S(1)}, f32[8]{0:T(128)S(1)}, u32[]{:S(2)}, u32[]{:S(2)}) collective-permute-start(f32[8]{0:T(128)S(1)} %fusion.10), channel_id=1, source_target_pairs={{0,2},{2,4},{4,6},{6,0},{1,3},{3,5},{5,7},{7,1},{8,10},{10,12},{12... | collective-permute-start | bytes 104 | tf_op jit(solution)/shard_map/ppermute | solution.py:75
  88.4 2.9 %copy-start.3 = (f32[2368,128]{1,0:T(8,128)S(1)}, f32[2368,128]{1,0:T(8,128)}, u32[]{:S(2)}) copy-start(f32[2368,128]{1,0:T(8,128)} %param.5) | copy-start | bytes 3637252
  88.5 2.9 %copy-start.4 = (f32[2368,128]{1,0:T(8,128)S(1)}, f32[2368,128]{1,0:T(8,128)}, u32[]{:S(2)}) copy-start(f32[2368,128]{1,0:T(8,128)} %get-tuple-element.9) | copy-start | bytes 3637252
  92.9 13.2 %collective-permute-start.5 = (bf16[2368,128]{1,0:T(8,128)(2,1)S(1)}, bf16[2368,128]{1,0:T(8,128)(2,1)S(1)}, u32[]{:S(2)}, u32[]{:S(2)}) collective-permute-start(bf16[2368,128]{1,0:T(8,128)(2,1)S(1)} %get-tuple-element.6), channel_id=1, source_target_pairs={{0,6},{2,0},{4,2},{6,4},{1,7},{3,1},{5,3},{7,5},{8,14},{10,8},{12,... | collective-permute-start | bytes 1818632 | tf_op jit(solution)/shard_map/ppermute | solution.py:90
  93.4 14.8 %collective-permute-start.7 = (bf16[2368,128]{1,0:T(8,128)(2,1)S(1)}, bf16[2368,128]{1,0:T(8,128)(2,1)S(1)}, u32[]{:S(2)}, u32[]{:S(2)}) collective-permute-start(bf16[2368,128]{1,0:T(8,128)(2,1)S(1)} %get-tuple-element.6), channel_id=1, source_target_pairs={{0,2},{2,4},{4,6},{6,0},{1,3},{3,5},{5,7},{7,1},{8,10},{10,12},{12... | collective-permute-start | bytes 1818632 | tf_op jit(solution)/shard_map/ppermute | solution.py:90
  94.4 17.0 %collective-permute-start.4 = (bf16[2368,128]{1,0:T(8,128)(2,1)S(1)}, bf16[2368,128]{1,0:T(8,128)(2,1)S(1)}, u32[]{:S(2)}, u32[]{:S(2)}) collective-permute-start(bf16[2368,128]{1,0:T(8,128)(2,1)S(1)} %get-tuple-element.6), channel_id=1, source_target_pairs={{0,1},{1,0},{2,3},{3,2},{4,5},{5,4},{6,7},{7,6},{8,9},{9,8},{10,11... | collective-permute-start | bytes 1818632 | tf_op jit(solution)/shard_map/ppermute | solution.py:100
  106.1 7.0 %collective-permute-start.9 = (bf16[1184,128]{1,0:T(8,128)(2,1)S(1)}, bf16[1184,128]{1,0:T(8,128)(2,1)S(1)}, u32[]{:S(2)}, u32[]{:S(2)}) collective-permute-start(bf16[1184,128]{1,0:T(8,128)(2,1)S(1)} %slice.49), channel_id=1, source_target_pairs={{0,6},{2,0},{4,2},{6,4},{1,7},{3,1},{5,3},{7,5},{8,14},{10,8},{12,... | collective-permute-start | bytes 909320 | tf_op jit(solution)/shard_map/ppermute | solution.py:90
  108.2 7.8 %collective-permute-start.11 = (bf16[1184,128]{1,0:T(8,128)(2,1)S(1)}, bf16[1184,128]{1,0:T(8,128)(2,1)S(1)}, u32[]{:S(2)}, u32[]{:S(2)}) collective-permute-start(bf16[1184,128]{1,0:T(8,128)(2,1)S(1)} %slice.50), channel_id=1, source_target_pairs={{0,2},{2,4},{4,6},{6,0},{1,3},{3,5},{5,7},{7,1},{8,10},{10,12},{12... | collective-permute-start | bytes 909320 | tf_op jit(solution)/shard_map/ppermute | solution.py:90
  108.3 10.9 %collective-permute-start.6 = (bf16[2368,128]{1,0:T(8,128)(2,1)S(1)}, bf16[2368,128]{1,0:T(8,128)(2,1)S(1)}, u32[]{:S(2)}, u32[]{:S(2)}) collective-permute-start(bf16[2368,128]{1,0:T(8,128)(2,1)S(1)} %collective-permute-done.5), channel_id=1, source_target_pairs={{0,1},{1,0},{2,3},{3,2},{4,5},{5,4},{6,7},{7,6},{8,9},{9,8},{10,11... | collective-permute-start | bytes 1818632 | tf_op jit(solution)/shard_map/ppermute | solution.py:100
  111.3 9.6 %collective-permute-start.8 = (bf16[2368,128]{1,0:T(8,128)(2,1)S(1)}, bf16[2368,128]{1,0:T(8,128)(2,1)S(1)}, u32[]{:S(2)}, u32[]{:S(2)}) collective-permute-start(bf16[2368,128]{1,0:T(8,128)(2,1)S(1)} %collective-permute-done.7), channel_id=1, source_target_pairs={{0,1},{1,0},{2,3},{3,2},{4,5},{5,4},{6,7},{7,6},{8,9},{9,8},{10,11... | collective-permute-start | bytes 1818632 | tf_op jit(solution)/shard_map/ppermute | solution.py:100
  113.1 9.4 %collective-permute-start.10 = (bf16[1184,128]{1,0:T(8,128)(2,1)S(1)}, bf16[1184,128]{1,0:T(8,128)(2,1)S(1)}, u32[]{:S(2)}, u32[]{:S(2)}) collective-permute-start(bf16[1184,128]{1,0:T(8,128)(2,1)S(1)} %collective-permute-done.9), channel_id=1, source_target_pairs={{0,1},{1,0},{2,3},{3,2},{4,5},{5,4},{6,7},{7,6},{8,9},{9,8},{10,11... | collective-permute-start | bytes 909320 | tf_op jit(solution)/shard_map/ppermute | solution.py:100
  115.9 8.0 %collective-permute-start.12 = (bf16[1184,128]{1,0:T(8,128)(2,1)S(1)}, bf16[1184,128]{1,0:T(8,128)(2,1)S(1)}, u32[]{:S(2)}, u32[]{:S(2)}) collective-permute-start(bf16[1184,128]{1,0:T(8,128)(2,1)S(1)} %collective-permute-done.11), channel_id=1, source_target_pairs={{0,1},{1,0},{2,3},{3,2},{4,5},{5,4},{6,7},{7,6},{8,9},{9,8},{10,11... | collective-permute-start | bytes 909320 | tf_op jit(solution)/shard_map/ppermute | solution.py:100

commit v6 on v5

--- a/solution.py
+++ b/solution.py
@@ -95,13 +95,24 @@
         pieces = [(b, 0, 0), (plus, 1, 0), (minus, 3, 0), (shift(plus[:half], 1), 2, 0), (shift(minus[half:], -1), 2, half)]
     else:
         pieces = [(b, 0, 0)] + [(shift(b, s), s, 0) for s in range(1, ny)]
-    out = jnp.zeros((rows, 2 * ny * width), b.dtype)
-    for mine, s, row in pieces:
-        other = lax.ppermute(mine, "core", swap)
-        chip = (y + s) % ny
-        out = lax.dynamic_update_slice(out, mine, (row, (2 * chip + core) * width))
-        out = lax.dynamic_update_slice(out, other, (row, (2 * chip + 1 - core) * width))
-    return out
+    mines = [m for m, _, _ in pieces]
+    others = [lax.ppermute(m, "core", swap) for m in mines]
+
+    def layout(k, c):
+        def build(mines, others):
+            blocks = []
+            for chip in range(ny):
+                s = (chip - k) % ny
+                parts = [i for i, (_, si, _) in enumerate(pieces) if si == s]
+                mine = jnp.concatenate([mines[i] for i in parts], 0)
+                other = jnp.concatenate([others[i] for i in parts], 0)
+                blocks += [mine, other] if c == 0 else [other, mine]
+            return jnp.concatenate(blocks, 1)
+
+        return build
+
+    branches = [layout(k, c) for k in range(ny) for c in range(2)]
+    return lax.switch(y * 2 + core, branches, mines, others)
 
 
 def make_shards(nz, nx, ny, ncore):

time: 125 us -> 129 us (1.032)
  other arithmetic: 5.06 us -> 11.7 us
  local copies, waits for them, and re-layouts: 14.1 us -> 8.61 us
  starting transfers between devices: 28.6 us -> 30.1 us
    dynamic_update_slice x9 -> x0, local copies, waits for them, and re-layouts: 7.24 us -> none  [the longest x5 4.05 us: tensor_gather(): lax.dynamic_update_slice(out, other, (row, (2 * chip + 1 - core) * width))]
    cond x0 -> x5, local copies, waits for them, and re-layouts: none -> 5.37 us
    cond x0 -> x2, other arithmetic: none -> 3.74 us
    broadcast_in_dim x1 -> x0, local copies, waits for them, and re-layouts: 2.85 us -> none  [tensor_gather(): out = jnp.zeros((rows, 2 * ny * width), b.dtype)]
    convert_element_type x0 -> x1, other arithmetic: none -> 2.69 us  [shards(): copies = tensor_gather(weights_new.astype(jnp.bfloat16), ny)]
    ppermute x4, starting transfers between devices: 3.56 us -> 5.49 us  [shift(): return lax.ppermute(v, 'y', [(i, (i - s) % ny) for i in range(ny)])]
    add x1, other arithmetic: 0.26 us -> 2.05 us  [adam_part(): second_new = beta_two * second_moment + (1.0 - beta_two) * grad * grad]
    ppermute x5, starting transfers between devices: 11.8 us -> 10.2 us  [tensor_gather(): others = [lax.ppermute(m, 'core', swap) for m in mines]]
  transfers between devices with their start and end apart: 14 -> 14, of which waited for: 4 -> 7; matrix products, arithmetic and copies ran while one was open for 6% -> 1% of each run, Pallas kernels for 0% -> 0%
where the time goes in v6:
time: 129 us; the launch traced here: 128 us
  blocking collectives  51.6 us (40%)
  starting transfers between devices  30.1 us (23%)
  waiting for transfers between devices  24.9 us (19%)
  other arithmetic  11.7 us (9%)
  local copies, waits for them, and re-layouts  8.61 us (7%)
    all_to_all x1, blocking collectives, dp_sum(): y = lax.all_to_all(x.reshape(nx, part, cols), 'x', 0, 0, tiled=False).sum(0)  19.9 us
    all_to_all x1, blocking collectives, dp_sum(): lax.all_to_all(y.reshape(nz, padded // nz, cols), 'z', 0, 0, tiled=False)  19.2 us
    all_to_all x1, blocking collectives, dp_sum(): lax.all_to_all(jnp.broadcast_to(y[None], (nz,) + y.shape), 'z', 0, 0, til...  12.5 us
    all_to_all x1, waiting for transfers between devices, dp_sum(): lax.all_to_all(jnp.broadcast_to(y[None], (nx,) + y.shape), 'x', 0, 0, til...  11.7 us
    ppermute x5, starting transfers between devices, tensor_gather(): others = [lax.ppermute(m, 'core', swap) for m in mines]  10.2 us
    ppermute x4, waiting for transfers between devices, shift(): return lax.ppermute(v, 'y', [(i, (i - s) % ny) for i in range(ny)])  9.7 us
    ppermute x1, starting transfers between devices, tensor_sum(): v = v + lax.ppermute(v, 'core', [(0, 1), (1, 0)])  5.88 us
    ppermute x4, starting transfers between devices, shift(): return lax.ppermute(v, 'y', [(i, (i - s) % ny) for i in range(ny)])  5.49 us
  transfers between devices with their start and end apart: 14, of which 7 were waited for; matrix products, arithmetic and copies ran while one was open for 1% of the time, Pallas kernels for 0%

profile of v6, /device:TPU:1, one launch (start us, length us, event | category | flops | bytes accessed | tf_op | source)
XLA Modules:
  0.0 128.3 jit_solution(12190938019701256624)
XLA Ops:
  0.6 19.9 %all_to_all.20 = f32[4,592,128]{2,1,0:T(8,128)S(1)} all-to-all(f32[4,592,128]{2,1,0:T(8,128)} %bitcast.27), channel_id=1, replica_groups=mesh['z'=8,'x'=4,'y'=4,'core'=2] {'x'}, dimensions={0} | all-to-all | bytes 2424832 | tf_op jit(solution)/shard_map/all_to_all | solution.py:57
  20.6 0.1 reduce_sum.37
  20.7 19.2 %all_to_all.21 = f32[8,80,128]{2,1,0:T(8,128)S(1)} all-to-all(f32[8,80,128]{2,1,0:T(8,128)S(1)} %bitcast.25), channel_id=1, replica_groups=mesh['z'=8,'x'=4,'y'=4,'core'=2] {'z'}, dimensions={0} | all-to-all | bytes 655360 | tf_op jit(solution)/shard_map/all_to_all | solution.py:59
  39.9 12.5 %all_to_all.22 = f32[8,80,128]{2,1,0:T(8,128)S(1)} all-to-all(f32[8,80,128]{2,1,0:T(8,128)S(1)} %broadcast_in_dim.40), channel_id=1, replica_groups=mesh['z'=8,'x'=4,'y'=4,'core'=2] {'z'}, dimensions={0} | all-to-all | bytes 655360 | tf_op jit(solution)/shard_map/all_to_all | solution.py:60
  52.5 1.1 broadcast_in_dim.41
  53.6 3.5 %all-to-all-start.3 = ((f32[4,592,128]{2,1,0:T(8,128)}), f32[4,592,128]{2,1,0:T(8,128)S(1)}, u32[]{:S(2)}, u32[]{:S(2)}) async-start(f32[4,592,128]{2,1,0:T(8,128)} %broadcast_in_dim.41), calls=%async_computation.3 | async-start | bytes 2424832 | tf_op jit(solution)/shard_map/all_to_all | solution.py:62
  57.3 0.0 copy-start.2
  57.3 11.7 %all-to-all-done.3 = f32[4,592,128]{2,1,0:T(8,128)S(1)} async-done(((f32[4,592,128]{2,1,0:T(8,128)}), f32[4,592,128]{2,1,0:T(8,128)S(1)}, u32[]{:S(2)}, u32[]{:S(2)}) %all-to-all-start.3) | async-done | bytes 1212448 | tf_op jit(solution)/shard_map/all_to_all | solution.py:62
  69.0 0.2 broadcast_multiply_fusion
  69.2 2.1 %bitcast_add_fusion = (f32[2368,128]{1,0:T(8,128)S(1)}, f32[2368,128]{1,0:T(8,128)S(1)}) fusion(f32[4,592,128]{2,1,0:T(8,128)S(1)} %get-tuple-element.262, f32[2368,128]{1,0:T(8,128)} %param.15, f32[4,592,128]{2,1,0:T(8,128)S(1)} %get-tuple-element.261, f32[2368,128]{1,0:T(8,128)} %param.14), kind=kLoop, calls=%fused_computation.64 | loop fusion | flops 1212416 | bytes 7274496 | tf_op jit(solution)/shard_map/add | solution.py:38
  71.3 0.0 copy-start
  71.3 0.0 copy-start.1
  71.3 1.0 copy-done
  72.3 2.0 %multiply_reduce_fusion = (f32[2368]{0:T(1024)S(1)}, f32[2368,128]{1,0:T(8,128)}, f32[2368]{0:T(1024)S(1)}) fusion(f32[2368,128]{1,0:T(8,128)S(1)} %copy-done.2, f32[2368]{0:T(1024)S(1)} %fusion.1, f32[2368,128]{1,0:T(8,128)S(1)} %get-tuple-element.265, f32[2368,128]{1,0:T(8,128)S(1)} %get-tuple-element.266), kind=kLoop, calls=%fused_computation.67 | loop fusion | flops 3026304 | bytes 4878080 | tf_op jit(solution)/shard_map/reduce_sum | solution.py:32
  74.3 0.1 convolution_bitcast_fusion
  74.5 0.2 convolution_bitcast_fusion.1
  74.7 0.1 pad_maximum_fusion
  74.8 5.9 %collective-permute-start = (f32[8]{0:T(128)S(1)}, f32[8]{0:T(128)S(1)}, u32[]{:S(2)}, u32[]{:S(2)}) collective-permute-start(f32[8]{0:T(128)S(1)} %pad_maximum_fusion), channel_id=1, source_target_pairs={{0,1},{1,0},{2,3},{3,2},{4,5},{5,4},{6,7},{7,6},{8,9},{9,8},{10,11... | collective-permute-start | bytes 104 | tf_op jit(solution)/shard_map/ppermute | solution.py:68
  80.7 0.8 collective-permute-done
  81.5 0.1 fusion.11
  81.6 1.3 %collective-permute-start.3 = (f32[8]{0:T(128)S(1)}, f32[8]{0:T(128)S(1)}, u32[]{:S(2)}, u32[]{:S(2)}) collective-permute-start(f32[8]{0:T(128)S(1)} %fusion.11), channel_id=1, source_target_pairs={{0,2},{2,4},{4,6},{6,0},{1,3},{3,5},{5,7},{7,1},{8,10},{10,12},{12... | collective-permute-start | bytes 104 | tf_op jit(solution)/shard_map/ppermute | solution.py:75
  82.9 2.6 %collective-permute-start.2 = (f32[8]{0:T(128)S(1)}, f32[8]{0:T(128)S(1)}, u32[]{:S(2)}, u32[]{:S(2)}) collective-permute-start(f32[8]{0:T(128)S(1)} %fusion.11), channel_id=1, source_target_pairs={{0,4},{2,6},{4,0},{6,2},{1,5},{3,7},{5,1},{7,3},{8,12},{10,14},{12... | collective-permute-start | bytes 104 | tf_op jit(solution)/shard_map/ppermute | solution.py:75
  85.5 1.1 collective-permute-start.1
  86.6 1.3 %collective-permute-done.1 = f32[8]{0:T(128)S(1)} collective-permute-done((f32[8]{0:T(128)S(1)}, f32[8]{0:T(128)S(1)}, u32[]{:S(2)}, u32[]{:S(2)}) %collective-permute-start.1) | collective-permute-done | bytes 64 | tf_op jit(solution)/shard_map/ppermute | solution.py:75
  88.0 0.3 convolution_reduce_fusion
  88.3 2.7 %fusion.3 = (bf16[2368,128]{1,0:T(8,128)(2,1)S(1)}, f32[2368,128]{1,0:T(8,128)}) fusion(f32[2368,128]{1,0:T(8,128)S(1)} %copy-done.2, f32[2368,128]{1,0:T(8,128)} %get-tuple-element.257, f32[2368]{0:T(1024)S(1)} %broadcast_multiply_fusion.1), kind=kLoop, calls=%fused_computation.87 | loop fusion | flops 909312 | bytes 4252928 | tf_op jit(solution)/shard_map/convert_element_type | solution.py:130
  91.0 0.1 collective-permute-start.6
  91.1 2.5 %collective-permute-start.4 = (bf16[2368,128]{1,0:T(8,128)(2,1)S(1)}, bf16[2368,128]{1,0:T(8,128)(2,1)S(1)}, u32[]{:S(2)}, u32[]{:S(2)}) collective-permute-start(bf16[2368,128]{1,0:T(8,128)(2,1)S(1)} %get-tuple-element.254), channel_id=1, source_target_pairs={{0,6},{2,0},{4,2},{6,4},{1,7},{3,1},{5,3},{7,5},{8,14},{10,8},{12,... | collective-permute-start | bytes 1818632 | tf_op jit(solution)/shard_map/ppermute | solution.py:90
  93.7 2.6 %collective-permute-start.10 = (bf16[2368,128]{1,0:T(8,128)(2,1)S(1)}, bf16[2368,128]{1,0:T(8,128)(2,1)S(1)}, u32[]{:S(2)}, u32[]{:S(2)}) collective-permute-start(bf16[2368,128]{1,0:T(8,128)(2,1)S(1)} %get-tuple-element.254), channel_id=1, source_target_pairs={{0,1},{1,0},{2,3},{3,2},{4,5},{5,4},{6,7},{7,6},{8,9},{9,8},{10,11... | collective-permute-start | bytes 1818632 | tf_op jit(solution)/shard_map/ppermute | solution.py:99
  96.3 9.1 %collective-permute-done.6 = bf16[2368,128]{1,0:T(8,128)(2,1)S(1)} collective-permute-done((bf16[2368,128]{1,0:T(8,128)(2,1)S(1)}, bf16[2368,128]{1,0:T(8,128)(2,1)S(1)}, u32[]{:S(2)}, u32[]{:S(2)}) %collective-permute-start.6) | collective-permute-done | bytes 606240 | tf_op jit(solution)/shard_map/ppermute | solution.py:90
  105.4 0.1 collective-permute-start.7
  105.5 2.7 %collective-permute-start.5 = (bf16[1184,128]{1,0:T(8,128)(2,1)S(1)}, bf16[1184,128]{1,0:T(8,128)(2,1)}, u32[]{:S(2)}, u32[]{:S(2)}) collective-permute-start(bf16[1184,128]{1,0:T(8,128)(2,1)S(1)} %slice.49), channel_id=1, source_target_pairs={{0,6},{2,0},{4,2},{6,4},{1,7},{3,1},{5,3},{7,5},{8,14},{10,8},{12,... | collective-permute-start | bytes 909320 | tf_op jit(solution)/shard_map/ppermute | solution.py:90
  108.3 3.5 %collective-permute-start.12 = (bf16[2368,128]{1,0:T(8,128)(2,1)S(1)}, bf16[2368,128]{1,0:T(8,128)(2,1)S(1)}, u32[]{:S(2)}, u32[]{:S(2)}) collective-permute-start(bf16[2368,128]{1,0:T(8,128)(2,1)S(1)} %collective-permute-done.6), channel_id=1, source_target_pairs={{0,1},{1,0},{2,3},{3,2},{4,5},{5,4},{6,7},{7,6},{8,9},{9,8},{10,11... | collective-permute-start | bytes 1818632 | tf_op jit(solution)/shard_map/ppermute | solution.py:99
  111.8 0.6 collective-permute-done.7
  112.4 4.1 %collective-permute-start.9 = (bf16[1184,128]{1,0:T(8,128)(2,1)S(1)}, bf16[1184,128]{1,0:T(8,128)(2,1)}, u32[]{:S(2)}, u32[]{:S(2)}) collective-permute-start(bf16[1184,128]{1,0:T(8,128)(2,1)S(1)} %collective-permute-done.7), channel_id=1, source_target_pairs={{0,1},{1,0},{2,3},{3,2},{4,5},{5,4},{6,7},{7,6},{8,9},{9,8},{10,11... | collective-permute-start | bytes 909320 | tf_op jit(solution)/shard_map/ppermute | solution.py:99
  116.4 0.0 collective-permute-start.8
  116.4 0.6 fusion.10
  117.0 0.8 collective-permute-done.9
  117.8 0.6 collective-permute-done.8
  118.4 10.0 %conditional.1 = (bf16[2368,1024]{1,0:T(8,128)(2,1)}) conditional(s32[]{:T(128)} %clamp.3, (bf16[1184,128]{1,0:T(8,128)(2,1)}, bf16[1184,128]{1,0:T(8,128)(2,1)S(1)}, bf16[1184,128]{1,0:T(8,128)(2,1)}, bf16[1184,128]{1,0:T(8,128)(2,1)}, bf16[2368,128]{1,0:T(8,128)(2,1)S(1)}, ...), branch_computations={%region_4.5_spmd, %region_5.6_spmd, %region_6.7_spmd, %region_7.8_... | conditional | flops 2424832 | bytes 9699336 | solution.py:115
  118.4 0.9 constant_dynamic-update-slice_fusion.11
  119.2 0.9 constant_dynamic-update-slice_fusion.10
  120.1 1.9 %constant_dynamic-update-slice_fusion.9 = bf16[2368,1024]{1,0:T(8,128)(2,1)} fusion(bf16[2368,1024]{1,0:T(8,128)(2,1)} %constant_dynamic-update-slice_fusion.10, bf16[2368,128]{1,0:T(8,128)(2,1)} %get-tuple-element.181), kind=kLoop, calls=%fused_computation.13 | loop fusion | bytes 1212416 | tf_op jit(solution)/shard_map/cond
  122.0 0.9 constant_dynamic-update-slice_fusion.8
  122.9 1.9 %maximum_dynamic-update-slice_fusion.3 = bf16[2368,1024]{1,0:T(8,128)(2,1)} fusion(bf16[2368,1024]{1,0:T(8,128)(2,1)} %constant_dynamic-update-slice_fusion.8, bf16[1184,128]{1,0:T(8,128)(2,1)} %get-tuple-element.184, bf16[1184,128]{1,0:T(8,128)(2,1)} %get-tuple-element.183), kind=kLoop, calls=%fused_computation.9 | loop fusion | flops 1212416 | bytes 1212416 | tf_op jit(solution)/shard_map/cond
  124.8 1.8 %maximum_dynamic-update-slice_fusion.2 = bf16[2368,1024]{1,0:T(8,128)(2,1)} fusion(bf16[2368,1024]{1,0:T(8,128)(2,1)} %maximum_dynamic-update-slice_fusion.3, bf16[1184,128]{1,0:T(8,128)(2,1)S(1)} %get-tuple-element.186, bf16[1184,128]{1,0:T(8,128)(2,1)} %get-tuple-element.185), kind=kLoop, calls=%fused_computation.8 | loop fusion | flops 1212416 | bytes 1212416 | tf_op jit(solution)/shard_map/cond
  126.6 0.9 constant_dynamic-update-slice_fusion.7
  127.5 0.9 constant_dynamic-update-slice_fusion.6
  (29 shorter events, 0.4 us)
Async XLA Ops:
  53.6 15.5 %all-to-all-start.3 = ((f32[4,592,128]{2,1,0:T(8,128)}), f32[4,592,128]{2,1,0:T(8,128)S(1)}, u32[]{:S(2)}, u32[]{:S(2)}) async-start(f32[4,592,128]{2,1,0:T(8,128)} %broadcast_in_dim.41), calls=%async_computation.3 | async-start | bytes 2424832 | tf_op jit(solution)/shard_map/all_to_all | solution.py:62
  57.3 15.1 %copy-start.2 = (f32[2368,128]{1,0:T(8,128)S(1)}, f32[2368,128]{1,0:T(8,128)}, u32[]{:S(2)}) copy-start(f32[2368,128]{1,0:T(8,128)} %param.13) | copy-start | bytes 3637252
  71.3 1.0 copy-start
  71.3 3.0 %copy-start.1 = (f32[2368,128]{1,0:T(8,128)}, f32[2368,128]{1,0:T(8,128)S(1)}, u32[]{:S(2)}) copy-start(f32[2368,128]{1,0:T(8,128)S(1)} %get-tuple-element.266) | copy-start | bytes 3637252
  74.8 6.7 %collective-permute-start = (f32[8]{0:T(128)S(1)}, f32[8]{0:T(128)S(1)}, u32[]{:S(2)}, u32[]{:S(2)}) collective-permute-start(f32[8]{0:T(128)S(1)} %pad_maximum_fusion), channel_id=1, source_target_pairs={{0,1},{1,0},{2,3},{3,2},{4,5},{5,4},{6,7},{7,6},{8,9},{9,8},{10,11... | collective-permute-start | bytes 104 | tf_op jit(solution)/shard_map/ppermute | solution.py:68
  81.6 6.4 %collective-permute-start.3 = (f32[8]{0:T(128)S(1)}, f32[8]{0:T(128)S(1)}, u32[]{:S(2)}, u32[]{:S(2)}) collective-permute-start(f32[8]{0:T(128)S(1)} %fusion.11), channel_id=1, source_target_pairs={{0,2},{2,4},{4,6},{6,0},{1,3},{3,5},{5,7},{7,1},{8,10},{10,12},{12... | collective-permute-start | bytes 104 | tf_op jit(solution)/shard_map/ppermute | solution.py:75
  82.9 5.1 %collective-permute-start.2 = (f32[8]{0:T(128)S(1)}, f32[8]{0:T(128)S(1)}, u32[]{:S(2)}, u32[]{:S(2)}) collective-permute-start(f32[8]{0:T(128)S(1)} %fusion.11), channel_id=1, source_target_pairs={{0,4},{2,6},{4,0},{6,2},{1,5},{3,7},{5,1},{7,3},{8,12},{10,14},{12... | collective-permute-start | bytes 104 | tf_op jit(solution)/shard_map/ppermute | solution.py:75
  85.5 2.4 %collective-permute-start.1 = (f32[8]{0:T(128)S(1)}, f32[8]{0:T(128)S(1)}, u32[]{:S(2)}, u32[]{:S(2)}) collective-permute-start(f32[8]{0:T(128)S(1)} %fusion.11), channel_id=1, source_target_pairs={{0,6},{2,0},{4,2},{6,4},{1,7},{3,1},{5,3},{7,5},{8,14},{10,8},{12,... | collective-permute-start | bytes 104 | tf_op jit(solution)/shard_map/ppermute | solution.py:75
  91.0 14.4 %collective-permute-start.6 = (bf16[2368,128]{1,0:T(8,128)(2,1)S(1)}, bf16[2368,128]{1,0:T(8,128)(2,1)S(1)}, u32[]{:S(2)}, u32[]{:S(2)}) collective-permute-start(bf16[2368,128]{1,0:T(8,128)(2,1)S(1)} %get-tuple-element.254), channel_id=1, source_target_pairs={{0,2},{2,4},{4,6},{6,0},{1,3},{3,5},{5,7},{7,1},{8,10},{10,12},{12... | collective-permute-start | bytes 1818632 | tf_op jit(solution)/shard_map/ppermute | solution.py:90
  91.1 14.4 %collective-permute-start.4 = (bf16[2368,128]{1,0:T(8,128)(2,1)S(1)}, bf16[2368,128]{1,0:T(8,128)(2,1)S(1)}, u32[]{:S(2)}, u32[]{:S(2)}) collective-permute-start(bf16[2368,128]{1,0:T(8,128)(2,1)S(1)} %get-tuple-element.254), channel_id=1, source_target_pairs={{0,6},{2,0},{4,2},{6,4},{1,7},{3,1},{5,3},{7,5},{8,14},{10,8},{12,... | collective-permute-start | bytes 1818632 | tf_op jit(solution)/shard_map/ppermute | solution.py:90
  93.7 23.4 %collective-permute-start.10 = (bf16[2368,128]{1,0:T(8,128)(2,1)S(1)}, bf16[2368,128]{1,0:T(8,128)(2,1)S(1)}, u32[]{:S(2)}, u32[]{:S(2)}) collective-permute-start(bf16[2368,128]{1,0:T(8,128)(2,1)S(1)} %get-tuple-element.254), channel_id=1, source_target_pairs={{0,1},{1,0},{2,3},{3,2},{4,5},{5,4},{6,7},{7,6},{8,9},{9,8},{10,11... | collective-permute-start | bytes 1818632 | tf_op jit(solution)/shard_map/ppermute | solution.py:99
  105.4 6.9 %collective-permute-start.7 = (bf16[1184,128]{1,0:T(8,128)(2,1)S(1)}, bf16[1184,128]{1,0:T(8,128)(2,1)S(1)}, u32[]{:S(2)}, u32[]{:S(2)}) collective-permute-start(bf16[1184,128]{1,0:T(8,128)(2,1)S(1)} %slice.50), channel_id=1, source_target_pairs={{0,2},{2,4},{4,6},{6,0},{1,3},{3,5},{5,7},{7,1},{8,10},{10,12},{12... | collective-permute-start | bytes 909320 | tf_op jit(solution)/shard_map/ppermute | solution.py:90
  105.5 10.9 %collective-permute-start.5 = (bf16[1184,128]{1,0:T(8,128)(2,1)S(1)}, bf16[1184,128]{1,0:T(8,128)(2,1)}, u32[]{:S(2)}, u32[]{:S(2)}) collective-permute-start(bf16[1184,128]{1,0:T(8,128)(2,1)S(1)} %slice.49), channel_id=1, source_target_pairs={{0,6},{2,0},{4,2},{6,4},{1,7},{3,1},{5,3},{7,5},{8,14},{10,8},{12,... | collective-permute-start | bytes 909320 | tf_op jit(solution)/shard_map/ppermute | solution.py:90
  108.3 9.5 %collective-permute-start.12 = (bf16[2368,128]{1,0:T(8,128)(2,1)S(1)}, bf16[2368,128]{1,0:T(8,128)(2,1)S(1)}, u32[]{:S(2)}, u32[]{:S(2)}) collective-permute-start(bf16[2368,128]{1,0:T(8,128)(2,1)S(1)} %collective-permute-done.6), channel_id=1, source_target_pairs={{0,1},{1,0},{2,3},{3,2},{4,5},{5,4},{6,7},{7,6},{8,9},{9,8},{10,11... | collective-permute-start | bytes 1818632 | tf_op jit(solution)/shard_map/ppermute | solution.py:99
  111.8 6.6 %collective-permute-start.11 = (bf16[2368,128]{1,0:T(8,128)(2,1)S(1)}, bf16[2368,128]{1,0:T(8,128)(2,1)}, u32[]{:S(2)}, u32[]{:S(2)}) collective-permute-start(bf16[2368,128]{1,0:T(8,128)(2,1)S(1)} %collective-permute-done.4), channel_id=1, source_target_pairs={{0,1},{1,0},{2,3},{3,2},{4,5},{5,4},{6,7},{7,6},{8,9},{9,8},{10,11... | collective-permute-start | bytes 1818632 | tf_op jit(solution)/shard_map/ppermute | solution.py:99
  112.4 5.4 %collective-permute-start.9 = (bf16[1184,128]{1,0:T(8,128)(2,1)S(1)}, bf16[1184,128]{1,0:T(8,128)(2,1)}, u32[]{:S(2)}, u32[]{:S(2)}) collective-permute-start(bf16[1184,128]{1,0:T(8,128)(2,1)S(1)} %collective-permute-done.7), channel_id=1, source_target_pairs={{0,1},{1,0},{2,3},{3,2},{4,5},{5,4},{6,7},{7,6},{8,9},{9,8},{10,11... | collective-permute-start | bytes 909320 | tf_op jit(solution)/shard_map/ppermute | solution.py:99
  116.4 1.9 %collective-permute-start.8 = (bf16[1184,128]{1,0:T(8,128)(2,1)}, bf16[1184,128]{1,0:T(8,128)(2,1)}, u32[]{:S(2)}, u32[]{:S(2)}) collective-permute-start(bf16[1184,128]{1,0:T(8,128)(2,1)} %collective-permute-done.5), channel_id=1, source_target_pairs={{0,1},{1,0},{2,3},{3,2},{4,5},{5,4},{6,7},{7,6},{8,9},{9,8},{10,11... | collective-permute-start | bytes 909320 | tf_op jit(solution)/shard_map/ppermute | solution.py:99

commit v7 on v5

--- a/solution.py
+++ b/solution.py
@@ -58,9 +58,22 @@
     y = jnp.pad(y, ((0, padded - part), (0, 0)))
     y = lax.all_to_all(y.reshape(nz, padded // nz, cols), "z", 0, 0, tiled=False).sum(0)
     y = lax.all_to_all(jnp.broadcast_to(y[None], (nz,) + y.shape), "z", 0, 0, tiled=False)
-    y = y.reshape(padded, cols)[:part]
-    y = lax.all_to_all(jnp.broadcast_to(y[None], (nx,) + y.shape), "x", 0, 0, tiled=False)
-    return y.reshape(rows, cols)
+    own = y.reshape(padded, cols)[:part]
+    y = lax.all_to_all(jnp.broadcast_to(own[None], (nx,) + own.shape), "x", 0, 0, tiled=False)
+    return y.reshape(rows, cols), own
+
+
+def axis_sum(v, axis, n):
+    me = lax.axis_index(axis)
+    slots = jnp.zeros((n,) + v.shape, v.dtype)
+    slots = lax.dynamic_update_index_in_dim(slots, v, me, 0)
+    for s in range(1, n):
+        got = lax.ppermute(v, axis, [(i, (i - s) % n) for i in range(n)])
+        slots = lax.dynamic_update_index_in_dim(slots, got, (me + s) % n, 0)
+    total = slots[0]
+    for k in range(1, n):
+        total = total + slots[k]
+    return total
 
 
 def tensor_sum(v, ny, ncore):
@@ -68,16 +81,7 @@
         v = v + lax.ppermute(v, "core", [(0, 1), (1, 0)])
     else:
         v = lax.psum(v, "core")
-    y = lax.axis_index("y")
-    slots = jnp.zeros((ny,) + v.shape, v.dtype)
-    slots = lax.dynamic_update_index_in_dim(slots, v, y, 0)
-    for s in range(1, ny):
-        got = lax.ppermute(v, "y", [(i, (i - s) % ny) for i in range(ny)])
-        slots = lax.dynamic_update_index_in_dim(slots, got, (y + s) % ny, 0)
-    total = slots[0]
-    for k in range(1, ny):
-        total = total + slots[k]
-    return total
+    return axis_sum(v, "y", ny)
 
 
 def tensor_gather(b, ny):
@@ -109,11 +113,21 @@
         local_grad = gradients[0]
         row_count = weights.shape[0]
         seg_table = group_table(row_count)
-        grad = dp_sum(local_grad, nz, nx) / (nz * nx)
+        total, own = dp_sum(local_grad, nz, nx)
+        grad = total / (nz * nx)
+        part = own.shape[0]
+        start = lax.axis_index("x") * part
+
+        def rows_of(a):
+            return lax.dynamic_slice_in_dim(a, start, part, 0)
+
+        _, _, own_update = adam_part(
+            own / (nz * nx), rows_of(weights), rows_of(first_moment), rows_of(second_moment), rows_of(seg_table)
+        )
+        both = jnp.concatenate([group_squares(weights, seg_table), group_squares(own_update, rows_of(seg_table))])
+        both = tensor_sum(both, ny, ncore)
+        weight_total, step_total = both[:4], axis_sum(both[4:], "x", nx)
         first_new, second_new, update = adam_part(grad, weights, first_moment, second_moment, seg_table)
-        both = jnp.concatenate([group_squares(weights, seg_table), group_squares(update, seg_table)])
-        both = tensor_sum(both, ny, ncore)
-        weight_total, step_total = both[:4], both[4:]
         weights_new, ratios = apply_ratios(weights, update, seg_table, weight_total, step_total)
         if ncore == 2:
             copies = tensor_gather(weights_new.astype(jnp.bfloat16), ny)

time: 125 us -> 127 us (1.016)
  blocking collectives: 51.6 us -> 19.9 us
  waiting for transfers between devices: 23.9 us -> 40.5 us
  starting transfers between devices: 28.6 us -> 43.9 us
    all_to_all x2 -> x0, blocking collectives: 31.7 us -> none  [the longest x1 19.2 us: dp_sum(): lax.all_to_all(y.reshape(nz, padded // nz, cols), 'z', 0, 0, tiled=False)]
    all_to_all x1 -> x3, starting transfers between devices: 3.53 us -> 15.8 us  [the longest x1 8.81 us: dp_sum(): lax.all_to_all(y.reshape(nz, padded // nz, cols), 'z', 0, 0, tiled=False)]
    all_to_all x1 -> x3, waiting for transfers between devices: 11.7 us -> 19.2 us  [the longest x1 9.72 us: dp_sum(): lax.all_to_all(jnp.broadcast_to(y[None], (nz,) + y.shape), 'z', 0, 0, til...]
    ppermute x3 -> x6, waiting for transfers between devices: 2.83 us -> 9.24 us  [axis_sum(): got = lax.ppermute(v, axis, [(i, (i - s) % n) for i in range(n)])]
    ppermute x3 -> x6, starting transfers between devices: 3.78 us -> 7.28 us  [axis_sum(): got = lax.ppermute(v, axis, [(i, (i - s) % n) for i in range(n)])]
    ppermute x4, waiting for transfers between devices: 8.51 us -> 12 us  [shift(): return lax.ppermute(v, 'y', [(i, (i - s) % ny) for i in range(ny)])]
    ppermute x4, starting transfers between devices: 3.56 us -> 6.49 us  [shift(): return lax.ppermute(v, 'y', [(i, (i - s) % ny) for i in range(ny)])]
    ppermute x5, starting transfers between devices: 11.8 us -> 9.18 us  [tensor_gather(): other = lax.ppermute(mine, 'core', swap)]
  transfers between devices with their start and end apart: 14 -> 19, of which waited for: 4 -> 9; matrix products, arithmetic and copies ran while one was open for 6% -> 7% of each run, Pallas kernels for 0% -> 0%
where the time goes in v7:
time: 127 us; the launch traced here: 126 us
  starting transfers between devices  43.9 us (35%)
  waiting for transfers between devices  40.5 us (32%)
  blocking collectives  19.9 us (16%)
  local copies, waits for them, and re-layouts  15.2 us (12%)
  other arithmetic  5.47 us (4%)
    all_to_all x1, blocking collectives, dp_sum(): y = lax.all_to_all(x.reshape(nx, part, cols), 'x', 0, 0, tiled=False).sum(0)  19.9 us
    ppermute x4, waiting for transfers between devices, shift(): return lax.ppermute(v, 'y', [(i, (i - s) % ny) for i in range(ny)])  12 us
    all_to_all x1, waiting for transfers between devices, dp_sum(): lax.all_to_all(jnp.broadcast_to(y[None], (nz,) + y.shape), 'z', 0, 0, til...  9.72 us
    all_to_all x1, waiting for transfers between devices, dp_sum(): lax.all_to_all(y.reshape(nz, padded // nz, cols), 'z', 0, 0, tiled=False)  9.52 us
    ppermute x6, waiting for transfers between devices, axis_sum(): got = lax.ppermute(v, axis, [(i, (i - s) % n) for i in range(n)])  9.24 us
    ppermute x5, starting transfers between devices, tensor_gather(): other = lax.ppermute(mine, 'core', swap)  9.18 us
    all_to_all x1, starting transfers between devices, dp_sum(): lax.all_to_all(y.reshape(nz, padded // nz, cols), 'z', 0, 0, tiled=False)  8.81 us
    ppermute x6, starting transfers between devices, axis_sum(): got = lax.ppermute(v, axis, [(i, (i - s) % n) for i in range(n)])  7.28 us
  transfers between devices with their start and end apart: 19, of which 9 were waited for; matrix products, arithmetic and copies ran while one was open for 7% of the time, Pallas kernels for 0%

profile of v7, /device:TPU:1, one launch (start us, length us, event | category | flops | bytes accessed | tf_op | source)
XLA Modules:
  0.0 126.4 jit_solution(11995863986819493424)
XLA Ops:
  0.6 19.9 %all_to_all.20 = f32[4,592,128]{2,1,0:T(8,128)S(1)} all-to-all(f32[4,592,128]{2,1,0:T(8,128)} %bitcast.29), channel_id=1, replica_groups=mesh['z'=8,'x'=4,'y'=4,'core'=2] {'x'}, dimensions={0} | all-to-all | bytes 2424832 | tf_op jit(solution)/shard_map/all_to_all | solution.py:57
  20.6 0.7 pad.4
  21.4 8.8 %all-to-all-start.1 = ((f32[8,80,128]{2,1,0:T(8,128)}), f32[8,80,128]{2,1,0:T(8,128)S(1)}, u32[]{:S(2)}, u32[]{:S(2)}) async-start(f32[8,80,128]{2,1,0:T(8,128)} %bitcast.2), calls=%async_computation.1 | async-start | bytes 655360 | tf_op jit(solution)/shard_map/all_to_all | solution.py:59
  30.2 0.4 multiply_reduce_fusion
  30.7 9.5 %all-to-all-done.1 = f32[8,80,128]{2,1,0:T(8,128)S(1)} async-done(((f32[8,80,128]{2,1,0:T(8,128)}), f32[8,80,128]{2,1,0:T(8,128)S(1)}, u32[]{:S(2)}, u32[]{:S(2)}) %all-to-all-start.1) | async-done | bytes 327712 | tf_op jit(solution)/shard_map/all_to_all | solution.py:59
  40.3 0.7 broadcast_in_dim.55
  41.0 3.4 %all-to-all-start.2 = ((f32[8,80,128]{2,1,0:T(8,128)}), f32[8,80,128]{2,1,0:T(8,128)S(1)}, u32[]{:S(2)}, u32[]{:S(2)}) async-start(f32[8,80,128]{2,1,0:T(8,128)} %broadcast_in_dim.55), calls=%async_computation.2 | async-start | bytes 655360 | tf_op jit(solution)/shard_map/all_to_all | solution.py:60
  44.8 9.7 %all-to-all-done.2 = f32[8,80,128]{2,1,0:T(8,128)S(1)} async-done(((f32[8,80,128]{2,1,0:T(8,128)}), f32[8,80,128]{2,1,0:T(8,128)S(1)}, u32[]{:S(2)}, u32[]{:S(2)}) %all-to-all-start.2) | async-done | bytes 327712 | tf_op jit(solution)/shard_map/all_to_all | solution.py:60
  54.5 1.4 %multiply_reduce_fusion.1 = (f32[592]{0:T(1024)S(1)}, f32[592,128]{1,0:T(8,128)S(1)}) fusion(f32[2368,128]{1,0:T(8,128)S(1)} %copy-done, s32[]{:T(128)S(6)} %select_n.123, f32[2368,128]{1,0:T(8,128)} %param.7, f32[2368,128]{1,0:T(8,128)} %param.6, f32[592]{0:T(1024)S(1)} %fusion.6, f32[640,128]{1,0:T(8,128)S(1)} %bitcast.28), kind=kLoop, calls=%fused_computation.9 | loop fusion | flops 1211824 | bytes 1520260 | tf_op jit(solution)/shard_map/reduce_sum | solution.py:32
  56.2 5.2 %collective-permute-start = (f32[8]{0:T(128)S(1)}, f32[8]{0:T(128)S(1)}, u32[]{:S(2)}, u32[]{:S(2)}) collective-permute-start(f32[8]{0:T(128)S(1)} %pad_maximum_fusion), channel_id=1, source_target_pairs={{0,1},{1,0},{2,3},{3,2},{4,5},{5,4},{6,7},{7,6},{8,9},{9,8},{10,11... | collective-permute-start | bytes 104 | tf_op jit(solution)/shard_map/ppermute | solution.py:81
  61.5 1.1 broadcast_in_dim.63
  62.6 3.5 %all-to-all-start.3 = ((f32[4,592,128]{2,1,0:T(8,128)}), f32[4,592,128]{2,1,0:T(8,128)S(1)}, u32[]{:S(2)}, u32[]{:S(2)}) async-start(f32[4,592,128]{2,1,0:T(8,128)} %broadcast_in_dim.63), calls=%async_computation.3 | async-start | bytes 2424832 | tf_op jit(solution)/shard_map/all_to_all | solution.py:62
  66.2 2.8 %collective-permute-start.1 = (f32[8]{0:T(128)S(1)}, f32[8]{0:T(128)S(1)}, u32[]{:S(2)}, u32[]{:S(2)}) collective-permute-start(f32[8]{0:T(128)S(1)} %fusion.13), channel_id=1, source_target_pairs={{0,6},{2,0},{4,2},{6,4},{1,7},{3,1},{5,3},{7,5},{8,14},{10,8},{12,... | collective-permute-start | bytes 104 | tf_op jit(solution)/shard_map/ppermute | solution.py:71
  68.9 0.3 collective-permute-start.2
  69.3 0.7 collective-permute-start.3
  70.1 2.8 %collective-permute-done.2 = f32[8]{0:T(128)S(1)} collective-permute-done((f32[8]{0:T(128)S(1)}, f32[8]{0:T(128)S(1)}, u32[]{:S(2)}, u32[]{:S(2)}) %collective-permute-start.2) | collective-permute-done | bytes 64 | tf_op jit(solution)/shard_map/ppermute | solution.py:71
  72.9 0.3 collective-permute-done.3
  73.3 2.6 %collective-permute-start.4 = (f32[4]{0:T(128)S(1)}, f32[4]{0:T(128)S(1)}, u32[]{:S(2)}, u32[]{:S(2)}) collective-permute-start(f32[4]{0:T(128)S(1)} %get-tuple-element.14), channel_id=1, source_target_pairs={{0,24},{8,0},{16,8},{24,16},{1,25},{9,1},{17,9},{25,17},{2,26},{10... | collective-permute-start | bytes 56 | tf_op jit(solution)/shard_map/ppermute | solution.py:71
  76.0 0.3 collective-permute-start.5
  76.3 0.6 collective-permute-start.6
  76.9 4.6 %collective-permute-done.4 = f32[4]{0:T(128)S(1)} collective-permute-done((f32[4]{0:T(128)S(1)}, f32[4]{0:T(128)S(1)}, u32[]{:S(2)}, u32[]{:S(2)}) %collective-permute-start.4) | collective-permute-done | bytes 48 | tf_op jit(solution)/shard_map/ppermute | solution.py:71
  81.5 1.5 %collective-permute-done.5 = f32[4]{0:T(128)S(1)} collective-permute-done((f32[4]{0:T(128)S(1)}, f32[4]{0:T(128)S(1)}, u32[]{:S(2)}, u32[]{:S(2)}) %collective-permute-start.5) | collective-permute-done | bytes 48 | tf_op jit(solution)/shard_map/ppermute | solution.py:71
  83.3 0.2 broadcast_multiply_fusion
  83.6 1.0 copy-done.4
  84.8 0.6 broadcast_in_dim.64
  85.4 0.4 copy-done.1
  85.8 0.7 copy-done.3
  86.5 2.8 %constant_dynamic-update-slice_fusion.6 = (bf16[2368,1024]{1,0:T(8,128)(2,1)S(1)}, bf16[2368,128]{1,0:T(8,128)(2,1)S(1)}, f32[2368,128]{1,0:T(8,128)}, f32[2368,128]{1,0:T(8,128)}) fusion(bf16[2368,1024]{1,0:T(8,128)(2,1)S(1)} %broadcast_in_dim.64, s32[]{:T(128)S(6)} %select_n.139, f32[2368,128]{1,0:T(8,128)S(1)} %copy-done, f32[2368]{0:T(1024)S(1)} %fusion.2, ...), kind=kLoop, calls=%fused_computation.25 | loop fusion | flops 3334144 | bytes 8511492 | tf_op jit(solution)/shard_map/dynamic_update_slice | solution.py:106
  89.3 2.2 %copy-done.2 = bf16[2368,1024]{1,0:T(8,128)(2,1)} copy-done((bf16[2368,1024]{1,0:T(8,128)(2,1)}, bf16[2368,1024]{1,0:T(8,128)(2,1)S(1)}, u32[]{:S(2)}) %copy-start.2) | copy-done | bytes 4849688
  91.5 2.7 %collective-permute-start.8 = (bf16[2368,128]{1,0:T(8,128)(2,1)S(1)}, bf16[2368,128]{1,0:T(8,128)(2,1)S(1)}, u32[]{:S(2)}, u32[]{:S(2)}) collective-permute-start(bf16[2368,128]{1,0:T(8,128)(2,1)S(1)} %get-tuple-element.6), channel_id=1, source_target_pairs={{0,6},{2,0},{4,2},{6,4},{1,7},{3,1},{5,3},{7,5},{8,14},{10,8},{12,... | collective-permute-start | bytes 1818632 | tf_op jit(solution)/shard_map/ppermute | solution.py:94
  94.2 1.2 collective-permute-start.7
  95.5 10.8 %collective-permute-done.8 = bf16[2368,128]{1,0:T(8,128)(2,1)S(1)} collective-permute-done((bf16[2368,128]{1,0:T(8,128)(2,1)S(1)}, bf16[2368,128]{1,0:T(8,128)(2,1)S(1)}, u32[]{:S(2)}, u32[]{:S(2)}) %collective-permute-start.8) | collective-permute-done | bytes 606240 | tf_op jit(solution)/shard_map/ppermute | solution.py:94
  106.3 3.5 %collective-permute-start.12 = (bf16[1184,128]{1,0:T(8,128)(2,1)S(1)}, bf16[1184,128]{1,0:T(8,128)(2,1)S(1)}, u32[]{:S(2)}, u32[]{:S(2)}) collective-permute-start(bf16[1184,128]{1,0:T(8,128)(2,1)S(1)} %slice.76), channel_id=1, source_target_pairs={{0,6},{2,0},{4,2},{6,4},{1,7},{3,1},{5,3},{7,5},{8,14},{10,8},{12,... | collective-permute-start | bytes 909320 | tf_op jit(solution)/shard_map/ppermute | solution.py:94
  109.8 0.3 collective-permute-start.14
  110.1 2.2 %collective-permute-start.9 = (bf16[2368,128]{1,0:T(8,128)(2,1)S(1)}, bf16[2368,128]{1,0:T(8,128)(2,1)S(1)}, u32[]{:S(2)}, u32[]{:S(2)}) collective-permute-start(bf16[2368,128]{1,0:T(8,128)(2,1)S(1)} %collective-permute-done.8), channel_id=1, source_target_pairs={{0,1},{1,0},{2,3},{3,2},{4,5},{5,4},{6,7},{7,6},{8,9},{9,8},{10,11... | collective-permute-start | bytes 1818632 | tf_op jit(solution)/shard_map/ppermute | solution.py:104
  112.4 0.9 constant_dynamic-update-slice_fusion.5
  113.3 0.9 constant_dynamic-update-slice_fusion.4
  114.1 0.4 collective-permute-done.12
  114.5 2.7 %collective-permute-start.13 = (bf16[1184,128]{1,0:T(8,128)(2,1)S(1)}, bf16[1184,128]{1,0:T(8,128)(2,1)S(1)}, u32[]{:S(2)}, u32[]{:S(2)}) collective-permute-start(bf16[1184,128]{1,0:T(8,128)(2,1)S(1)} %collective-permute-done.12), channel_id=1, source_target_pairs={{0,1},{1,0},{2,3},{3,2},{4,5},{5,4},{6,7},{7,6},{8,9},{9,8},{10,11... | collective-permute-start | bytes 909320 | tf_op jit(solution)/shard_map/ppermute | solution.py:104
  117.2 0.7 collective-permute-done.14
  117.9 3.0 %collective-permute-start.15 = (bf16[1184,128]{1,0:T(8,128)(2,1)S(1)}, bf16[1184,128]{1,0:T(8,128)(2,1)S(1)}, u32[]{:S(2)}, u32[]{:S(2)}) collective-permute-start(bf16[1184,128]{1,0:T(8,128)(2,1)S(1)} %collective-permute-done.14), channel_id=1, source_target_pairs={{0,1},{1,0},{2,3},{3,2},{4,5},{5,4},{6,7},{7,6},{8,9},{9,8},{10,11... | collective-permute-start | bytes 909320 | tf_op jit(solution)/shard_map/ppermute | solution.py:104
  120.9 0.9 constant_dynamic-update-slice_fusion.3
  121.8 0.9 constant_dynamic-update-slice_fusion.2
  122.6 0.9 constant_dynamic-update-slice_fusion.1
  123.5 0.7 constant_dynamic-update-slice_fusion
  124.2 0.7 constant_dynamic-update-slice_fusion.7
  125.0 0.7 constant_dynamic-update-slice_fusion.9
  125.7 0.7 constant_dynamic-update-slice_fusion.8
  (51 shorter events, 1.8 us)
Async XLA Ops:
  20.6 9.6 %copy-start = (f32[2368,128]{1,0:T(8,128)S(1)}, f32[2368,128]{1,0:T(8,128)}, u32[]{:S(2)}) copy-start(f32[2368,128]{1,0:T(8,128)} %param.5) | copy-start | bytes 3637252
  21.4 18.8 %all-to-all-start.1 = ((f32[8,80,128]{2,1,0:T(8,128)}), f32[8,80,128]{2,1,0:T(8,128)S(1)}, u32[]{:S(2)}, u32[]{:S(2)}) async-start(f32[8,80,128]{2,1,0:T(8,128)} %bitcast.2), calls=%async_computation.1 | async-start | bytes 655360 | tf_op jit(solution)/shard_map/all_to_all | solution.py:59
  41.0 13.5 %all-to-all-start.2 = ((f32[8,80,128]{2,1,0:T(8,128)}), f32[8,80,128]{2,1,0:T(8,128)S(1)}, u32[]{:S(2)}, u32[]{:S(2)}) async-start(f32[8,80,128]{2,1,0:T(8,128)} %broadcast_in_dim.55), calls=%async_computation.2 | async-start | bytes 655360 | tf_op jit(solution)/shard_map/all_to_all | solution.py:60
  56.2 9.9 %collective-permute-start = (f32[8]{0:T(128)S(1)}, f32[8]{0:T(128)S(1)}, u32[]{:S(2)}, u32[]{:S(2)}) collective-permute-start(f32[8]{0:T(128)S(1)} %pad_maximum_fusion), channel_id=1, source_target_pairs={{0,1},{1,0},{2,3},{3,2},{4,5},{5,4},{6,7},{7,6},{8,9},{9,8},{10,11... | collective-permute-start | bytes 104 | tf_op jit(solution)/shard_map/ppermute | solution.py:81
  62.6 20.7 %all-to-all-start.3 = ((f32[4,592,128]{2,1,0:T(8,128)}), f32[4,592,128]{2,1,0:T(8,128)S(1)}, u32[]{:S(2)}, u32[]{:S(2)}) async-start(f32[4,592,128]{2,1,0:T(8,128)} %broadcast_in_dim.63), calls=%async_computation.3 | async-start | bytes 2424832 | tf_op jit(solution)/shard_map/all_to_all | solution.py:62
  66.2 3.8 %collective-permute-start.1 = (f32[8]{0:T(128)S(1)}, f32[8]{0:T(128)S(1)}, u32[]{:S(2)}, u32[]{:S(2)}) collective-permute-start(f32[8]{0:T(128)S(1)} %fusion.13), channel_id=1, source_target_pairs={{0,6},{2,0},{4,2},{6,4},{1,7},{3,1},{5,3},{7,5},{8,14},{10,8},{12,... | collective-permute-start | bytes 104 | tf_op jit(solution)/shard_map/ppermute | solution.py:71
  68.9 3.9 %collective-permute-start.2 = (f32[8]{0:T(128)S(1)}, f32[8]{0:T(128)S(1)}, u32[]{:S(2)}, u32[]{:S(2)}) collective-permute-start(f32[8]{0:T(128)S(1)} %fusion.13), channel_id=1, source_target_pairs={{0,4},{2,6},{4,0},{6,2},{1,5},{3,7},{5,1},{7,3},{8,12},{10,14},{12... | collective-permute-start | bytes 104 | tf_op jit(solution)/shard_map/ppermute | solution.py:71
  69.3 3.9 %collective-permute-start.3 = (f32[8]{0:T(128)S(1)}, f32[8]{0:T(128)S(1)}, u32[]{:S(2)}, u32[]{:S(2)}) collective-permute-start(f32[8]{0:T(128)S(1)} %fusion.13), channel_id=1, source_target_pairs={{0,2},{2,4},{4,6},{6,0},{1,3},{3,5},{5,7},{7,1},{8,10},{10,12},{12... | collective-permute-start | bytes 104 | tf_op jit(solution)/shard_map/ppermute | solution.py:71
  73.3 8.2 %collective-permute-start.4 = (f32[4]{0:T(128)S(1)}, f32[4]{0:T(128)S(1)}, u32[]{:S(2)}, u32[]{:S(2)}) collective-permute-start(f32[4]{0:T(128)S(1)} %get-tuple-element.14), channel_id=1, source_target_pairs={{0,24},{8,0},{16,8},{24,16},{1,25},{9,1},{17,9},{25,17},{2,26},{10... | collective-permute-start | bytes 56 | tf_op jit(solution)/shard_map/ppermute | solution.py:71
  76.0 7.0 %collective-permute-start.5 = (f32[4]{0:T(128)S(1)}, f32[4]{0:T(128)S(1)}, u32[]{:S(2)}, u32[]{:S(2)}) collective-permute-start(f32[4]{0:T(128)S(1)} %get-tuple-element.14), channel_id=1, source_target_pairs={{0,16},{8,24},{16,0},{24,8},{1,17},{9,25},{17,1},{25,9},{2,18},{10... | collective-permute-start | bytes 56 | tf_op jit(solution)/shard_map/ppermute | solution.py:71
  76.3 6.8 %collective-permute-start.6 = (f32[4]{0:T(128)S(1)}, f32[4]{0:T(128)S(1)}, u32[]{:S(2)}, u32[]{:S(2)}) collective-permute-start(f32[4]{0:T(128)S(1)} %get-tuple-element.14), channel_id=1, source_target_pairs={{0,8},{8,16},{16,24},{24,0},{1,9},{9,17},{17,25},{25,1},{2,10},{10... | collective-permute-start | bytes 56 | tf_op jit(solution)/shard_map/ppermute | solution.py:71
  83.1 0.5 copy-start.5
  83.3 1.3 %copy-start.4 = (f32[2368,128]{1,0:T(8,128)S(1)}, f32[2368,128]{1,0:T(8,128)}, u32[]{:S(2)}) copy-start(f32[2368,128]{1,0:T(8,128)} %param.6) | copy-start | bytes 3637252
  84.7 1.0 copy-start.1
  84.8 1.7 %copy-start.3 = (f32[2368,128]{1,0:T(8,128)S(1)}, f32[2368,128]{1,0:T(8,128)}, u32[]{:S(2)}) copy-start(f32[2368,128]{1,0:T(8,128)} %param.7) | copy-start | bytes 3637252
  89.3 2.2 %copy-start.2 = (bf16[2368,1024]{1,0:T(8,128)(2,1)}, bf16[2368,1024]{1,0:T(8,128)(2,1)S(1)}, u32[]{:S(2)}) copy-start(bf16[2368,1024]{1,0:T(8,128)(2,1)S(1)} %get-tuple-element.5) | copy-start | bytes 14548996
  91.5 14.8 %collective-permute-start.8 = (bf16[2368,128]{1,0:T(8,128)(2,1)S(1)}, bf16[2368,128]{1,0:T(8,128)(2,1)S(1)}, u32[]{:S(2)}, u32[]{:S(2)}) collective-permute-start(bf16[2368,128]{1,0:T(8,128)(2,1)S(1)} %get-tuple-element.6), channel_id=1, source_target_pairs={{0,6},{2,0},{4,2},{6,4},{1,7},{3,1},{5,3},{7,5},{8,14},{10,8},{12,... | collective-permute-start | bytes 1818632 | tf_op jit(solution)/shard_map/ppermute | solution.py:94
  94.2 15.6 %collective-permute-start.10 = (bf16[2368,128]{1,0:T(8,128)(2,1)S(1)}, bf16[2368,128]{1,0:T(8,128)(2,1)S(1)}, u32[]{:S(2)}, u32[]{:S(2)}) collective-permute-start(bf16[2368,128]{1,0:T(8,128)(2,1)S(1)} %get-tuple-element.6), channel_id=1, source_target_pairs={{0,2},{2,4},{4,6},{6,0},{1,3},{3,5},{5,7},{7,1},{8,10},{10,12},{12... | collective-permute-start | bytes 1818632 | tf_op jit(solution)/shard_map/ppermute | solution.py:94
  94.2 18.2 %collective-permute-start.7 = (bf16[2368,128]{1,0:T(8,128)(2,1)S(1)}, bf16[2368,128]{1,0:T(8,128)(2,1)S(1)}, u32[]{:S(2)}, u32[]{:S(2)}) collective-permute-start(bf16[2368,128]{1,0:T(8,128)(2,1)S(1)} %get-tuple-element.6), channel_id=1, source_target_pairs={{0,1},{1,0},{2,3},{3,2},{4,5},{5,4},{6,7},{7,6},{8,9},{9,8},{10,11... | collective-permute-start | bytes 1818632 | tf_op jit(solution)/shard_map/ppermute | solution.py:104
  106.3 8.2 %collective-permute-start.12 = (bf16[1184,128]{1,0:T(8,128)(2,1)S(1)}, bf16[1184,128]{1,0:T(8,128)(2,1)S(1)}, u32[]{:S(2)}, u32[]{:S(2)}) collective-permute-start(bf16[1184,128]{1,0:T(8,128)(2,1)S(1)} %slice.76), channel_id=1, source_target_pairs={{0,6},{2,0},{4,2},{6,4},{1,7},{3,1},{5,3},{7,5},{8,14},{10,8},{12,... | collective-permute-start | bytes 909320 | tf_op jit(solution)/shard_map/ppermute | solution.py:94
  109.8 8.1 %collective-permute-start.14 = (bf16[1184,128]{1,0:T(8,128)(2,1)S(1)}, bf16[1184,128]{1,0:T(8,128)(2,1)S(1)}, u32[]{:S(2)}, u32[]{:S(2)}) collective-permute-start(bf16[1184,128]{1,0:T(8,128)(2,1)S(1)} %slice.77), channel_id=1, source_target_pairs={{0,2},{2,4},{4,6},{6,0},{1,3},{3,5},{5,7},{7,1},{8,10},{10,12},{12... | collective-permute-start | bytes 909320 | tf_op jit(solution)/shard_map/ppermute | solution.py:94
  110.1 10.8 %collective-permute-start.9 = (bf16[2368,128]{1,0:T(8,128)(2,1)S(1)}, bf16[2368,128]{1,0:T(8,128)(2,1)S(1)}, u32[]{:S(2)}, u32[]{:S(2)}) collective-permute-start(bf16[2368,128]{1,0:T(8,128)(2,1)S(1)} %collective-permute-done.8), channel_id=1, source_target_pairs={{0,1},{1,0},{2,3},{3,2},{4,5},{5,4},{6,7},{7,6},{8,9},{9,8},{10,11... | collective-permute-start | bytes 1818632 | tf_op jit(solution)/shard_map/ppermute | solution.py:104
  112.3 10.3 %collective-permute-start.11 = (bf16[2368,128]{1,0:T(8,128)(2,1)S(1)}, bf16[2368,128]{1,0:T(8,128)(2,1)S(1)}, u32[]{:S(2)}, u32[]{:S(2)}) collective-permute-start(bf16[2368,128]{1,0:T(8,128)(2,1)S(1)} %collective-permute-done.10), channel_id=1, source_target_pairs={{0,1},{1,0},{2,3},{3,2},{4,5},{5,4},{6,7},{7,6},{8,9},{9,8},{10,11... | collective-permute-start | bytes 1818632 | tf_op jit(solution)/shard_map/ppermute | solution.py:104
  114.5 9.7 %collective-permute-start.13 = (bf16[1184,128]{1,0:T(8,128)(2,1)S(1)}, bf16[1184,128]{1,0:T(8,128)(2,1)S(1)}, u32[]{:S(2)}, u32[]{:S(2)}) collective-permute-start(bf16[1184,128]{1,0:T(8,128)(2,1)S(1)} %collective-permute-done.12), channel_id=1, source_target_pairs={{0,1},{1,0},{2,3},{3,2},{4,5},{5,4},{6,7},{7,6},{8,9},{9,8},{10,11... | collective-permute-start | bytes 909320 | tf_op jit(solution)/shard_map/ppermute | solution.py:104
  117.9 7.8 %collective-permute-start.15 = (bf16[1184,128]{1,0:T(8,128)(2,1)S(1)}, bf16[1184,128]{1,0:T(8,128)(2,1)S(1)}, u32[]{:S(2)}, u32[]{:S(2)}) collective-permute-start(bf16[1184,128]{1,0:T(8,128)(2,1)S(1)} %collective-permute-done.14), channel_id=1, source_target_pairs={{0,1},{1,0},{2,3},{3,2},{4,5},{5,4},{6,7},{7,6},{8,9},{9,8},{10,11... | collective-permute-start | bytes 909320 | tf_op jit(solution)/shard_map/ppermute | solution.py:104

commit v8 on v5

--- a/solution.py
+++ b/solution.py
@@ -17,7 +17,7 @@
 learn_rate = 0.01
 decay_rate = 0.01
 
-DP = ("z", "x")
+DP = ("zh", "zl", "x")
 TN = ("y", "core")
 
 
@@ -53,12 +53,21 @@
 def dp_sum(x, nz, nx):
     rows, cols = x.shape
     part = rows // nx
-    padded = -(-part // (8 * nz)) * (8 * nz)
+    padded = -(-part // (16 * nz)) * (16 * nz)
+    half = padded // 2
     y = lax.all_to_all(x.reshape(nx, part, cols), "x", 0, 0, tiled=False).sum(0)
     y = jnp.pad(y, ((0, padded - part), (0, 0)))
-    y = lax.all_to_all(y.reshape(nz, padded // nz, cols), "z", 0, 0, tiled=False).sum(0)
-    y = lax.all_to_all(jnp.broadcast_to(y[None], (nz,) + y.shape), "z", 0, 0, tiled=False)
-    y = y.reshape(padded, cols)[:part]
+    zl = lax.axis_index("zl")
+    swap = [(0, 1), (1, 0)]
+    keep = lax.dynamic_slice_in_dim(y, zl * half, half, 0)
+    send = lax.dynamic_slice_in_dim(y, (1 - zl) * half, half, 0)
+    y = keep + lax.ppermute(send, "zl", swap)
+    nh = nz // 2
+    y = lax.all_to_all(y.reshape(nh, half // nh, cols), "zh", 0, 0, tiled=False).sum(0)
+    y = lax.all_to_all(jnp.broadcast_to(y[None], (nh,) + y.shape), "zh", 0, 0, tiled=False)
+    y = y.reshape(half, cols)
+    got = lax.ppermute(y, "zl", swap)
+    y = jnp.where(zl == 0, jnp.concatenate([y, got], 0), jnp.concatenate([got, y], 0))[:part]
     y = lax.all_to_all(jnp.broadcast_to(y[None], (nx,) + y.shape), "x", 0, 0, tiled=False)
     return y.reshape(rows, cols)
 
@@ -132,7 +141,7 @@
     tn_devices = devices[0, :]
     ncore = len({d.core_on_chip for d in tn_devices})
     ny = tn_devices.size // ncore
-    return Mesh(devices.reshape(nz, nx, ny, ncore), ("z", "x", "y", "core")), (nz, nx, ny, ncore)
+    return Mesh(devices.reshape(nz // 2, 2, nx, ny, ncore), ("zh", "zl", "x", "y", "core")), (nz, nx, ny, ncore)
 
 
 def solution(mesh):

time: 125 us -> 130 us (1.040)
  blocking collectives: 51.6 us -> 25.1 us
  waiting for transfers between devices: 23.9 us -> 44.3 us
  starting transfers between devices: 28.6 us -> 39.3 us
    all_to_all x3 -> x2, blocking collectives: 51.6 us -> 25.1 us  [the longest x1 15.2 us: dp_sum(): lax.all_to_all(y.reshape(nh, half // nh, cols), 'zh', 0, 0, tiled=False)]
    all_to_all x0 -> x1, waiting for transfers between devices: none -> 15.1 us  [dp_sum(): y = lax.all_to_all(x.reshape(nx, part, cols), 'x', 0, 0, tiled=False).sum(0)]
    ppermute x0 -> x2, waiting for transfers between devices: none -> 6.64 us  [the longest x1 3.93 us: dp_sum(): got = lax.ppermute(y, 'zl', swap)]
    all_to_all x0 -> x1, starting transfers between devices: none -> 4.84 us  [dp_sum(): y = lax.all_to_all(x.reshape(nx, part, cols), 'x', 0, 0, tiled=False).sum(0)]
    ppermute x0 -> x2, starting transfers between devices: none -> 3.39 us  [the longest x1 2.65 us: dp_sum(): y = keep + lax.ppermute(send, 'zl', swap)]
    ppermute x1, starting transfers between devices: 5.88 us -> 8.34 us  [tensor_sum(): v = v + lax.ppermute(v, 'core', [(0, 1), (1, 0)])]
    all_to_all x1, waiting for transfers between devices: 11.7 us -> 10.4 us  [dp_sum(): lax.all_to_all(jnp.broadcast_to(y[None], (nx,) + y.shape), 'x', 0, 0, til...]
  transfers between devices with their start and end apart: 14 -> 17, of which waited for: 4 -> 7; matrix products, arithmetic and copies ran while one was open for 6% -> 6% of each run, Pallas kernels for 0% -> 0%
where the time goes in v8:
time: 130 us; the launch traced here: 129 us
  waiting for transfers between devices  44.3 us (34%)
  starting transfers between devices  39.3 us (30%)
  blocking collectives  25.1 us (19%)
  local copies, waits for them, and re-layouts  14.1 us (11%)
  other arithmetic  5.08 us (4%)
    all_to_all x1, blocking collectives, dp_sum(): lax.all_to_all(y.reshape(nh, half // nh, cols), 'zh', 0, 0, tiled=False)  15.2 us
    all_to_all x1, waiting for transfers between devices, dp_sum(): y = lax.all_to_all(x.reshape(nx, part, cols), 'x', 0, 0, tiled=False).sum(0)  15.1 us
    ppermute x5, starting transfers between devices, tensor_gather(): other = lax.ppermute(mine, 'core', swap)  11.8 us
    all_to_all x1, waiting for transfers between devices, dp_sum(): lax.all_to_all(jnp.broadcast_to(y[None], (nx,) + y.shape), 'x', 0, 0, til...  10.4 us
    all_to_all x1, blocking collectives, dp_sum(): lax.all_to_all(jnp.broadcast_to(y[None], (nh,) + y.shape), 'zh', 0, 0, ti...  9.87 us
    ppermute x4, waiting for transfers between devices, shift(): return lax.ppermute(v, 'y', [(i, (i - s) % ny) for i in range(ny)])  8.51 us
    ppermute x1, starting transfers between devices, tensor_sum(): v = v + lax.ppermute(v, 'core', [(0, 1), (1, 0)])  8.34 us
    all_to_all x1, starting transfers between devices, dp_sum(): y = lax.all_to_all(x.reshape(nx, part, cols), 'x', 0, 0, tiled=False).sum(0)  4.84 us
  transfers between devices with their start and end apart: 17, of which 7 were waited for; matrix products, arithmetic and copies ran while one was open for 6% of the time, Pallas kernels for 0%

profile of v8, /device:TPU:1, one launch (start us, length us, event | category | flops | bytes accessed | tf_op | source)
XLA Modules:
  0.0 129.2 jit_solution(15597108885728046938)
XLA Ops:
  0.6 4.8 %all-to-all-start = ((f32[4,592,128]{2,1,0:T(8,128)}), f32[4,592,128]{2,1,0:T(8,128)S(1)}, u32[]{:S(2)}, u32[]{:S(2)}) async-start(f32[4,592,128]{2,1,0:T(8,128)} %bitcast.25), calls=%async_computation | async-start | bytes 2424832 | tf_op jit(solution)/shard_map/all_to_all | solution.py:58
  5.5 15.1 %all-to-all-done = f32[4,592,128]{2,1,0:T(8,128)S(1)} async-done(((f32[4,592,128]{2,1,0:T(8,128)}), f32[4,592,128]{2,1,0:T(8,128)S(1)}, u32[]{:S(2)}, u32[]{:S(2)}) %all-to-all-start) | async-done | bytes 1212448 | tf_op jit(solution)/shard_map/all_to_all | solution.py:58
  20.7 2.6 %collective-permute-start = (f32[320,128]{1,0:T(8,128)S(1)}, f32[320,128]{1,0:T(8,128)S(1)}, u32[]{:S(2)}, u32[]{:S(2)}) collective-permute-start(f32[320,128]{1,0:T(8,128)S(1)} %pad_dynamic-slice_fusion), channel_id=1, source_target_pairs={{0,32},{32,0},{1,33},{33,1},{2,34},{34,2},{3,35},{35,3},{4,36},{36... | collective-permute-start | bytes 491528 | tf_op jit(solution)/shard_map/ppermute | solution.py:64
  23.3 2.7 %collective-permute-done = f32[320,128]{1,0:T(8,128)S(1)} collective-permute-done((f32[320,128]{1,0:T(8,128)S(1)}, f32[320,128]{1,0:T(8,128)S(1)}, u32[]{:S(2)}, u32[]{:S(2)}) %collective-permute-start) | collective-permute-done | bytes 163872 | tf_op jit(solution)/shard_map/ppermute | solution.py:64
  26.0 15.2 %all_to_all.20 = f32[4,80,128]{2,1,0:T(8,128)S(1)} all-to-all(f32[4,80,128]{2,1,0:T(8,128)S(1)} %bitcast.28), channel_id=1, replica_groups=mesh['zh'=4,'zl'=2,'x'=4,'y'=4,'core'=2] {'zh'}, dimensions={0} | all-to-all | bytes 327680 | tf_op jit(solution)/shard_map/all_to_all | solution.py:66
  41.3 9.9 %all_to_all.21 = f32[4,80,128]{2,1,0:T(8,128)S(1)} all-to-all(f32[4,80,128]{2,1,0:T(8,128)S(1)} %broadcast_in_dim.43), channel_id=1, replica_groups=mesh['zh'=4,'zl'=2,'x'=4,'y'=4,'core'=2] {'zh'}, dimensions={0} | all-to-all | bytes 327680 | tf_op jit(solution)/shard_map/all_to_all | solution.py:67
  51.2 0.7 collective-permute-start.1
  51.9 3.9 %collective-permute-done.1 = f32[320,128]{1,0:T(8,128)S(1)} collective-permute-done((f32[320,128]{1,0:T(8,128)S(1)}, f32[320,128]{1,0:T(8,128)S(1)}, u32[]{:S(2)}, u32[]{:S(2)}) %collective-permute-start.1) | collective-permute-done | bytes 163872 | tf_op jit(solution)/shard_map/ppermute | solution.py:69
  55.9 1.1 broadcast_in_dim.44
  57.0 3.5 %all-to-all-start.3 = ((f32[4,592,128]{2,1,0:T(8,128)}), f32[4,592,128]{2,1,0:T(8,128)S(1)}, u32[]{:S(2)}, u32[]{:S(2)}) async-start(f32[4,592,128]{2,1,0:T(8,128)} %broadcast_in_dim.44), calls=%async_computation.3 | async-start | bytes 2424832 | tf_op jit(solution)/shard_map/all_to_all | solution.py:71
  60.7 10.4 %all-to-all-done.3 = f32[4,592,128]{2,1,0:T(8,128)S(1)} async-done(((f32[4,592,128]{2,1,0:T(8,128)}), f32[4,592,128]{2,1,0:T(8,128)S(1)}, u32[]{:S(2)}, u32[]{:S(2)}) %all-to-all-start.3) | async-done | bytes 1212448 | tf_op jit(solution)/shard_map/all_to_all | solution.py:71
  71.1 0.2 broadcast_multiply_fusion
  71.3 1.1 copy-done.5
  72.4 0.4 copy-done.6
  72.7 0.3 bitcast_add_fusion
  73.0 1.2 copy-done.2
  74.2 2.0 %multiply_reduce_fusion = (f32[2368]{0:T(1024)S(1)}, f32[2368,128]{1,0:T(8,128)}, f32[2368]{0:T(1024)S(1)}) fusion(f32[2368,128]{1,0:T(8,128)S(1)} %copy-done.2, f32[2368]{0:T(1024)S(1)} %fusion.3, f32[2368,128]{1,0:T(8,128)S(1)} %get-tuple-element.17, f32[2368,128]{1,0:T(8,128)S(1)} %get-tuple-element.18), kind=kLoop, calls=%fused_computation.3 | loop fusion | flops 3026304 | bytes 4878080 | tf_op jit(solution)/shard_map/reduce_sum | solution.py:32
  76.2 0.1 convolution_bitcast_fusion.1
  76.4 0.2 convolution_bitcast_fusion
  76.6 0.1 pad_maximum_fusion.2
  76.7 8.3 %collective-permute-start.2 = (f32[8]{0:T(128)S(1)}, f32[8]{0:T(128)S(1)}, u32[]{:S(2)}, u32[]{:S(2)}) collective-permute-start(f32[8]{0:T(128)S(1)} %pad_maximum_fusion.2), channel_id=1, source_target_pairs={{0,1},{1,0},{2,3},{3,2},{4,5},{5,4},{6,7},{7,6},{8,9},{9,8},{10,11... | collective-permute-start | bytes 104 | tf_op jit(solution)/shard_map/ppermute | solution.py:77
  85.0 0.8 collective-permute-done.2
  85.9 2.7 %collective-permute-start.3 = (f32[8]{0:T(128)S(1)}, f32[8]{0:T(128)S(1)}, u32[]{:S(2)}, u32[]{:S(2)}) collective-permute-start(f32[8]{0:T(128)S(1)} %fusion.12), channel_id=1, source_target_pairs={{0,6},{2,0},{4,2},{6,4},{1,7},{3,1},{5,3},{7,5},{8,14},{10,8},{12,... | collective-permute-start | bytes 104 | tf_op jit(solution)/shard_map/ppermute | solution.py:84
  88.7 0.3 collective-permute-start.4
  89.0 0.7 collective-permute-start.5
  89.8 2.8 %collective-permute-done.4 = f32[8]{0:T(128)S(1)} collective-permute-done((f32[8]{0:T(128)S(1)}, f32[8]{0:T(128)S(1)}, u32[]{:S(2)}, u32[]{:S(2)}) %collective-permute-start.4) | collective-permute-done | bytes 64 | tf_op jit(solution)/shard_map/ppermute | solution.py:84
  92.7 0.3 convolution_reduce_fusion
  93.0 2.8 %broadcast_in_dim.49 = bf16[2368,1024]{1,0:T(8,128)(2,1)} broadcast(bf16[]{:T(256)} %constant.108.clone.1), dimensions={} | broadcast | bytes 4849666 | tf_op jit(solution)/shard_map/broadcast_in_dim | solution.py:107
  95.9 1.6 %constant_dynamic-update-slice_fusion.7 = (bf16[2368,1024]{1,0:T(8,128)(2,1)}, bf16[2368,128]{1,0:T(8,128)(2,1)S(1)}, f32[2368,128]{1,0:T(8,128)}) fusion(bf16[2368,1024]{1,0:T(8,128)(2,1)} %broadcast_in_dim.49, s32[]{:T(128)S(6)} %select_n.113, f32[2368,128]{1,0:T(8,128)S(1)} %copy-done.3, f32[2368,128]{1,0:T(8,128)S(1)} %copy-done.4, ...), kind=kLoop, calls=%fused_computation.32 | loop fusion | flops 909312 | bytes 4859140 | tf_op jit(solution)/shard_map/dynamic_update_slice | solution.py:111
  97.5 0.4 collective-permute-start.7
  97.9 1.0 collective-permute-start.9
  98.9 2.6 %collective-permute-start.6 = (bf16[2368,128]{1,0:T(8,128)(2,1)S(1)}, bf16[2368,128]{1,0:T(8,128)(2,1)S(1)}, u32[]{:S(2)}, u32[]{:S(2)}) collective-permute-start(bf16[2368,128]{1,0:T(8,128)(2,1)S(1)} %get-tuple-element.6), channel_id=1, source_target_pairs={{0,1},{1,0},{2,3},{3,2},{4,5},{5,4},{6,7},{7,6},{8,9},{9,8},{10,11... | collective-permute-start | bytes 1818632 | tf_op jit(solution)/shard_map/ppermute | solution.py:109
  101.5 0.6 fusion.11
  102.1 8.5 %collective-permute-done.7 = bf16[2368,128]{1,0:T(8,128)(2,1)S(1)} collective-permute-done((bf16[2368,128]{1,0:T(8,128)(2,1)S(1)}, bf16[2368,128]{1,0:T(8,128)(2,1)S(1)}, u32[]{:S(2)}, u32[]{:S(2)}) %collective-permute-start.7) | collective-permute-done | bytes 606240 | tf_op jit(solution)/shard_map/ppermute | solution.py:99
  110.7 2.0 %collective-permute-start.11 = (bf16[1184,128]{1,0:T(8,128)(2,1)S(1)}, bf16[1184,128]{1,0:T(8,128)(2,1)S(1)}, u32[]{:S(2)}, u32[]{:S(2)}) collective-permute-start(bf16[1184,128]{1,0:T(8,128)(2,1)S(1)} %slice.48), channel_id=1, source_target_pairs={{0,6},{2,0},{4,2},{6,4},{1,7},{3,1},{5,3},{7,5},{8,14},{10,8},{12,... | collective-permute-start | bytes 909320 | tf_op jit(solution)/shard_map/ppermute | solution.py:99
  112.8 3.0 %collective-permute-start.8 = (bf16[2368,128]{1,0:T(8,128)(2,1)S(1)}, bf16[2368,128]{1,0:T(8,128)(2,1)S(1)}, u32[]{:S(2)}, u32[]{:S(2)}) collective-permute-start(bf16[2368,128]{1,0:T(8,128)(2,1)S(1)} %collective-permute-done.7), channel_id=1, source_target_pairs={{0,1},{1,0},{2,3},{3,2},{4,5},{5,4},{6,7},{7,6},{8,9},{9,8},{10,11... | collective-permute-start | bytes 1818632 | tf_op jit(solution)/shard_map/ppermute | solution.py:109
  115.8 0.1 collective-permute-start.10
  115.9 0.9 constant_dynamic-update-slice_fusion.6
  116.8 0.9 constant_dynamic-update-slice_fusion.5
  117.6 2.8 %collective-permute-start.12 = (bf16[1184,128]{1,0:T(8,128)(2,1)S(1)}, bf16[1184,128]{1,0:T(8,128)(2,1)S(1)}, u32[]{:S(2)}, u32[]{:S(2)}) collective-permute-start(bf16[1184,128]{1,0:T(8,128)(2,1)S(1)} %collective-permute-done.11), channel_id=1, source_target_pairs={{0,1},{1,0},{2,3},{3,2},{4,5},{5,4},{6,7},{7,6},{8,9},{9,8},{10,11... | collective-permute-start | bytes 909320 | tf_op jit(solution)/shard_map/ppermute | solution.py:109
  120.5 3.2 %collective-permute-start.14 = (bf16[1184,128]{1,0:T(8,128)(2,1)S(1)}, bf16[1184,128]{1,0:T(8,128)(2,1)S(1)}, u32[]{:S(2)}, u32[]{:S(2)}) collective-permute-start(bf16[1184,128]{1,0:T(8,128)(2,1)S(1)} %collective-permute-done.13), channel_id=1, source_target_pairs={{0,1},{1,0},{2,3},{3,2},{4,5},{5,4},{6,7},{7,6},{8,9},{9,8},{10,11... | collective-permute-start | bytes 909320 | tf_op jit(solution)/shard_map/ppermute | solution.py:109
  123.7 0.9 constant_dynamic-update-slice_fusion.4
  124.6 0.9 constant_dynamic-update-slice_fusion.3
  125.4 0.9 constant_dynamic-update-slice_fusion.2
  126.3 0.7 constant_dynamic-update-slice_fusion.1
  127.0 0.7 constant_dynamic-update-slice_fusion
  127.8 0.7 constant_dynamic-update-slice_fusion.9
  128.5 0.7 constant_dynamic-update-slice_fusion.8
  (44 shorter events, 0.7 us)
Async XLA Ops:
  0.6 19.9 %all-to-all-start = ((f32[4,592,128]{2,1,0:T(8,128)}), f32[4,592,128]{2,1,0:T(8,128)S(1)}, u32[]{:S(2)}, u32[]{:S(2)}) async-start(f32[4,592,128]{2,1,0:T(8,128)} %bitcast.25), calls=%async_computation | async-start | bytes 2424832 | tf_op jit(solution)/shard_map/all_to_all | solution.py:58
  20.7 5.4 %collective-permute-start = (f32[320,128]{1,0:T(8,128)S(1)}, f32[320,128]{1,0:T(8,128)S(1)}, u32[]{:S(2)}, u32[]{:S(2)}) collective-permute-start(f32[320,128]{1,0:T(8,128)S(1)} %pad_dynamic-slice_fusion), channel_id=1, source_target_pairs={{0,32},{32,0},{1,33},{33,1},{2,34},{34,2},{3,35},{35,3},{4,36},{36... | collective-permute-start | bytes 491528 | tf_op jit(solution)/shard_map/ppermute | solution.py:64
  51.2 4.7 %collective-permute-start.1 = (f32[320,128]{1,0:T(8,128)S(1)}, f32[320,128]{1,0:T(8,128)S(1)}, u32[]{:S(2)}, u32[]{:S(2)}) collective-permute-start(f32[320,128]{1,0:T(8,128)S(1)} %bitcast.26), channel_id=1, source_target_pairs={{0,32},{32,0},{1,33},{33,1},{2,34},{34,2},{3,35},{35,3},{4,36},{36... | collective-permute-start | bytes 491528 | tf_op jit(solution)/shard_map/ppermute | solution.py:69
  57.0 14.1 %all-to-all-start.3 = ((f32[4,592,128]{2,1,0:T(8,128)}), f32[4,592,128]{2,1,0:T(8,128)S(1)}, u32[]{:S(2)}, u32[]{:S(2)}) async-start(f32[4,592,128]{2,1,0:T(8,128)} %broadcast_in_dim.44), calls=%async_computation.3 | async-start | bytes 2424832 | tf_op jit(solution)/shard_map/all_to_all | solution.py:71
  71.1 1.3 copy-start.5
  71.1 1.6 %copy-start.6 = (f32[2368,128]{1,0:T(8,128)S(1)}, f32[2368,128]{1,0:T(8,128)}, u32[]{:S(2)}) copy-start(f32[2368,128]{1,0:T(8,128)} %param.6) | copy-start | bytes 3637252
  72.7 1.5 %copy-start.2 = (f32[2368,128]{1,0:T(8,128)S(1)}, f32[2368,128]{1,0:T(8,128)}, u32[]{:S(2)}) copy-start(f32[2368,128]{1,0:T(8,128)} %param.5) | copy-start | bytes 3637252
  73.0 3.2 %copy-start = (f32[2368,128]{1,0:T(8,128)}, f32[2368,128]{1,0:T(8,128)S(1)}, u32[]{:S(2)}) copy-start(f32[2368,128]{1,0:T(8,128)S(1)} %get-tuple-element.17) | copy-start | bytes 3637252
  73.0 3.2 %copy-start.1 = (f32[2368,128]{1,0:T(8,128)}, f32[2368,128]{1,0:T(8,128)S(1)}, u32[]{:S(2)}) copy-start(f32[2368,128]{1,0:T(8,128)S(1)} %get-tuple-element.18) | copy-start | bytes 3637252
  76.7 9.2 %collective-permute-start.2 = (f32[8]{0:T(128)S(1)}, f32[8]{0:T(128)S(1)}, u32[]{:S(2)}, u32[]{:S(2)}) collective-permute-start(f32[8]{0:T(128)S(1)} %pad_maximum_fusion.2), channel_id=1, source_target_pairs={{0,1},{1,0},{2,3},{3,2},{4,5},{5,4},{6,7},{7,6},{8,9},{9,8},{10,11... | collective-permute-start | bytes 104 | tf_op jit(solution)/shard_map/ppermute | solution.py:77
  85.9 3.8 %collective-permute-start.3 = (f32[8]{0:T(128)S(1)}, f32[8]{0:T(128)S(1)}, u32[]{:S(2)}, u32[]{:S(2)}) collective-permute-start(f32[8]{0:T(128)S(1)} %fusion.12), channel_id=1, source_target_pairs={{0,6},{2,0},{4,2},{6,4},{1,7},{3,1},{5,3},{7,5},{8,14},{10,8},{12,... | collective-permute-start | bytes 104 | tf_op jit(solution)/shard_map/ppermute | solution.py:84
  88.7 3.9 %collective-permute-start.4 = (f32[8]{0:T(128)S(1)}, f32[8]{0:T(128)S(1)}, u32[]{:S(2)}, u32[]{:S(2)}) collective-permute-start(f32[8]{0:T(128)S(1)} %fusion.12), channel_id=1, source_target_pairs={{0,4},{2,6},{4,0},{6,2},{1,5},{3,7},{5,1},{7,3},{8,12},{10,14},{12... | collective-permute-start | bytes 104 | tf_op jit(solution)/shard_map/ppermute | solution.py:84
  89.0 3.6 %collective-permute-start.5 = (f32[8]{0:T(128)S(1)}, f32[8]{0:T(128)S(1)}, u32[]{:S(2)}, u32[]{:S(2)}) collective-permute-start(f32[8]{0:T(128)S(1)} %fusion.12), channel_id=1, source_target_pairs={{0,2},{2,4},{4,6},{6,0},{1,3},{3,5},{5,7},{7,1},{8,10},{10,12},{12... | collective-permute-start | bytes 104 | tf_op jit(solution)/shard_map/ppermute | solution.py:84
  93.0 2.9 %copy-start.3 = (f32[2368,128]{1,0:T(8,128)S(1)}, f32[2368,128]{1,0:T(8,128)}, u32[]{:S(2)}) copy-start(f32[2368,128]{1,0:T(8,128)} %param.5) | copy-start | bytes 3637252
  93.0 2.9 %copy-start.4 = (f32[2368,128]{1,0:T(8,128)S(1)}, f32[2368,128]{1,0:T(8,128)}, u32[]{:S(2)}) copy-start(f32[2368,128]{1,0:T(8,128)} %get-tuple-element.9) | copy-start | bytes 3637252
  97.5 13.2 %collective-permute-start.7 = (bf16[2368,128]{1,0:T(8,128)(2,1)S(1)}, bf16[2368,128]{1,0:T(8,128)(2,1)S(1)}, u32[]{:S(2)}, u32[]{:S(2)}) collective-permute-start(bf16[2368,128]{1,0:T(8,128)(2,1)S(1)} %get-tuple-element.6), channel_id=1, source_target_pairs={{0,6},{2,0},{4,2},{6,4},{1,7},{3,1},{5,3},{7,5},{8,14},{10,8},{12,... | collective-permute-start | bytes 1818632 | tf_op jit(solution)/shard_map/ppermute | solution.py:99
  97.9 14.8 %collective-permute-start.9 = (bf16[2368,128]{1,0:T(8,128)(2,1)S(1)}, bf16[2368,128]{1,0:T(8,128)(2,1)S(1)}, u32[]{:S(2)}, u32[]{:S(2)}) collective-permute-start(bf16[2368,128]{1,0:T(8,128)(2,1)S(1)} %get-tuple-element.6), channel_id=1, source_target_pairs={{0,2},{2,4},{4,6},{6,0},{1,3},{3,5},{5,7},{7,1},{8,10},{10,12},{12... | collective-permute-start | bytes 1818632 | tf_op jit(solution)/shard_map/ppermute | solution.py:99
  98.9 17.0 %collective-permute-start.6 = (bf16[2368,128]{1,0:T(8,128)(2,1)S(1)}, bf16[2368,128]{1,0:T(8,128)(2,1)S(1)}, u32[]{:S(2)}, u32[]{:S(2)}) collective-permute-start(bf16[2368,128]{1,0:T(8,128)(2,1)S(1)} %get-tuple-element.6), channel_id=1, source_target_pairs={{0,1},{1,0},{2,3},{3,2},{4,5},{5,4},{6,7},{7,6},{8,9},{9,8},{10,11... | collective-permute-start | bytes 1818632 | tf_op jit(solution)/shard_map/ppermute | solution.py:109
  110.7 7.0 %collective-permute-start.11 = (bf16[1184,128]{1,0:T(8,128)(2,1)S(1)}, bf16[1184,128]{1,0:T(8,128)(2,1)S(1)}, u32[]{:S(2)}, u32[]{:S(2)}) collective-permute-start(bf16[1184,128]{1,0:T(8,128)(2,1)S(1)} %slice.48), channel_id=1, source_target_pairs={{0,6},{2,0},{4,2},{6,4},{1,7},{3,1},{5,3},{7,5},{8,14},{10,8},{12,... | collective-permute-start | bytes 909320 | tf_op jit(solution)/shard_map/ppermute | solution.py:99
  112.7 7.8 %collective-permute-start.13 = (bf16[1184,128]{1,0:T(8,128)(2,1)S(1)}, bf16[1184,128]{1,0:T(8,128)(2,1)S(1)}, u32[]{:S(2)}, u32[]{:S(2)}) collective-permute-start(bf16[1184,128]{1,0:T(8,128)(2,1)S(1)} %slice.49), channel_id=1, source_target_pairs={{0,2},{2,4},{4,6},{6,0},{1,3},{3,5},{5,7},{7,1},{8,10},{10,12},{12... | collective-permute-start | bytes 909320 | tf_op jit(solution)/shard_map/ppermute | solution.py:99
  112.8 10.9 %collective-permute-start.8 = (bf16[2368,128]{1,0:T(8,128)(2,1)S(1)}, bf16[2368,128]{1,0:T(8,128)(2,1)S(1)}, u32[]{:S(2)}, u32[]{:S(2)}) collective-permute-start(bf16[2368,128]{1,0:T(8,128)(2,1)S(1)} %collective-permute-done.7), channel_id=1, source_target_pairs={{0,1},{1,0},{2,3},{3,2},{4,5},{5,4},{6,7},{7,6},{8,9},{9,8},{10,11... | collective-permute-start | bytes 1818632 | tf_op jit(solution)/shard_map/ppermute | solution.py:109
  115.8 9.6 %collective-permute-start.10 = (bf16[2368,128]{1,0:T(8,128)(2,1)S(1)}, bf16[2368,128]{1,0:T(8,128)(2,1)S(1)}, u32[]{:S(2)}, u32[]{:S(2)}) collective-permute-start(bf16[2368,128]{1,0:T(8,128)(2,1)S(1)} %collective-permute-done.9), channel_id=1, source_target_pairs={{0,1},{1,0},{2,3},{3,2},{4,5},{5,4},{6,7},{7,6},{8,9},{9,8},{10,11... | collective-permute-start | bytes 1818632 | tf_op jit(solution)/shard_map/ppermute | solution.py:109
  117.6 9.4 %collective-permute-start.12 = (bf16[1184,128]{1,0:T(8,128)(2,1)S(1)}, bf16[1184,128]{1,0:T(8,128)(2,1)S(1)}, u32[]{:S(2)}, u32[]{:S(2)}) collective-permute-start(bf16[1184,128]{1,0:T(8,128)(2,1)S(1)} %collective-permute-done.11), channel_id=1, source_target_pairs={{0,1},{1,0},{2,3},{3,2},{4,5},{5,4},{6,7},{7,6},{8,9},{9,8},{10,11... | collective-permute-start | bytes 909320 | tf_op jit(solution)/shard_map/ppermute | solution.py:109
  120.5 8.0 %collective-permute-start.14 = (bf16[1184,128]{1,0:T(8,128)(2,1)S(1)}, bf16[1184,128]{1,0:T(8,128)(2,1)S(1)}, u32[]{:S(2)}, u32[]{:S(2)}) collective-permute-start(bf16[1184,128]{1,0:T(8,128)(2,1)S(1)} %collective-permute-done.13), channel_id=1, source_target_pairs={{0,1},{1,0},{2,3},{3,2},{4,5},{5,4},{6,7},{7,6},{8,9},{9,8},{10,11... | collective-permute-start | bytes 909320 | tf_op jit(solution)/shard_map/ppermute | solution.py:109

commit v9 on v5

--- a/solution.py
+++ b/solution.py
@@ -59,8 +59,26 @@
     y = lax.all_to_all(y.reshape(nz, padded // nz, cols), "z", 0, 0, tiled=False).sum(0)
     y = lax.all_to_all(jnp.broadcast_to(y[None], (nz,) + y.shape), "z", 0, 0, tiled=False)
     y = y.reshape(padded, cols)[:part]
+    if nx == 4 and part % 16 == 0:
+        return ring_gather_rows(y, "x", nx)
     y = lax.all_to_all(jnp.broadcast_to(y[None], (nx,) + y.shape), "x", 0, 0, tiled=False)
     return y.reshape(rows, cols)
+
+
+def ring_gather_rows(v, axis, n):
+    me = lax.axis_index(axis)
+    rows = v.shape[0]
+    half = rows // 2
+
+    def shift(a, s):
+        return lax.ppermute(a, axis, [(i, (i - s) % n) for i in range(n)])
+
+    plus, minus = shift(v, 1), shift(v, -1)
+    pieces = [(v, 0, 0), (plus, 1, 0), (minus, n - 1, 0), (shift(plus[:half], 1), 2, 0), (shift(minus[half:], -1), 2, half)]
+    out = jnp.zeros((n * rows,) + v.shape[1:], v.dtype)
+    for piece, s, row in pieces:
+        out = lax.dynamic_update_slice_in_dim(out, piece, ((me + s) % n) * rows + row, 0)
+    return out
 
 
 def tensor_sum(v, ny, ncore):

time: 125 us -> 126 us (level)
  blocking collectives: 51.6 us -> 39.1 us
  waiting for transfers between devices: 23.9 us -> 33.1 us
  starting transfers between devices: 28.6 us -> 33.6 us
  local copies, waits for them, and re-layouts: 14.1 us -> 11.3 us
  other arithmetic: 5.06 us -> 6.6 us
    all_to_all x1 -> x0, blocking collectives: 12.5 us -> none  [dp_sum(): lax.all_to_all(jnp.broadcast_to(y[None], (nz,) + y.shape), 'z', 0, 0, til...]
    ppermute x0 -> x4, waiting for transfers between devices: none -> 11 us  [shift(): return lax.ppermute(a, axis, [(i, (i - s) % n) for i in range(n)])]
    ppermute x0 -> x4, starting transfers between devices: none -> 3.89 us  [shift(): return lax.ppermute(a, axis, [(i, (i - s) % n) for i in range(n)])]
    unnamed x14 -> x6, local copies, waits for them, and re-layouts: 2.64 us -> 0.02 us
    reduce_sum x1, other arithmetic: 1.99 us -> 4 us  [group_squares(): row_sums = jnp.sum(values * values, axis=1)]
    all_to_all x1, waiting for transfers between devices: 11.7 us -> 9.93 us  [dp_sum(): lax.all_to_all(jnp.broadcast_to(y[None], (nz,) + y.shape), 'z', 0, 0, til...]
  transfers between devices with their start and end apart: 14 -> 18, of which waited for: 4 -> 7; matrix products, arithmetic and copies ran while one was open for 6% -> 6% of each run, Pallas kernels for 0% -> 0%
where the time goes in v9:
time: 126 us; the launch traced here: 125 us
  blocking collectives  39.1 us (31%)
  starting transfers between devices  33.6 us (27%)
  waiting for transfers between devices  33.1 us (26%)
  local copies, waits for them, and re-layouts  11.3 us (9%)
  other arithmetic  6.6 us (5%)
    all_to_all x1, blocking collectives, dp_sum(): y = lax.all_to_all(x.reshape(nx, part, cols), 'x', 0, 0, tiled=False).sum(0)  19.9 us
    all_to_all x1, blocking collectives, dp_sum(): lax.all_to_all(y.reshape(nz, padded // nz, cols), 'z', 0, 0, tiled=False)  19.2 us
    ppermute x5, starting transfers between devices, tensor_gather(): other = lax.ppermute(mine, 'core', swap)  11.8 us
    ppermute x4, waiting for transfers between devices, shift(): return lax.ppermute(a, axis, [(i, (i - s) % n) for i in range(n)])  11 us
    all_to_all x1, waiting for transfers between devices, dp_sum(): lax.all_to_all(jnp.broadcast_to(y[None], (nz,) + y.shape), 'z', 0, 0, til...  9.93 us
    ppermute x4, waiting for transfers between devices, shift(): return lax.ppermute(v, 'y', [(i, (i - s) % ny) for i in range(ny)])  8.51 us
    ppermute x1, starting transfers between devices, tensor_sum(): v = v + lax.ppermute(v, 'core', [(0, 1), (1, 0)])  6.92 us
    dynamic_update_slice x5, local copies, waits for them, and re-layouts, tensor_gather(): lax.dynamic_update_slice(out, other, (row, (2 * chip + 1 - core) * width))  4.05 us
  transfers between devices with their start and end apart: 18, of which 7 were waited for; matrix products, arithmetic and copies ran while one was open for 6% of the time, Pallas kernels for 0%

profile of v9, /device:TPU:1, one launch (start us, length us, event | category | flops | bytes accessed | tf_op | source)
XLA Modules:
  0.0 125.3 jit_solution(14994957312465169539)
XLA Ops:
  0.6 19.9 %all_to_all.15 = f32[4,592,128]{2,1,0:T(8,128)S(1)} all-to-all(f32[4,592,128]{2,1,0:T(8,128)} %bitcast.23), channel_id=1, replica_groups=mesh['z'=8,'x'=4,'y'=4,'core'=2] {'x'}, dimensions={0} | all-to-all | bytes 2424832 | tf_op jit(solution)/shard_map/all_to_all | solution.py:57
  20.6 0.1 reduce_sum.37
  20.7 19.2 %all_to_all.16 = f32[8,80,128]{2,1,0:T(8,128)S(1)} all-to-all(f32[8,80,128]{2,1,0:T(8,128)S(1)} %bitcast.21), channel_id=1, replica_groups=mesh['z'=8,'x'=4,'y'=4,'core'=2] {'z'}, dimensions={0} | all-to-all | bytes 655360 | tf_op jit(solution)/shard_map/all_to_all | solution.py:59
  39.9 0.7 broadcast_in_dim.41
  40.6 3.4 %all-to-all-start.2 = ((f32[8,80,128]{2,1,0:T(8,128)}), f32[8,80,128]{2,1,0:T(8,128)S(1)}, u32[]{:S(2)}, u32[]{:S(2)}) async-start(f32[8,80,128]{2,1,0:T(8,128)} %broadcast_in_dim.41), calls=%async_computation.2 | async-start | bytes 655360 | tf_op jit(solution)/shard_map/all_to_all | solution.py:60
  44.1 9.9 %all-to-all-done.2 = f32[8,80,128]{2,1,0:T(8,128)S(1)} async-done(((f32[8,80,128]{2,1,0:T(8,128)}), f32[8,80,128]{2,1,0:T(8,128)S(1)}, u32[]{:S(2)}, u32[]{:S(2)}) %all-to-all-start.2) | async-done | bytes 327712 | tf_op jit(solution)/shard_map/all_to_all | solution.py:60
  54.0 0.1 broadcast_in_dim.40
  54.2 1.1 collective-permute-start
  55.2 0.5 collective-permute-start.1
  55.9 4.0 %collective-permute-done = f32[592,128]{1,0:T(8,128)S(1)} collective-permute-done((f32[592,128]{1,0:T(8,128)S(1)}, f32[592,128]{1,0:T(8,128)S(1)}, u32[]{:S(2)}, u32[]{:S(2)}) %collective-permute-start) | collective-permute-done | bytes 303136 | tf_op jit(solution)/shard_map/ppermute | solution.py:74
  59.9 2.3 %collective-permute-start.2 = (f32[296,128]{1,0:T(8,128)S(1)}, f32[296,128]{1,0:T(8,128)S(1)}, u32[]{:S(2)}, u32[]{:S(2)}) collective-permute-start(f32[296,128]{1,0:T(8,128)S(1)} %slice.55), channel_id=1, source_target_pairs={{0,24},{8,0},{16,8},{24,16},{1,25},{9,1},{17,9},{25,17},{2,26},{10... | collective-permute-start | bytes 454664 | tf_op jit(solution)/shard_map/ppermute | solution.py:74
  62.2 0.1 collective-permute-start.3
  62.4 3.6 %collective-permute-done.2 = f32[296,128]{1,0:T(8,128)S(1)} collective-permute-done((f32[296,128]{1,0:T(8,128)S(1)}, f32[296,128]{1,0:T(8,128)S(1)}, u32[]{:S(2)}, u32[]{:S(2)}) %collective-permute-start.2) | collective-permute-done | bytes 151584 | tf_op jit(solution)/shard_map/ppermute | solution.py:74
  66.0 3.4 %collective-permute-done.3 = f32[296,128]{1,0:T(8,128)S(1)} collective-permute-done((f32[296,128]{1,0:T(8,128)S(1)}, f32[296,128]{1,0:T(8,128)S(1)}, u32[]{:S(2)}, u32[]{:S(2)}) %collective-permute-start.3) | collective-permute-done | bytes 151584 | tf_op jit(solution)/shard_map/ppermute | solution.py:74
  69.5 4.0 %multiply_reduce_fusion = (f32[2368]{0:T(1024)S(1)}, f32[2368,128]{1,0:T(8,128)}, f32[2368,128]{1,0:T(8,128)}, f32[2368,128]{1,0:T(8,128)}, f32[2368]{0:T(1024)S(1)}) fusion(f32[2368,128]{1,0:T(8,128)S(1)} %copy-done, f32[2368]{0:T(1024)S(1)} %fusion.1, f32[2368,128]{1,0:T(8,128)S(1)} %constant_dynamic-update-slice_fusion.8, f32[2368,128]{1,0:T(8,128)S(1)} %copy-done.2, ...), kind=kLoop, calls=%fused_computation.1 | loop fusion | flops 5451136 | bytes 8515328 | tf_op jit(solution)/shard_map/reduce_sum | solution.py:32
  73.5 0.1 convolution_bitcast_fusion.1
  73.6 0.2 convolution_bitcast_fusion
  73.8 0.1 pad_maximum_fusion
  74.0 6.9 %collective-permute-start.4 = (f32[8]{0:T(128)S(1)}, f32[8]{0:T(128)S(1)}, u32[]{:S(2)}, u32[]{:S(2)}) collective-permute-start(f32[8]{0:T(128)S(1)} %pad_maximum_fusion), channel_id=1, source_target_pairs={{0,1},{1,0},{2,3},{3,2},{4,5},{5,4},{6,7},{7,6},{8,9},{9,8},{10,11... | collective-permute-start | bytes 104 | tf_op jit(solution)/shard_map/ppermute | solution.py:86
  80.9 0.8 collective-permute-done.4
  81.7 0.1 fusion.11
  81.8 2.7 %collective-permute-start.5 = (f32[8]{0:T(128)S(1)}, f32[8]{0:T(128)S(1)}, u32[]{:S(2)}, u32[]{:S(2)}) collective-permute-start(f32[8]{0:T(128)S(1)} %fusion.11), channel_id=1, source_target_pairs={{0,6},{2,0},{4,2},{6,4},{1,7},{3,1},{5,3},{7,5},{8,14},{10,8},{12,... | collective-permute-start | bytes 104 | tf_op jit(solution)/shard_map/ppermute | solution.py:93
  84.5 0.3 collective-permute-start.6
  84.9 0.7 collective-permute-start.7
  85.6 2.8 %collective-permute-done.6 = f32[8]{0:T(128)S(1)} collective-permute-done((f32[8]{0:T(128)S(1)}, f32[8]{0:T(128)S(1)}, u32[]{:S(2)}, u32[]{:S(2)}) %collective-permute-start.6) | collective-permute-done | bytes 64 | tf_op jit(solution)/shard_map/ppermute | solution.py:93
  88.5 0.3 convolution_reduce_fusion
  88.8 2.8 %broadcast_in_dim.46 = bf16[2368,1024]{1,0:T(8,128)(2,1)} broadcast(bf16[]{:T(256)} %constant.130.clone.1), dimensions={} | broadcast | bytes 4849666 | tf_op jit(solution)/shard_map/broadcast_in_dim | solution.py:116
  91.7 1.6 %constant_dynamic-update-slice_fusion.7 = (bf16[2368,1024]{1,0:T(8,128)(2,1)}, bf16[2368,128]{1,0:T(8,128)(2,1)S(1)}, f32[2368,128]{1,0:T(8,128)}) fusion(bf16[2368,1024]{1,0:T(8,128)(2,1)} %broadcast_in_dim.46, s32[]{:T(128)S(6)} %select_n.137, f32[2368,128]{1,0:T(8,128)S(1)} %copy-done, f32[2368,128]{1,0:T(8,128)S(1)} %copy-done.1, ...), kind=kLoop, calls=%fused_computation.24 | loop fusion | flops 909312 | bytes 4859140 | tf_op jit(solution)/shard_map/dynamic_update_slice | solution.py:120
  93.3 0.4 collective-permute-start.9
  93.7 1.0 collective-permute-start.11
  94.7 2.6 %collective-permute-start.8 = (bf16[2368,128]{1,0:T(8,128)(2,1)S(1)}, bf16[2368,128]{1,0:T(8,128)(2,1)S(1)}, u32[]{:S(2)}, u32[]{:S(2)}) collective-permute-start(bf16[2368,128]{1,0:T(8,128)(2,1)S(1)} %get-tuple-element.6), channel_id=1, source_target_pairs={{0,1},{1,0},{2,3},{3,2},{4,5},{5,4},{6,7},{7,6},{8,9},{9,8},{10,11... | collective-permute-start | bytes 1818632 | tf_op jit(solution)/shard_map/ppermute | solution.py:118
  97.4 0.6 fusion.10
  98.0 8.5 %collective-permute-done.9 = bf16[2368,128]{1,0:T(8,128)(2,1)S(1)} collective-permute-done((bf16[2368,128]{1,0:T(8,128)(2,1)S(1)}, bf16[2368,128]{1,0:T(8,128)(2,1)S(1)}, u32[]{:S(2)}, u32[]{:S(2)}) %collective-permute-start.9) | collective-permute-done | bytes 606240 | tf_op jit(solution)/shard_map/ppermute | solution.py:108
  106.5 2.2 %collective-permute-start.13 = (bf16[1184,128]{1,0:T(8,128)(2,1)S(1)}, bf16[1184,128]{1,0:T(8,128)(2,1)S(1)}, u32[]{:S(2)}, u32[]{:S(2)}) collective-permute-start(bf16[1184,128]{1,0:T(8,128)(2,1)S(1)} %slice.59), channel_id=1, source_target_pairs={{0,6},{2,0},{4,2},{6,4},{1,7},{3,1},{5,3},{7,5},{8,14},{10,8},{12,... | collective-permute-start | bytes 909320 | tf_op jit(solution)/shard_map/ppermute | solution.py:108
  108.7 0.1 collective-permute-start.15
  108.8 3.0 %collective-permute-start.10 = (bf16[2368,128]{1,0:T(8,128)(2,1)S(1)}, bf16[2368,128]{1,0:T(8,128)(2,1)S(1)}, u32[]{:S(2)}, u32[]{:S(2)}) collective-permute-start(bf16[2368,128]{1,0:T(8,128)(2,1)S(1)} %collective-permute-done.9), channel_id=1, source_target_pairs={{0,1},{1,0},{2,3},{3,2},{4,5},{5,4},{6,7},{7,6},{8,9},{9,8},{10,11... | collective-permute-start | bytes 1818632 | tf_op jit(solution)/shard_map/ppermute | solution.py:118
  111.8 0.1 collective-permute-start.12
  111.9 0.9 constant_dynamic-update-slice_fusion.6
  112.8 0.9 constant_dynamic-update-slice_fusion.5
  113.6 2.8 %collective-permute-start.14 = (bf16[1184,128]{1,0:T(8,128)(2,1)S(1)}, bf16[1184,128]{1,0:T(8,128)(2,1)S(1)}, u32[]{:S(2)}, u32[]{:S(2)}) collective-permute-start(bf16[1184,128]{1,0:T(8,128)(2,1)S(1)} %collective-permute-done.13), channel_id=1, source_target_pairs={{0,1},{1,0},{2,3},{3,2},{4,5},{5,4},{6,7},{7,6},{8,9},{9,8},{10,11... | collective-permute-start | bytes 909320 | tf_op jit(solution)/shard_map/ppermute | solution.py:118
  116.5 3.2 %collective-permute-start.16 = (bf16[1184,128]{1,0:T(8,128)(2,1)S(1)}, bf16[1184,128]{1,0:T(8,128)(2,1)S(1)}, u32[]{:S(2)}, u32[]{:S(2)}) collective-permute-start(bf16[1184,128]{1,0:T(8,128)(2,1)S(1)} %collective-permute-done.15), channel_id=1, source_target_pairs={{0,1},{1,0},{2,3},{3,2},{4,5},{5,4},{6,7},{7,6},{8,9},{9,8},{10,11... | collective-permute-start | bytes 909320 | tf_op jit(solution)/shard_map/ppermute | solution.py:118
  119.7 0.9 constant_dynamic-update-slice_fusion.4
  120.6 0.9 constant_dynamic-update-slice_fusion.3
  121.4 0.9 constant_dynamic-update-slice_fusion.2
  122.3 0.7 constant_dynamic-update-slice_fusion.1
  123.0 0.7 constant_dynamic-update-slice_fusion
  123.8 0.7 constant_dynamic-update-slice_fusion.14
  124.5 0.7 constant_dynamic-update-slice_fusion.13
  (41 shorter events, 0.6 us)
Async XLA Ops:
  40.6 13.4 %all-to-all-start.2 = ((f32[8,80,128]{2,1,0:T(8,128)}), f32[8,80,128]{2,1,0:T(8,128)S(1)}, u32[]{:S(2)}, u32[]{:S(2)}) async-start(f32[8,80,128]{2,1,0:T(8,128)} %broadcast_in_dim.41), calls=%async_computation.2 | async-start | bytes 655360 | tf_op jit(solution)/shard_map/all_to_all | solution.py:60
  54.2 5.7 %collective-permute-start = (f32[592,128]{1,0:T(8,128)S(1)}, f32[592,128]{1,0:T(8,128)S(1)}, u32[]{:S(2)}, u32[]{:S(2)}) collective-permute-start(f32[592,128]{1,0:T(8,128)S(1)} %get-tuple-element.15), channel_id=1, source_target_pairs={{0,24},{8,0},{16,8},{24,16},{1,25},{9,1},{17,9},{25,17},{2,26},{10... | collective-permute-start | bytes 909320 | tf_op jit(solution)/shard_map/ppermute | solution.py:74
  55.2 7.0 %collective-permute-start.1 = (f32[592,128]{1,0:T(8,128)S(1)}, f32[592,128]{1,0:T(8,128)S(1)}, u32[]{:S(2)}, u32[]{:S(2)}) collective-permute-start(f32[592,128]{1,0:T(8,128)S(1)} %get-tuple-element.15), channel_id=1, source_target_pairs={{0,8},{8,16},{16,24},{24,0},{1,9},{9,17},{17,25},{25,1},{2,10},{10... | collective-permute-start | bytes 909320 | tf_op jit(solution)/shard_map/ppermute | solution.py:74
  55.9 13.5 %copy-start = (f32[2368,128]{1,0:T(8,128)S(1)}, f32[2368,128]{1,0:T(8,128)}, u32[]{:S(2)}) copy-start(f32[2368,128]{1,0:T(8,128)} %param.5) | copy-start | bytes 3637252
  55.9 13.5 %copy-start.2 = (f32[2368,128]{1,0:T(8,128)S(1)}, f32[2368,128]{1,0:T(8,128)}, u32[]{:S(2)}) copy-start(f32[2368,128]{1,0:T(8,128)} %param.6) | copy-start | bytes 3637252
  59.9 6.0 %collective-permute-start.2 = (f32[296,128]{1,0:T(8,128)S(1)}, f32[296,128]{1,0:T(8,128)S(1)}, u32[]{:S(2)}, u32[]{:S(2)}) collective-permute-start(f32[296,128]{1,0:T(8,128)S(1)} %slice.55), channel_id=1, source_target_pairs={{0,24},{8,0},{16,8},{24,16},{1,25},{9,1},{17,9},{25,17},{2,26},{10... | collective-permute-start | bytes 454664 | tf_op jit(solution)/shard_map/ppermute | solution.py:74
  62.2 7.2 %collective-permute-start.3 = (f32[296,128]{1,0:T(8,128)S(1)}, f32[296,128]{1,0:T(8,128)S(1)}, u32[]{:S(2)}, u32[]{:S(2)}) collective-permute-start(f32[296,128]{1,0:T(8,128)S(1)} %slice.56), channel_id=1, source_target_pairs={{0,8},{8,16},{16,24},{24,0},{1,9},{9,17},{17,25},{25,1},{2,10},{10... | collective-permute-start | bytes 454664 | tf_op jit(solution)/shard_map/ppermute | solution.py:74
  74.0 7.7 %collective-permute-start.4 = (f32[8]{0:T(128)S(1)}, f32[8]{0:T(128)S(1)}, u32[]{:S(2)}, u32[]{:S(2)}) collective-permute-start(f32[8]{0:T(128)S(1)} %pad_maximum_fusion), channel_id=1, source_target_pairs={{0,1},{1,0},{2,3},{3,2},{4,5},{5,4},{6,7},{7,6},{8,9},{9,8},{10,11... | collective-permute-start | bytes 104 | tf_op jit(solution)/shard_map/ppermute | solution.py:86
  81.8 3.8 %collective-permute-start.5 = (f32[8]{0:T(128)S(1)}, f32[8]{0:T(128)S(1)}, u32[]{:S(2)}, u32[]{:S(2)}) collective-permute-start(f32[8]{0:T(128)S(1)} %fusion.11), channel_id=1, source_target_pairs={{0,6},{2,0},{4,2},{6,4},{1,7},{3,1},{5,3},{7,5},{8,14},{10,8},{12,... | collective-permute-start | bytes 104 | tf_op jit(solution)/shard_map/ppermute | solution.py:93
  84.5 3.9 %collective-permute-start.6 = (f32[8]{0:T(128)S(1)}, f32[8]{0:T(128)S(1)}, u32[]{:S(2)}, u32[]{:S(2)}) collective-permute-start(f32[8]{0:T(128)S(1)} %fusion.11), channel_id=1, source_target_pairs={{0,4},{2,6},{4,0},{6,2},{1,5},{3,7},{5,1},{7,3},{8,12},{10,14},{12... | collective-permute-start | bytes 104 | tf_op jit(solution)/shard_map/ppermute | solution.py:93
  84.9 3.6 %collective-permute-start.7 = (f32[8]{0:T(128)S(1)}, f32[8]{0:T(128)S(1)}, u32[]{:S(2)}, u32[]{:S(2)}) collective-permute-start(f32[8]{0:T(128)S(1)} %fusion.11), channel_id=1, source_target_pairs={{0,2},{2,4},{4,6},{6,0},{1,3},{3,5},{5,7},{7,1},{8,10},{10,12},{12... | collective-permute-start | bytes 104 | tf_op jit(solution)/shard_map/ppermute | solution.py:93
  88.8 2.9 %copy-start.1 = (f32[2368,128]{1,0:T(8,128)S(1)}, f32[2368,128]{1,0:T(8,128)}, u32[]{:S(2)}) copy-start(f32[2368,128]{1,0:T(8,128)} %get-tuple-element.9) | copy-start | bytes 3637252
  93.3 13.2 %collective-permute-start.9 = (bf16[2368,128]{1,0:T(8,128)(2,1)S(1)}, bf16[2368,128]{1,0:T(8,128)(2,1)S(1)}, u32[]{:S(2)}, u32[]{:S(2)}) collective-permute-start(bf16[2368,128]{1,0:T(8,128)(2,1)S(1)} %get-tuple-element.6), channel_id=1, source_target_pairs={{0,6},{2,0},{4,2},{6,4},{1,7},{3,1},{5,3},{7,5},{8,14},{10,8},{12,... | collective-permute-start | bytes 1818632 | tf_op jit(solution)/shard_map/ppermute | solution.py:108
  93.7 15.0 %collective-permute-start.11 = (bf16[2368,128]{1,0:T(8,128)(2,1)S(1)}, bf16[2368,128]{1,0:T(8,128)(2,1)S(1)}, u32[]{:S(2)}, u32[]{:S(2)}) collective-permute-start(bf16[2368,128]{1,0:T(8,128)(2,1)S(1)} %get-tuple-element.6), channel_id=1, source_target_pairs={{0,2},{2,4},{4,6},{6,0},{1,3},{3,5},{5,7},{7,1},{8,10},{10,12},{12... | collective-permute-start | bytes 1818632 | tf_op jit(solution)/shard_map/ppermute | solution.py:108
  94.7 17.2 %collective-permute-start.8 = (bf16[2368,128]{1,0:T(8,128)(2,1)S(1)}, bf16[2368,128]{1,0:T(8,128)(2,1)S(1)}, u32[]{:S(2)}, u32[]{:S(2)}) collective-permute-start(bf16[2368,128]{1,0:T(8,128)(2,1)S(1)} %get-tuple-element.6), channel_id=1, source_target_pairs={{0,1},{1,0},{2,3},{3,2},{4,5},{5,4},{6,7},{7,6},{8,9},{9,8},{10,11... | collective-permute-start | bytes 1818632 | tf_op jit(solution)/shard_map/ppermute | solution.py:118
  106.5 7.1 %collective-permute-start.13 = (bf16[1184,128]{1,0:T(8,128)(2,1)S(1)}, bf16[1184,128]{1,0:T(8,128)(2,1)S(1)}, u32[]{:S(2)}, u32[]{:S(2)}) collective-permute-start(bf16[1184,128]{1,0:T(8,128)(2,1)S(1)} %slice.59), channel_id=1, source_target_pairs={{0,6},{2,0},{4,2},{6,4},{1,7},{3,1},{5,3},{7,5},{8,14},{10,8},{12,... | collective-permute-start | bytes 909320 | tf_op jit(solution)/shard_map/ppermute | solution.py:108
  108.7 7.8 %collective-permute-start.15 = (bf16[1184,128]{1,0:T(8,128)(2,1)S(1)}, bf16[1184,128]{1,0:T(8,128)(2,1)S(1)}, u32[]{:S(2)}, u32[]{:S(2)}) collective-permute-start(bf16[1184,128]{1,0:T(8,128)(2,1)S(1)} %slice.60), channel_id=1, source_target_pairs={{0,2},{2,4},{4,6},{6,0},{1,3},{3,5},{5,7},{7,1},{8,10},{10,12},{12... | collective-permute-start | bytes 909320 | tf_op jit(solution)/shard_map/ppermute | solution.py:108
  108.8 10.9 %collective-permute-start.10 = (bf16[2368,128]{1,0:T(8,128)(2,1)S(1)}, bf16[2368,128]{1,0:T(8,128)(2,1)S(1)}, u32[]{:S(2)}, u32[]{:S(2)}) collective-permute-start(bf16[2368,128]{1,0:T(8,128)(2,1)S(1)} %collective-permute-done.9), channel_id=1, source_target_pairs={{0,1},{1,0},{2,3},{3,2},{4,5},{5,4},{6,7},{7,6},{8,9},{9,8},{10,11... | collective-permute-start | bytes 1818632 | tf_op jit(solution)/shard_map/ppermute | solution.py:118
  111.8 9.6 %collective-permute-start.12 = (bf16[2368,128]{1,0:T(8,128)(2,1)S(1)}, bf16[2368,128]{1,0:T(8,128)(2,1)S(1)}, u32[]{:S(2)}, u32[]{:S(2)}) collective-permute-start(bf16[2368,128]{1,0:T(8,128)(2,1)S(1)} %collective-permute-done.11), channel_id=1, source_target_pairs={{0,1},{1,0},{2,3},{3,2},{4,5},{5,4},{6,7},{7,6},{8,9},{9,8},{10,11... | collective-permute-start | bytes 1818632 | tf_op jit(solution)/shard_map/ppermute | solution.py:118
  113.6 9.4 %collective-permute-start.14 = (bf16[1184,128]{1,0:T(8,128)(2,1)S(1)}, bf16[1184,128]{1,0:T(8,128)(2,1)S(1)}, u32[]{:S(2)}, u32[]{:S(2)}) collective-permute-start(bf16[1184,128]{1,0:T(8,128)(2,1)S(1)} %collective-permute-done.13), channel_id=1, source_target_pairs={{0,1},{1,0},{2,3},{3,2},{4,5},{5,4},{6,7},{7,6},{8,9},{9,8},{10,11... | collective-permute-start | bytes 909320 | tf_op jit(solution)/shard_map/ppermute | solution.py:118
  116.5 8.0 %collective-permute-start.16 = (bf16[1184,128]{1,0:T(8,128)(2,1)S(1)}, bf16[1184,128]{1,0:T(8,128)(2,1)S(1)}, u32[]{:S(2)}, u32[]{:S(2)}) collective-permute-start(bf16[1184,128]{1,0:T(8,128)(2,1)S(1)} %collective-permute-done.15), channel_id=1, source_target_pairs={{0,1},{1,0},{2,3},{3,2},{4,5},{5,4},{6,7},{7,6},{8,9},{9,8},{10,11... | collective-permute-start | bytes 909320 | tf_op jit(solution)/shard_map/ppermute | solution.py:118

commit v10 on v5

--- a/solution.py
+++ b/solution.py
@@ -95,7 +95,8 @@
         pieces = [(b, 0, 0), (plus, 1, 0), (minus, 3, 0), (shift(plus[:half], 1), 2, 0), (shift(minus[half:], -1), 2, half)]
     else:
         pieces = [(b, 0, 0)] + [(shift(b, s), s, 0) for s in range(1, ny)]
-    out = jnp.zeros((rows, 2 * ny * width), b.dtype)
+    first = pieces[1][0]
+    out = jnp.tile(first, (1, 2 * ny))
     for mine, s, row in pieces:
         other = lax.ppermute(mine, "core", swap)
         chip = (y + s) % ny

time: 125 us -> 127 us (1.016)
    another operation x0 -> x1, local copies, waits for them, and re-layouts: none -> 6.28 us  [tensor_gather(): out = jnp.tile(first, (1, 2 * ny))]
    dynamic_update_slice x5, local copies, waits for them, and re-layouts: 4.05 us -> 0.83 us  [tensor_gather(): lax.dynamic_update_slice(out, other, (row, (2 * chip + 1 - core) * width))]
    broadcast_in_dim x1 -> x0, local copies, waits for them, and re-layouts: 2.85 us -> none  [tensor_gather(): out = jnp.zeros((rows, 2 * ny * width), b.dtype)]
    unnamed x14 -> x13, local copies, waits for them, and re-layouts: 2.64 us -> 5.45 us
    dynamic_update_slice x4 -> x5, local copies, waits for them, and re-layouts: 3.19 us -> 0.83 us  [tensor_gather(): out = lax.dynamic_update_slice(out, mine, (row, (2 * chip + core) * width))]
    dynamic_update_slice x1 -> x0, other arithmetic: 1.6 us -> none  [tensor_gather(): out = lax.dynamic_update_slice(out, mine, (row, (2 * chip + core) * width))]
    convert_element_type x0 -> x1, other arithmetic: none -> 1.41 us  [shards(): copies = tensor_gather(weights_new.astype(jnp.bfloat16), ny)]
  transfers between devices with their start and end apart: 14 -> 14, of which waited for: 4 -> 5; matrix products, arithmetic and copies ran while one was open for 6% -> 8% of each run, Pallas kernels for 0% -> 0%
where the time goes in v10:
time: 127 us; the launch traced here: 126 us
  blocking collectives  51.6 us (41%)
  starting transfers between devices  29.8 us (23%)
  waiting for transfers between devices  24.1 us (19%)
  local copies, waits for them, and re-layouts  14.7 us (12%)
  other arithmetic  4.24 us (3%)
    all_to_all x1, blocking collectives, dp_sum(): y = lax.all_to_all(x.reshape(nx, part, cols), 'x', 0, 0, tiled=False).sum(0)  19.9 us
    all_to_all x1, blocking collectives, dp_sum(): lax.all_to_all(y.reshape(nz, padded // nz, cols), 'z', 0, 0, tiled=False)  19.2 us
    ppermute x5, starting transfers between devices, tensor_gather(): other = lax.ppermute(mine, 'core', swap)  12.9 us
    all_to_all x1, blocking collectives, dp_sum(): lax.all_to_all(jnp.broadcast_to(y[None], (nz,) + y.shape), 'z', 0, 0, til...  12.5 us
    all_to_all x1, waiting for transfers between devices, dp_sum(): lax.all_to_all(jnp.broadcast_to(y[None], (nx,) + y.shape), 'x', 0, 0, til...  11.7 us
    ppermute x4, waiting for transfers between devices, shift(): return lax.ppermute(v, 'y', [(i, (i - s) % ny) for i in range(ny)])  8.51 us
    another operation x1, local copies, waits for them, and re-layouts, tensor_gather(): out = jnp.tile(first, (1, 2 * ny))  6.28 us
    ppermute x1, starting transfers between devices, tensor_sum(): v = v + lax.ppermute(v, 'core', [(0, 1), (1, 0)])  5.88 us
  transfers between devices with their start and end apart: 14, of which 5 were waited for; matrix products, arithmetic and copies ran while one was open for 8% of the time, Pallas kernels for 0%

profile of v10, /device:TPU:1, one launch (start us, length us, event | category | flops | bytes accessed | tf_op | source)
XLA Modules:
  0.0 126.1 jit_solution(7745285953261968061)
XLA Ops:
  0.6 19.9 %all_to_all.20 = f32[4,592,128]{2,1,0:T(8,128)S(1)} all-to-all(f32[4,592,128]{2,1,0:T(8,128)} %bitcast.33), channel_id=1, replica_groups=mesh['z'=8,'x'=4,'y'=4,'core'=2] {'x'}, dimensions={0} | all-to-all | bytes 2424832 | tf_op jit(solution)/shard_map/all_to_all | solution.py:57
  20.6 0.1 reduce_sum.37
  20.7 19.2 %all_to_all.21 = f32[8,80,128]{2,1,0:T(8,128)S(1)} all-to-all(f32[8,80,128]{2,1,0:T(8,128)S(1)} %bitcast.31), channel_id=1, replica_groups=mesh['z'=8,'x'=4,'y'=4,'core'=2] {'z'}, dimensions={0} | all-to-all | bytes 655360 | tf_op jit(solution)/shard_map/all_to_all | solution.py:59
  39.9 12.5 %all_to_all.22 = f32[8,80,128]{2,1,0:T(8,128)S(1)} all-to-all(f32[8,80,128]{2,1,0:T(8,128)S(1)} %broadcast_in_dim.40), channel_id=1, replica_groups=mesh['z'=8,'x'=4,'y'=4,'core'=2] {'z'}, dimensions={0} | all-to-all | bytes 655360 | tf_op jit(solution)/shard_map/all_to_all | solution.py:60
  52.5 1.1 broadcast_in_dim.41
  53.6 3.5 %all-to-all-start.3 = ((f32[4,592,128]{2,1,0:T(8,128)}), f32[4,592,128]{2,1,0:T(8,128)S(1)}, u32[]{:S(2)}, u32[]{:S(2)}) async-start(f32[4,592,128]{2,1,0:T(8,128)} %broadcast_in_dim.41), calls=%async_computation.3 | async-start | bytes 2424832 | tf_op jit(solution)/shard_map/all_to_all | solution.py:62
  57.3 11.7 %all-to-all-done.3 = f32[4,592,128]{2,1,0:T(8,128)S(1)} async-done(((f32[4,592,128]{2,1,0:T(8,128)}), f32[4,592,128]{2,1,0:T(8,128)S(1)}, u32[]{:S(2)}, u32[]{:S(2)}) %all-to-all-start.3) | async-done | bytes 1212448 | tf_op jit(solution)/shard_map/all_to_all | solution.py:62
  69.0 0.2 broadcast_multiply_fusion
  69.2 1.1 copy-done.5
  70.3 0.4 bitcast_add_fusion
  70.7 0.9 copy-done.3
  71.6 1.3 %multiply_reduce_fusion = (f32[2368]{0:T(1024)S(1)}, f32[2368,128]{1,0:T(8,128)S(1)}, f32[2368]{0:T(1024)S(1)}) fusion(f32[2368,128]{1,0:T(8,128)S(1)} %copy-done.3, f32[2368]{0:T(1024)S(1)} %fusion.1, f32[2368,128]{1,0:T(8,128)S(1)} %get-tuple-element.16, f32[2368,128]{1,0:T(8,128)S(1)} %get-tuple-element.17), kind=kLoop, calls=%fused_computation.4 | loop fusion | flops 3026304 | bytes 4878080 | tf_op jit(solution)/shard_map/reduce_sum | solution.py:32
  72.9 0.1 convolution_bitcast_fusion
  73.0 0.2 convolution_bitcast_fusion.1
  73.2 0.1 pad_maximum_fusion
  73.4 5.9 %collective-permute-start = (f32[8]{0:T(128)S(1)}, f32[8]{0:T(128)S(1)}, u32[]{:S(2)}, u32[]{:S(2)}) collective-permute-start(f32[8]{0:T(128)S(1)} %pad_maximum_fusion), channel_id=1, source_target_pairs={{0,1},{1,0},{2,3},{3,2},{4,5},{5,4},{6,7},{7,6},{8,9},{9,8},{10,11... | collective-permute-start | bytes 104 | tf_op jit(solution)/shard_map/ppermute | solution.py:68
  79.2 0.8 collective-permute-done
  80.1 2.7 %collective-permute-start.1 = (f32[8]{0:T(128)S(1)}, f32[8]{0:T(128)S(1)}, u32[]{:S(2)}, u32[]{:S(2)}) collective-permute-start(f32[8]{0:T(128)S(1)} %fusion.11), channel_id=1, source_target_pairs={{0,6},{2,0},{4,2},{6,4},{1,7},{3,1},{5,3},{7,5},{8,14},{10,8},{12,... | collective-permute-start | bytes 104 | tf_op jit(solution)/shard_map/ppermute | solution.py:75
  82.9 0.3 collective-permute-start.2
  83.2 0.7 collective-permute-start.3
  84.0 2.8 %collective-permute-done.2 = f32[8]{0:T(128)S(1)} collective-permute-done((f32[8]{0:T(128)S(1)}, f32[8]{0:T(128)S(1)}, u32[]{:S(2)}, u32[]{:S(2)}) %collective-permute-start.2) | collective-permute-done | bytes 64 | tf_op jit(solution)/shard_map/ppermute | solution.py:75
  86.9 0.3 convolution_reduce_fusion
  87.2 1.4 %fusion.3 = (bf16[2368,128]{1,0:T(8,128)(2,1)S(1)}, f32[2368,128]{1,0:T(8,128)}) fusion(f32[2368,128]{1,0:T(8,128)S(1)} %copy-done.3, f32[2368,128]{1,0:T(8,128)S(1)} %get-tuple-element.8, f32[2368]{0:T(1024)S(1)} %broadcast_multiply_fusion.1), kind=kLoop, calls=%fused_computation.34 | loop fusion | flops 909312 | bytes 4252928 | tf_op jit(solution)/shard_map/convert_element_type | solution.py:120
  88.6 0.4 collective-permute-start.4
  89.0 1.0 collective-permute-start.7
  90.1 2.6 %collective-permute-start.5 = (bf16[2368,128]{1,0:T(8,128)(2,1)S(1)}, bf16[2368,128]{1,0:T(8,128)(2,1)S(1)}, u32[]{:S(2)}, u32[]{:S(2)}) collective-permute-start(bf16[2368,128]{1,0:T(8,128)(2,1)S(1)} %get-tuple-element.5), channel_id=1, source_target_pairs={{0,1},{1,0},{2,3},{3,2},{4,5},{5,4},{6,7},{7,6},{8,9},{9,8},{10,11... | collective-permute-start | bytes 1818632 | tf_op jit(solution)/shard_map/ppermute | solution.py:101
  92.7 0.6 fusion.10
  93.3 8.5 %collective-permute-done.4 = bf16[2368,128]{1,0:T(8,128)(2,1)S(1)} collective-permute-done((bf16[2368,128]{1,0:T(8,128)(2,1)S(1)}, bf16[2368,128]{1,0:T(8,128)(2,1)S(1)}, u32[]{:S(2)}, u32[]{:S(2)}) %collective-permute-start.4) | collective-permute-done | bytes 606240 | tf_op jit(solution)/shard_map/ppermute | solution.py:90
  101.8 6.3 %tile.4 = bf16[2368,8,128]{2,1,0:T(8,128)(2,1)S(1)} broadcast(bf16[2368,128]{1,0:T(8,128)(2,1)S(1)} %collective-permute-done.4), dimensions={0,2} | broadcast | bytes 5455872 | tf_op jit(solution)/shard_map/tile | solution.py:99
  108.1 1.3 copy.11
  109.3 2.2 %collective-permute-start.9 = (bf16[1184,128]{1,0:T(8,128)(2,1)S(1)}, bf16[1184,128]{1,0:T(8,128)(2,1)S(1)}, u32[]{:S(2)}, u32[]{:S(2)}) collective-permute-start(bf16[1184,128]{1,0:T(8,128)(2,1)S(1)} %slice.49), channel_id=1, source_target_pairs={{0,6},{2,0},{4,2},{6,4},{1,7},{3,1},{5,3},{7,5},{8,14},{10,8},{12,... | collective-permute-start | bytes 909320 | tf_op jit(solution)/shard_map/ppermute | solution.py:90
  111.6 0.1 collective-permute-start.11
  111.7 3.0 %collective-permute-start.6 = (bf16[2368,128]{1,0:T(8,128)(2,1)S(1)}, bf16[2368,128]{1,0:T(8,128)(2,1)S(1)}, u32[]{:S(2)}, u32[]{:S(2)}) collective-permute-start(bf16[2368,128]{1,0:T(8,128)(2,1)S(1)} %collective-permute-done.4), channel_id=1, source_target_pairs={{0,1},{1,0},{2,3},{3,2},{4,5},{5,4},{6,7},{7,6},{8,9},{9,8},{10,11... | collective-permute-start | bytes 1818632 | tf_op jit(solution)/shard_map/ppermute | solution.py:101
  114.7 0.1 collective-permute-start.8
  114.8 0.2 constant_dynamic-update-slice_fusion.7
  115.0 0.2 constant_dynamic-update-slice_fusion.6
  115.2 0.2 constant_dynamic-update-slice_fusion.5
  115.4 3.9 %collective-permute-start.10 = (bf16[1184,128]{1,0:T(8,128)(2,1)S(1)}, bf16[1184,128]{1,0:T(8,128)(2,1)S(1)}, u32[]{:S(2)}, u32[]{:S(2)}) collective-permute-start(bf16[1184,128]{1,0:T(8,128)(2,1)S(1)} %collective-permute-done.9), channel_id=1, source_target_pairs={{0,1},{1,0},{2,3},{3,2},{4,5},{5,4},{6,7},{7,6},{8,9},{9,8},{10,11... | collective-permute-start | bytes 909320 | tf_op jit(solution)/shard_map/ppermute | solution.py:101
  119.3 3.2 %collective-permute-start.12 = (bf16[1184,128]{1,0:T(8,128)(2,1)S(1)}, bf16[1184,128]{1,0:T(8,128)(2,1)S(1)}, u32[]{:S(2)}, u32[]{:S(2)}) collective-permute-start(bf16[1184,128]{1,0:T(8,128)(2,1)S(1)} %collective-permute-done.11), channel_id=1, source_target_pairs={{0,1},{1,0},{2,3},{3,2},{4,5},{5,4},{6,7},{7,6},{8,9},{9,8},{10,11... | collective-permute-start | bytes 909320 | tf_op jit(solution)/shard_map/ppermute | solution.py:101
  122.6 0.2 constant_dynamic-update-slice_fusion.4
  122.8 0.2 constant_dynamic-update-slice_fusion.3
  123.0 0.2 constant_dynamic-update-slice_fusion.2
  123.3 0.1 constant_dynamic-update-slice_fusion.1
  123.4 0.1 constant_dynamic-update-slice_fusion
  123.5 0.1 constant_dynamic-update-slice_fusion.9
  123.6 0.2 collective-permute-done.12
  123.8 0.1 constant_dynamic-update-slice_fusion.8
  123.9 2.2 %copy-done.2 = bf16[2368,1024]{1,0:T(8,128)(2,1)} copy-done((bf16[2368,1024]{1,0:T(8,128)(2,1)}, bf16[2368,1024]{1,0:T(8,128)(2,1)S(1)}, u32[]{:S(2)}) %copy-start.2) | copy-done | bytes 4849688
  (38 shorter events, 0.5 us)
Async XLA Ops:
  53.6 15.5 %all-to-all-start.3 = ((f32[4,592,128]{2,1,0:T(8,128)}), f32[4,592,128]{2,1,0:T(8,128)S(1)}, u32[]{:S(2)}, u32[]{:S(2)}) async-start(f32[4,592,128]{2,1,0:T(8,128)} %broadcast_in_dim.41), calls=%async_computation.3 | async-start | bytes 2424832 | tf_op jit(solution)/shard_map/all_to_all | solution.py:62
  57.3 12.0 %copy-start.4 = (f32[2368,128]{1,0:T(8,128)S(1)}, f32[2368,128]{1,0:T(8,128)}, u32[]{:S(2)}) copy-start(f32[2368,128]{1,0:T(8,128)} %param.7) | copy-start | bytes 3637252
  69.0 1.3 %copy-start.5 = (f32[2368,128]{1,0:T(8,128)S(1)}, f32[2368,128]{1,0:T(8,128)}, u32[]{:S(2)}) copy-start(f32[2368,128]{1,0:T(8,128)} %param.6) | copy-start | bytes 3637252
  70.3 1.3 %copy-start.3 = (f32[2368,128]{1,0:T(8,128)S(1)}, f32[2368,128]{1,0:T(8,128)}, u32[]{:S(2)}) copy-start(f32[2368,128]{1,0:T(8,128)} %param.5) | copy-start | bytes 3637252
  70.7 2.2 %copy-start = (f32[2368,128]{1,0:T(8,128)}, f32[2368,128]{1,0:T(8,128)S(1)}, u32[]{:S(2)}) copy-start(f32[2368,128]{1,0:T(8,128)S(1)} %get-tuple-element.16) | copy-start | bytes 3637252
  70.7 2.2 %copy-start.1 = (f32[2368,128]{1,0:T(8,128)}, f32[2368,128]{1,0:T(8,128)S(1)}, u32[]{:S(2)}) copy-start(f32[2368,128]{1,0:T(8,128)S(1)} %get-tuple-element.17) | copy-start | bytes 3637252
  73.4 6.7 %collective-permute-start = (f32[8]{0:T(128)S(1)}, f32[8]{0:T(128)S(1)}, u32[]{:S(2)}, u32[]{:S(2)}) collective-permute-start(f32[8]{0:T(128)S(1)} %pad_maximum_fusion), channel_id=1, source_target_pairs={{0,1},{1,0},{2,3},{3,2},{4,5},{5,4},{6,7},{7,6},{8,9},{9,8},{10,11... | collective-permute-start | bytes 104 | tf_op jit(solution)/shard_map/ppermute | solution.py:68
  80.1 3.8 %collective-permute-start.1 = (f32[8]{0:T(128)S(1)}, f32[8]{0:T(128)S(1)}, u32[]{:S(2)}, u32[]{:S(2)}) collective-permute-start(f32[8]{0:T(128)S(1)} %fusion.11), channel_id=1, source_target_pairs={{0,6},{2,0},{4,2},{6,4},{1,7},{3,1},{5,3},{7,5},{8,14},{10,8},{12,... | collective-permute-start | bytes 104 | tf_op jit(solution)/shard_map/ppermute | solution.py:75
  82.9 3.9 %collective-permute-start.2 = (f32[8]{0:T(128)S(1)}, f32[8]{0:T(128)S(1)}, u32[]{:S(2)}, u32[]{:S(2)}) collective-permute-start(f32[8]{0:T(128)S(1)} %fusion.11), channel_id=1, source_target_pairs={{0,4},{2,6},{4,0},{6,2},{1,5},{3,7},{5,1},{7,3},{8,12},{10,14},{12... | collective-permute-start | bytes 104 | tf_op jit(solution)/shard_map/ppermute | solution.py:75
  83.2 3.6 %collective-permute-start.3 = (f32[8]{0:T(128)S(1)}, f32[8]{0:T(128)S(1)}, u32[]{:S(2)}, u32[]{:S(2)}) collective-permute-start(f32[8]{0:T(128)S(1)} %fusion.11), channel_id=1, source_target_pairs={{0,2},{2,4},{4,6},{6,0},{1,3},{3,5},{5,7},{7,1},{8,10},{10,12},{12... | collective-permute-start | bytes 104 | tf_op jit(solution)/shard_map/ppermute | solution.py:75
  88.6 13.2 %collective-permute-start.4 = (bf16[2368,128]{1,0:T(8,128)(2,1)S(1)}, bf16[2368,128]{1,0:T(8,128)(2,1)S(1)}, u32[]{:S(2)}, u32[]{:S(2)}) collective-permute-start(bf16[2368,128]{1,0:T(8,128)(2,1)S(1)} %get-tuple-element.5), channel_id=1, source_target_pairs={{0,6},{2,0},{4,2},{6,4},{1,7},{3,1},{5,3},{7,5},{8,14},{10,8},{12,... | collective-permute-start | bytes 1818632 | tf_op jit(solution)/shard_map/ppermute | solution.py:90
  89.0 22.5 %collective-permute-start.7 = (bf16[2368,128]{1,0:T(8,128)(2,1)S(1)}, bf16[2368,128]{1,0:T(8,128)(2,1)S(1)}, u32[]{:S(2)}, u32[]{:S(2)}) collective-permute-start(bf16[2368,128]{1,0:T(8,128)(2,1)S(1)} %get-tuple-element.5), channel_id=1, source_target_pairs={{0,2},{2,4},{4,6},{6,0},{1,3},{3,5},{5,7},{7,1},{8,10},{10,12},{12... | collective-permute-start | bytes 1818632 | tf_op jit(solution)/shard_map/ppermute | solution.py:90
  90.1 24.9 %collective-permute-start.5 = (bf16[2368,128]{1,0:T(8,128)(2,1)S(1)}, bf16[2368,128]{1,0:T(8,128)(2,1)S(1)}, u32[]{:S(2)}, u32[]{:S(2)}) collective-permute-start(bf16[2368,128]{1,0:T(8,128)(2,1)S(1)} %get-tuple-element.5), channel_id=1, source_target_pairs={{0,1},{1,0},{2,3},{3,2},{4,5},{5,4},{6,7},{7,6},{8,9},{9,8},{10,11... | collective-permute-start | bytes 1818632 | tf_op jit(solution)/shard_map/ppermute | solution.py:101
  109.3 6.1 %collective-permute-start.9 = (bf16[1184,128]{1,0:T(8,128)(2,1)S(1)}, bf16[1184,128]{1,0:T(8,128)(2,1)S(1)}, u32[]{:S(2)}, u32[]{:S(2)}) collective-permute-start(bf16[1184,128]{1,0:T(8,128)(2,1)S(1)} %slice.49), channel_id=1, source_target_pairs={{0,6},{2,0},{4,2},{6,4},{1,7},{3,1},{5,3},{7,5},{8,14},{10,8},{12,... | collective-permute-start | bytes 909320 | tf_op jit(solution)/shard_map/ppermute | solution.py:90
  111.6 7.8 %collective-permute-start.11 = (bf16[1184,128]{1,0:T(8,128)(2,1)S(1)}, bf16[1184,128]{1,0:T(8,128)(2,1)S(1)}, u32[]{:S(2)}, u32[]{:S(2)}) collective-permute-start(bf16[1184,128]{1,0:T(8,128)(2,1)S(1)} %slice.50), channel_id=1, source_target_pairs={{0,2},{2,4},{4,6},{6,0},{1,3},{3,5},{5,7},{7,1},{8,10},{10,12},{12... | collective-permute-start | bytes 909320 | tf_op jit(solution)/shard_map/ppermute | solution.py:90
  111.7 10.9 %collective-permute-start.6 = (bf16[2368,128]{1,0:T(8,128)(2,1)S(1)}, bf16[2368,128]{1,0:T(8,128)(2,1)S(1)}, u32[]{:S(2)}, u32[]{:S(2)}) collective-permute-start(bf16[2368,128]{1,0:T(8,128)(2,1)S(1)} %collective-permute-done.4), channel_id=1, source_target_pairs={{0,1},{1,0},{2,3},{3,2},{4,5},{5,4},{6,7},{7,6},{8,9},{9,8},{10,11... | collective-permute-start | bytes 1818632 | tf_op jit(solution)/shard_map/ppermute | solution.py:101
  114.7 8.4 %collective-permute-start.8 = (bf16[2368,128]{1,0:T(8,128)(2,1)S(1)}, bf16[2368,128]{1,0:T(8,128)(2,1)S(1)}, u32[]{:S(2)}, u32[]{:S(2)}) collective-permute-start(bf16[2368,128]{1,0:T(8,128)(2,1)S(1)} %collective-permute-done.7), channel_id=1, source_target_pairs={{0,1},{1,0},{2,3},{3,2},{4,5},{5,4},{6,7},{7,6},{8,9},{9,8},{10,11... | collective-permute-start | bytes 1818632 | tf_op jit(solution)/shard_map/ppermute | solution.py:101
  115.4 7.9 %collective-permute-start.10 = (bf16[1184,128]{1,0:T(8,128)(2,1)S(1)}, bf16[1184,128]{1,0:T(8,128)(2,1)S(1)}, u32[]{:S(2)}, u32[]{:S(2)}) collective-permute-start(bf16[1184,128]{1,0:T(8,128)(2,1)S(1)} %collective-permute-done.9), channel_id=1, source_target_pairs={{0,1},{1,0},{2,3},{3,2},{4,5},{5,4},{6,7},{7,6},{8,9},{9,8},{10,11... | collective-permute-start | bytes 909320 | tf_op jit(solution)/shard_map/ppermute | solution.py:101
  119.3 4.5 %collective-permute-start.12 = (bf16[1184,128]{1,0:T(8,128)(2,1)S(1)}, bf16[1184,128]{1,0:T(8,128)(2,1)S(1)}, u32[]{:S(2)}, u32[]{:S(2)}) collective-permute-start(bf16[1184,128]{1,0:T(8,128)(2,1)S(1)} %collective-permute-done.11), channel_id=1, source_target_pairs={{0,1},{1,0},{2,3},{3,2},{4,5},{5,4},{6,7},{7,6},{8,9},{9,8},{10,11... | collective-permute-start | bytes 909320 | tf_op jit(solution)/shard_map/ppermute | solution.py:101
  123.9 2.2 %copy-start.2 = (bf16[2368,1024]{1,0:T(8,128)(2,1)}, bf16[2368,1024]{1,0:T(8,128)(2,1)S(1)}, u32[]{:S(2)}) copy-start(bf16[2368,1024]{1,0:T(8,128)(2,1)S(1)} %constant_dynamic-update-slice_fusion.8) | copy-start | bytes 14548996

commit v11 on v5

--- a/solution.py
+++ b/solution.py
@@ -95,9 +95,9 @@
         pieces = [(b, 0, 0), (plus, 1, 0), (minus, 3, 0), (shift(plus[:half], 1), 2, 0), (shift(minus[half:], -1), 2, half)]
     else:
         pieces = [(b, 0, 0)] + [(shift(b, s), s, 0) for s in range(1, ny)]
-    out = jnp.zeros((rows, 2 * ny * width), b.dtype)
-    for mine, s, row in pieces:
-        other = lax.ppermute(mine, "core", swap)
+    others = [lax.ppermute(mine, "core", swap) for mine, _, _ in pieces]
+    out = jnp.tile(others[0], (1, 2 * ny))
+    for (mine, s, row), other in zip(pieces, others):
         chip = (y + s) % ny
         out = lax.dynamic_update_slice(out, mine, (row, (2 * chip + core) * width))
         out = lax.dynamic_update_slice(out, other, (row, (2 * chip + 1 - core) * width))

time: 125 us -> 122 us (0.976)
  starting transfers between devices: 28.6 us -> 23.8 us
  waiting for transfers between devices: 23.9 us -> 26 us
    another operation x0 -> x1, local copies, waits for them, and re-layouts: none -> 6.28 us  [tensor_gather(): out = jnp.tile(others[0], (1, 2 * ny))]
    ppermute x5, starting transfers between devices: 11.8 us -> 7.38 us  [tensor_gather(): others = [lax.ppermute(mine, 'core', swap) for mine, _, _ in pieces]]
    dynamic_update_slice x5, local copies, waits for them, and re-layouts: 4.05 us -> 0.82 us  [tensor_gather(): lax.dynamic_update_slice(out, other, (row, (2 * chip + 1 - core) * width))]
    broadcast_in_dim x1 -> x0, local copies, waits for them, and re-layouts: 2.85 us -> none  [tensor_gather(): out = jnp.zeros((rows, 2 * ny * width), b.dtype)]
    unnamed x14 -> x13, local copies, waits for them, and re-layouts: 2.64 us -> 5.45 us
    dynamic_update_slice x4 -> x5, local copies, waits for them, and re-layouts: 3.19 us -> 0.83 us  [tensor_gather(): out = lax.dynamic_update_slice(out, mine, (row, (2 * chip + core) * width))]
    ppermute x4, waiting for transfers between devices: 8.51 us -> 10.4 us  [shift(): return lax.ppermute(v, 'y', [(i, (i - s) % ny) for i in range(ny)])]
    dynamic_update_slice x1 -> x0, other arithmetic: 1.6 us -> none  [tensor_gather(): out = lax.dynamic_update_slice(out, mine, (row, (2 * chip + core) * width))]
  transfers between devices with their start and end apart: 14 -> 14, of which waited for: 4 -> 7; matrix products, arithmetic and copies ran while one was open for 6% -> 8% of each run, Pallas kernels for 0% -> 0%
where the time goes in v11:
time: 122 us
  blocking collectives  51.6 us (42%)
  waiting for transfers between devices  26 us (21%)
  starting transfers between devices  23.8 us (20%)
  local copies, waits for them, and re-layouts  14.7 us (12%)
  other arithmetic  4.24 us (3%)
    all_to_all x1, blocking collectives, dp_sum(): y = lax.all_to_all(x.reshape(nx, part, cols), 'x', 0, 0, tiled=False).sum(0)  19.9 us
    all_to_all x1, blocking collectives, dp_sum(): lax.all_to_all(y.reshape(nz, padded // nz, cols), 'z', 0, 0, tiled=False)  19.2 us
    all_to_all x1, blocking collectives, dp_sum(): lax.all_to_all(jnp.broadcast_to(y[None], (nz,) + y.shape), 'z', 0, 0, til...  12.5 us
    all_to_all x1, waiting for transfers between devices, dp_sum(): lax.all_to_all(jnp.broadcast_to(y[None], (nx,) + y.shape), 'x', 0, 0, til...  11.7 us
    ppermute x4, waiting for transfers between devices, shift(): return lax.ppermute(v, 'y', [(i, (i - s) % ny) for i in range(ny)])  10.4 us
    ppermute x5, starting transfers between devices, tensor_gather(): others = [lax.ppermute(mine, 'core', swap) for mine, _, _ in pieces]  7.38 us
    another operation x1, local copies, waits for them, and re-layouts, tensor_gather(): out = jnp.tile(others[0], (1, 2 * ny))  6.28 us
    ppermute x1, starting transfers between devices, tensor_sum(): v = v + lax.ppermute(v, 'core', [(0, 1), (1, 0)])  5.88 us
  transfers between devices with their start and end apart: 14, of which 7 were waited for; matrix products, arithmetic and copies ran while one was open for 8% of the time, Pallas kernels for 0%

profile of v11, /device:TPU:1, one launch (start us, length us, event | category | flops | bytes accessed | tf_op | source)
XLA Modules:
  0.0 122.0 jit_solution(18036633038163088959)
XLA Ops:
  0.6 19.9 %all_to_all.20 = f32[4,592,128]{2,1,0:T(8,128)S(1)} all-to-all(f32[4,592,128]{2,1,0:T(8,128)} %bitcast.33), channel_id=1, replica_groups=mesh['z'=8,'x'=4,'y'=4,'core'=2] {'x'}, dimensions={0} | all-to-all | bytes 2424832 | tf_op jit(solution)/shard_map/all_to_all | solution.py:57
  20.7 19.2 %all_to_all.21 = f32[8,80,128]{2,1,0:T(8,128)S(1)} all-to-all(f32[8,80,128]{2,1,0:T(8,128)S(1)} %bitcast.31), channel_id=1, replica_groups=mesh['z'=8,'x'=4,'y'=4,'core'=2] {'z'}, dimensions={0} | all-to-all | bytes 655360 | tf_op jit(solution)/shard_map/all_to_all | solution.py:59
  39.9 12.5 %all_to_all.22 = f32[8,80,128]{2,1,0:T(8,128)S(1)} all-to-all(f32[8,80,128]{2,1,0:T(8,128)S(1)} %broadcast_in_dim.40), channel_id=1, replica_groups=mesh['z'=8,'x'=4,'y'=4,'core'=2] {'z'}, dimensions={0} | all-to-all | bytes 655360 | tf_op jit(solution)/shard_map/all_to_all | solution.py:60
  52.5 1.1 broadcast_in_dim.41
  53.6 3.5 %all-to-all-start.3 = ((f32[4,592,128]{2,1,0:T(8,128)}), f32[4,592,128]{2,1,0:T(8,128)S(1)}, u32[]{:S(2)}, u32[]{:S(2)}) async-start(f32[4,592,128]{2,1,0:T(8,128)} %broadcast_in_dim.41), calls=%async_computation.3 | async-start | bytes 2424832 | tf_op jit(solution)/shard_map/all_to_all | solution.py:62
  57.3 11.7 %all-to-all-done.3 = f32[4,592,128]{2,1,0:T(8,128)S(1)} async-done(((f32[4,592,128]{2,1,0:T(8,128)}), f32[4,592,128]{2,1,0:T(8,128)S(1)}, u32[]{:S(2)}, u32[]{:S(2)}) %all-to-all-start.3) | async-done | bytes 1212448 | tf_op jit(solution)/shard_map/all_to_all | solution.py:62
  69.0 0.2 broadcast_multiply_fusion
  69.2 1.1 copy-done.5
  70.3 0.4 bitcast_add_fusion
  70.7 0.9 copy-done.3
  71.6 1.3 %multiply_reduce_fusion = (f32[2368]{0:T(1024)S(1)}, f32[2368,128]{1,0:T(8,128)S(1)}, f32[2368]{0:T(1024)S(1)}) fusion(f32[2368,128]{1,0:T(8,128)S(1)} %copy-done.3, f32[2368]{0:T(1024)S(1)} %fusion.1, f32[2368,128]{1,0:T(8,128)S(1)} %get-tuple-element.16, f32[2368,128]{1,0:T(8,128)S(1)} %get-tuple-element.17), kind=kLoop, calls=%fused_computation.4 | loop fusion | flops 3026304 | bytes 4878080 | tf_op jit(solution)/shard_map/reduce_sum | solution.py:32
  72.9 0.1 convolution_bitcast_fusion
  73.0 0.2 convolution_bitcast_fusion.1
  73.2 0.1 pad_maximum_fusion
  73.4 5.9 %collective-permute-start = (f32[8]{0:T(128)S(1)}, f32[8]{0:T(128)S(1)}, u32[]{:S(2)}, u32[]{:S(2)}) collective-permute-start(f32[8]{0:T(128)S(1)} %pad_maximum_fusion), channel_id=1, source_target_pairs={{0,1},{1,0},{2,3},{3,2},{4,5},{5,4},{6,7},{7,6},{8,9},{9,8},{10,11... | collective-permute-start | bytes 104 | tf_op jit(solution)/shard_map/ppermute | solution.py:68
  79.2 0.8 collective-permute-done
  80.1 2.7 %collective-permute-start.1 = (f32[8]{0:T(128)S(1)}, f32[8]{0:T(128)S(1)}, u32[]{:S(2)}, u32[]{:S(2)}) collective-permute-start(f32[8]{0:T(128)S(1)} %fusion.11), channel_id=1, source_target_pairs={{0,6},{2,0},{4,2},{6,4},{1,7},{3,1},{5,3},{7,5},{8,14},{10,8},{12,... | collective-permute-start | bytes 104 | tf_op jit(solution)/shard_map/ppermute | solution.py:75
  82.9 0.3 collective-permute-start.2
  83.2 0.7 collective-permute-start.3
  84.0 2.8 %collective-permute-done.2 = f32[8]{0:T(128)S(1)} collective-permute-done((f32[8]{0:T(128)S(1)}, f32[8]{0:T(128)S(1)}, u32[]{:S(2)}, u32[]{:S(2)}) %collective-permute-start.2) | collective-permute-done | bytes 64 | tf_op jit(solution)/shard_map/ppermute | solution.py:75
  86.9 0.3 convolution_reduce_fusion
  87.2 1.4 %fusion.3 = (bf16[2368,128]{1,0:T(8,128)(2,1)S(1)}, f32[2368,128]{1,0:T(8,128)}) fusion(f32[2368,128]{1,0:T(8,128)S(1)} %copy-done.3, f32[2368,128]{1,0:T(8,128)S(1)} %get-tuple-element.8, f32[2368]{0:T(1024)S(1)} %broadcast_multiply_fusion.1), kind=kLoop, calls=%fused_computation.34 | loop fusion | flops 909312 | bytes 4252928 | tf_op jit(solution)/shard_map/convert_element_type | solution.py:119
  88.6 2.1 %collective-permute-start.4 = (bf16[2368,128]{1,0:T(8,128)(2,1)S(1)}, bf16[2368,128]{1,0:T(8,128)(2,1)S(1)}, u32[]{:S(2)}, u32[]{:S(2)}) collective-permute-start(bf16[2368,128]{1,0:T(8,128)(2,1)S(1)} %get-tuple-element.5), channel_id=1, source_target_pairs={{0,1},{1,0},{2,3},{3,2},{4,5},{5,4},{6,7},{7,6},{8,9},{9,8},{10,11... | collective-permute-start | bytes 1818632 | tf_op jit(solution)/shard_map/ppermute | solution.py:98
  90.7 0.2 collective-permute-start.5
  90.8 1.3 %collective-permute-start.7 = (bf16[2368,128]{1,0:T(8,128)(2,1)S(1)}, bf16[2368,128]{1,0:T(8,128)(2,1)S(1)}, u32[]{:S(2)}, u32[]{:S(2)}) collective-permute-start(bf16[2368,128]{1,0:T(8,128)(2,1)S(1)} %get-tuple-element.5), channel_id=1, source_target_pairs={{0,2},{2,4},{4,6},{6,0},{1,3},{3,5},{5,7},{7,1},{8,10},{10,12},{12... | collective-permute-start | bytes 1818632 | tf_op jit(solution)/shard_map/ppermute | solution.py:90
  92.1 0.6 fusion.10
  92.7 6.3 %tile.4 = bf16[2368,8,128]{2,1,0:T(8,128)(2,1)S(1)} broadcast(bf16[2368,128]{1,0:T(8,128)(2,1)S(1)} %collective-permute-done.4), dimensions={0,2} | broadcast | bytes 5455872 | tf_op jit(solution)/shard_map/tile | solution.py:99
  99.0 1.3 %copy.11 = bf16[296,8,8,128]{3,1,2,0:T(8,128)(2,1)S(1)} copy(bf16[296,8,8,128]{3,2,1,0:T(8,128)(2,1)S(1)} %bitcast.29) | data formatting | bytes 9699328
  100.3 5.6 %collective-permute-done.5 = bf16[2368,128]{1,0:T(8,128)(2,1)S(1)} collective-permute-done((bf16[2368,128]{1,0:T(8,128)(2,1)S(1)}, bf16[2368,128]{1,0:T(8,128)(2,1)S(1)}, u32[]{:S(2)}, u32[]{:S(2)}) %collective-permute-start.5) | collective-permute-done | bytes 606240 | tf_op jit(solution)/shard_map/ppermute | solution.py:90
  105.9 1.6 %collective-permute-start.9 = (bf16[1184,128]{1,0:T(8,128)(2,1)S(1)}, bf16[1184,128]{1,0:T(8,128)(2,1)S(1)}, u32[]{:S(2)}, u32[]{:S(2)}) collective-permute-start(bf16[1184,128]{1,0:T(8,128)(2,1)S(1)} %slice.49), channel_id=1, source_target_pairs={{0,6},{2,0},{4,2},{6,4},{1,7},{3,1},{5,3},{7,5},{8,14},{10,8},{12,... | collective-permute-start | bytes 909320 | tf_op jit(solution)/shard_map/ppermute | solution.py:90
  107.6 0.2 collective-permute-start.11
  107.7 0.2 constant_dynamic-update-slice_fusion.7
  108.0 1.5 %collective-permute-start.6 = (bf16[2368,128]{1,0:T(8,128)(2,1)S(1)}, bf16[2368,128]{1,0:T(8,128)(2,1)S(1)}, u32[]{:S(2)}, u32[]{:S(2)}) collective-permute-start(bf16[2368,128]{1,0:T(8,128)(2,1)S(1)} %collective-permute-done.5), channel_id=1, source_target_pairs={{0,1},{1,0},{2,3},{3,2},{4,5},{5,4},{6,7},{7,6},{8,9},{9,8},{10,11... | collective-permute-start | bytes 1818632 | tf_op jit(solution)/shard_map/ppermute | solution.py:98
  109.5 0.1 collective-permute-start.8
  109.6 0.2 constant_dynamic-update-slice_fusion.6
  109.8 0.2 constant_dynamic-update-slice_fusion.5
  110.0 4.1 %collective-permute-done.9 = bf16[1184,128]{1,0:T(8,128)(2,1)S(1)} collective-permute-done((bf16[1184,128]{1,0:T(8,128)(2,1)S(1)}, bf16[1184,128]{1,0:T(8,128)(2,1)S(1)}, u32[]{:S(2)}, u32[]{:S(2)}) %collective-permute-start.9) | collective-permute-done | bytes 303136 | tf_op jit(solution)/shard_map/ppermute | solution.py:90
  114.0 1.7 %collective-permute-start.10 = (bf16[1184,128]{1,0:T(8,128)(2,1)S(1)}, bf16[1184,128]{1,0:T(8,128)(2,1)S(1)}, u32[]{:S(2)}, u32[]{:S(2)}) collective-permute-start(bf16[1184,128]{1,0:T(8,128)(2,1)S(1)} %collective-permute-done.9), channel_id=1, source_target_pairs={{0,1},{1,0},{2,3},{3,2},{4,5},{5,4},{6,7},{7,6},{8,9},{9,8},{10,11... | collective-permute-start | bytes 909320 | tf_op jit(solution)/shard_map/ppermute | solution.py:98
  115.8 0.7 collective-permute-done.11
  116.5 2.0 %collective-permute-start.12 = (bf16[1184,128]{1,0:T(8,128)(2,1)S(1)}, bf16[1184,128]{1,0:T(8,128)(2,1)S(1)}, u32[]{:S(2)}, u32[]{:S(2)}) collective-permute-start(bf16[1184,128]{1,0:T(8,128)(2,1)S(1)} %collective-permute-done.11), channel_id=1, source_target_pairs={{0,1},{1,0},{2,3},{3,2},{4,5},{5,4},{6,7},{7,6},{8,9},{9,8},{10,11... | collective-permute-start | bytes 909320 | tf_op jit(solution)/shard_map/ppermute | solution.py:98
  118.5 0.2 constant_dynamic-update-slice_fusion.4
  118.7 0.2 constant_dynamic-update-slice_fusion.3
  118.9 0.2 constant_dynamic-update-slice_fusion.2
  119.1 0.1 constant_dynamic-update-slice_fusion.1
  119.2 0.1 constant_dynamic-update-slice_fusion
  119.4 0.1 constant_dynamic-update-slice_fusion.9
  119.5 0.2 collective-permute-done.12
  119.8 2.2 %copy-done.2 = bf16[2368,1024]{1,0:T(8,128)(2,1)} copy-done((bf16[2368,1024]{1,0:T(8,128)(2,1)}, bf16[2368,1024]{1,0:T(8,128)(2,1)S(1)}, u32[]{:S(2)}) %copy-start.2) | copy-done | bytes 4849688
  (38 shorter events, 0.7 us)
Async XLA Ops:
  53.6 15.5 %all-to-all-start.3 = ((f32[4,592,128]{2,1,0:T(8,128)}), f32[4,592,128]{2,1,0:T(8,128)S(1)}, u32[]{:S(2)}, u32[]{:S(2)}) async-start(f32[4,592,128]{2,1,0:T(8,128)} %broadcast_in_dim.41), calls=%async_computation.3 | async-start | bytes 2424832 | tf_op jit(solution)/shard_map/all_to_all | solution.py:62
  57.3 12.0 %copy-start.4 = (f32[2368,128]{1,0:T(8,128)S(1)}, f32[2368,128]{1,0:T(8,128)}, u32[]{:S(2)}) copy-start(f32[2368,128]{1,0:T(8,128)} %param.7) | copy-start | bytes 3637252
  69.0 1.3 %copy-start.5 = (f32[2368,128]{1,0:T(8,128)S(1)}, f32[2368,128]{1,0:T(8,128)}, u32[]{:S(2)}) copy-start(f32[2368,128]{1,0:T(8,128)} %param.6) | copy-start | bytes 3637252
  70.3 1.3 %copy-start.3 = (f32[2368,128]{1,0:T(8,128)S(1)}, f32[2368,128]{1,0:T(8,128)}, u32[]{:S(2)}) copy-start(f32[2368,128]{1,0:T(8,128)} %param.5) | copy-start | bytes 3637252
  70.7 2.2 %copy-start = (f32[2368,128]{1,0:T(8,128)}, f32[2368,128]{1,0:T(8,128)S(1)}, u32[]{:S(2)}) copy-start(f32[2368,128]{1,0:T(8,128)S(1)} %get-tuple-element.16) | copy-start | bytes 3637252
  70.7 2.2 %copy-start.1 = (f32[2368,128]{1,0:T(8,128)}, f32[2368,128]{1,0:T(8,128)S(1)}, u32[]{:S(2)}) copy-start(f32[2368,128]{1,0:T(8,128)S(1)} %get-tuple-element.17) | copy-start | bytes 3637252
  73.4 6.7 %collective-permute-start = (f32[8]{0:T(128)S(1)}, f32[8]{0:T(128)S(1)}, u32[]{:S(2)}, u32[]{:S(2)}) collective-permute-start(f32[8]{0:T(128)S(1)} %pad_maximum_fusion), channel_id=1, source_target_pairs={{0,1},{1,0},{2,3},{3,2},{4,5},{5,4},{6,7},{7,6},{8,9},{9,8},{10,11... | collective-permute-start | bytes 104 | tf_op jit(solution)/shard_map/ppermute | solution.py:68
  80.1 3.8 %collective-permute-start.1 = (f32[8]{0:T(128)S(1)}, f32[8]{0:T(128)S(1)}, u32[]{:S(2)}, u32[]{:S(2)}) collective-permute-start(f32[8]{0:T(128)S(1)} %fusion.11), channel_id=1, source_target_pairs={{0,6},{2,0},{4,2},{6,4},{1,7},{3,1},{5,3},{7,5},{8,14},{10,8},{12,... | collective-permute-start | bytes 104 | tf_op jit(solution)/shard_map/ppermute | solution.py:75
  82.9 3.9 %collective-permute-start.2 = (f32[8]{0:T(128)S(1)}, f32[8]{0:T(128)S(1)}, u32[]{:S(2)}, u32[]{:S(2)}) collective-permute-start(f32[8]{0:T(128)S(1)} %fusion.11), channel_id=1, source_target_pairs={{0,4},{2,6},{4,0},{6,2},{1,5},{3,7},{5,1},{7,3},{8,12},{10,14},{12... | collective-permute-start | bytes 104 | tf_op jit(solution)/shard_map/ppermute | solution.py:75
  83.2 3.6 %collective-permute-start.3 = (f32[8]{0:T(128)S(1)}, f32[8]{0:T(128)S(1)}, u32[]{:S(2)}, u32[]{:S(2)}) collective-permute-start(f32[8]{0:T(128)S(1)} %fusion.11), channel_id=1, source_target_pairs={{0,2},{2,4},{4,6},{6,0},{1,3},{3,5},{5,7},{7,1},{8,10},{10,12},{12... | collective-permute-start | bytes 104 | tf_op jit(solution)/shard_map/ppermute | solution.py:75
  88.6 4.1 %collective-permute-start.4 = (bf16[2368,128]{1,0:T(8,128)(2,1)S(1)}, bf16[2368,128]{1,0:T(8,128)(2,1)S(1)}, u32[]{:S(2)}, u32[]{:S(2)}) collective-permute-start(bf16[2368,128]{1,0:T(8,128)(2,1)S(1)} %get-tuple-element.5), channel_id=1, source_target_pairs={{0,1},{1,0},{2,3},{3,2},{4,5},{5,4},{6,7},{7,6},{8,9},{9,8},{10,11... | collective-permute-start | bytes 1818632 | tf_op jit(solution)/shard_map/ppermute | solution.py:98
  90.7 15.2 %collective-permute-start.5 = (bf16[2368,128]{1,0:T(8,128)(2,1)S(1)}, bf16[2368,128]{1,0:T(8,128)(2,1)S(1)}, u32[]{:S(2)}, u32[]{:S(2)}) collective-permute-start(bf16[2368,128]{1,0:T(8,128)(2,1)S(1)} %get-tuple-element.5), channel_id=1, source_target_pairs={{0,6},{2,0},{4,2},{6,4},{1,7},{3,1},{5,3},{7,5},{8,14},{10,8},{12,... | collective-permute-start | bytes 1818632 | tf_op jit(solution)/shard_map/ppermute | solution.py:90
  90.8 16.7 %collective-permute-start.7 = (bf16[2368,128]{1,0:T(8,128)(2,1)S(1)}, bf16[2368,128]{1,0:T(8,128)(2,1)S(1)}, u32[]{:S(2)}, u32[]{:S(2)}) collective-permute-start(bf16[2368,128]{1,0:T(8,128)(2,1)S(1)} %get-tuple-element.5), channel_id=1, source_target_pairs={{0,2},{2,4},{4,6},{6,0},{1,3},{3,5},{5,7},{7,1},{8,10},{10,12},{12... | collective-permute-start | bytes 1818632 | tf_op jit(solution)/shard_map/ppermute | solution.py:90
  105.9 8.1 %collective-permute-start.9 = (bf16[1184,128]{1,0:T(8,128)(2,1)S(1)}, bf16[1184,128]{1,0:T(8,128)(2,1)S(1)}, u32[]{:S(2)}, u32[]{:S(2)}) collective-permute-start(bf16[1184,128]{1,0:T(8,128)(2,1)S(1)} %slice.49), channel_id=1, source_target_pairs={{0,6},{2,0},{4,2},{6,4},{1,7},{3,1},{5,3},{7,5},{8,14},{10,8},{12,... | collective-permute-start | bytes 909320 | tf_op jit(solution)/shard_map/ppermute | solution.py:90
  107.6 8.9 %collective-permute-start.11 = (bf16[1184,128]{1,0:T(8,128)(2,1)S(1)}, bf16[1184,128]{1,0:T(8,128)(2,1)S(1)}, u32[]{:S(2)}, u32[]{:S(2)}) collective-permute-start(bf16[1184,128]{1,0:T(8,128)(2,1)S(1)} %slice.50), channel_id=1, source_target_pairs={{0,2},{2,4},{4,6},{6,0},{1,3},{3,5},{5,7},{7,1},{8,10},{10,12},{12... | collective-permute-start | bytes 909320 | tf_op jit(solution)/shard_map/ppermute | solution.py:90
  108.0 10.5 %collective-permute-start.6 = (bf16[2368,128]{1,0:T(8,128)(2,1)S(1)}, bf16[2368,128]{1,0:T(8,128)(2,1)S(1)}, u32[]{:S(2)}, u32[]{:S(2)}) collective-permute-start(bf16[2368,128]{1,0:T(8,128)(2,1)S(1)} %collective-permute-done.5), channel_id=1, source_target_pairs={{0,1},{1,0},{2,3},{3,2},{4,5},{5,4},{6,7},{7,6},{8,9},{9,8},{10,11... | collective-permute-start | bytes 1818632 | tf_op jit(solution)/shard_map/ppermute | solution.py:98
  109.5 9.4 %collective-permute-start.8 = (bf16[2368,128]{1,0:T(8,128)(2,1)S(1)}, bf16[2368,128]{1,0:T(8,128)(2,1)S(1)}, u32[]{:S(2)}, u32[]{:S(2)}) collective-permute-start(bf16[2368,128]{1,0:T(8,128)(2,1)S(1)} %collective-permute-done.7), channel_id=1, source_target_pairs={{0,1},{1,0},{2,3},{3,2},{4,5},{5,4},{6,7},{7,6},{8,9},{9,8},{10,11... | collective-permute-start | bytes 1818632 | tf_op jit(solution)/shard_map/ppermute | solution.py:98
  114.0 5.2 %collective-permute-start.10 = (bf16[1184,128]{1,0:T(8,128)(2,1)S(1)}, bf16[1184,128]{1,0:T(8,128)(2,1)S(1)}, u32[]{:S(2)}, u32[]{:S(2)}) collective-permute-start(bf16[1184,128]{1,0:T(8,128)(2,1)S(1)} %collective-permute-done.9), channel_id=1, source_target_pairs={{0,1},{1,0},{2,3},{3,2},{4,5},{5,4},{6,7},{7,6},{8,9},{9,8},{10,11... | collective-permute-start | bytes 909320 | tf_op jit(solution)/shard_map/ppermute | solution.py:98
  116.5 3.2 %collective-permute-start.12 = (bf16[1184,128]{1,0:T(8,128)(2,1)S(1)}, bf16[1184,128]{1,0:T(8,128)(2,1)S(1)}, u32[]{:S(2)}, u32[]{:S(2)}) collective-permute-start(bf16[1184,128]{1,0:T(8,128)(2,1)S(1)} %collective-permute-done.11), channel_id=1, source_target_pairs={{0,1},{1,0},{2,3},{3,2},{4,5},{5,4},{6,7},{7,6},{8,9},{9,8},{10,11... | collective-permute-start | bytes 909320 | tf_op jit(solution)/shard_map/ppermute | solution.py:98
  119.8 2.2 %copy-start.2 = (bf16[2368,1024]{1,0:T(8,128)(2,1)}, bf16[2368,1024]{1,0:T(8,128)(2,1)S(1)}, u32[]{:S(2)}) copy-start(bf16[2368,1024]{1,0:T(8,128)(2,1)S(1)} %constant_dynamic-update-slice_fusion.8) | copy-start | bytes 14548996

commit v12 on v11

--- a/solution.py
+++ b/solution.py
@@ -64,18 +64,15 @@
 
 
 def tensor_sum(v, ny, ncore):
-    if ncore == 2:
-        v = v + lax.ppermute(v, "core", [(0, 1), (1, 0)])
-    else:
-        v = lax.psum(v, "core")
-    y = lax.axis_index("y")
-    slots = jnp.zeros((ny,) + v.shape, v.dtype)
-    slots = lax.dynamic_update_index_in_dim(slots, v, y, 0)
-    for s in range(1, ny):
-        got = lax.ppermute(v, "y", [(i, (i - s) % ny) for i in range(ny)])
-        slots = lax.dynamic_update_index_in_dim(slots, got, (y + s) % ny, 0)
+    n = ny * ncore
+    me = lax.axis_index(TN)
+    slots = jnp.zeros((n,) + v.shape, v.dtype)
+    slots = lax.dynamic_update_index_in_dim(slots, v, me, 0)
+    for s in range(1, n):
+        got = lax.ppermute(v, TN, [(i, (i - s) % n) for i in range(n)])
+        slots = lax.dynamic_update_index_in_dim(slots, got, (me + s) % n, 0)
     total = slots[0]
-    for k in range(1, ny):
+    for k in range(1, n):
         total = total + slots[k]
     return total
 

time: 122 us -> 125 us (1.025)
  starting transfers between devices: 23.8 us -> 27.7 us
  waiting for transfers between devices: 26 us -> 24.5 us
    ppermute x4 -> x7, starting transfers between devices: 9.66 us -> 14.2 us  [tensor_sum(): got = lax.ppermute(v, TN, [(i, (i - s) % n) for i in range(n)])]
    ppermute x4 -> x7, waiting for transfers between devices: 3.65 us -> 1.85 us  [tensor_sum(): got = lax.ppermute(v, TN, [(i, (i - s) % n) for i in range(n)])]
    ppermute x5, starting transfers between devices: 7.38 us -> 5.96 us  [tensor_gather(): others = [lax.ppermute(mine, 'core', swap) for mine, _, _ in pieces]]
  transfers between devices with their start and end apart: 14 -> 17, of which waited for: 7 -> 6; matrix products, arithmetic and copies ran while one was open for 8% -> 8% of each run, Pallas kernels for 0% -> 0%
where the time goes in v12:
time: 125 us; the launch traced here: 124 us
  blocking collectives  51.6 us (41%)
  starting transfers between devices  27.7 us (22%)
  waiting for transfers between devices  24.5 us (20%)
  local copies, waits for them, and re-layouts  14.9 us (12%)
  other arithmetic  4.17 us (3%)
    all_to_all x1, blocking collectives, dp_sum(): y = lax.all_to_all(x.reshape(nx, part, cols), 'x', 0, 0, tiled=False).sum(0)  19.9 us
    all_to_all x1, blocking collectives, dp_sum(): lax.all_to_all(y.reshape(nz, padded // nz, cols), 'z', 0, 0, tiled=False)  19.2 us
    ppermute x7, starting transfers between devices, tensor_sum(): got = lax.ppermute(v, TN, [(i, (i - s) % n) for i in range(n)])  14.2 us
    all_to_all x1, blocking collectives, dp_sum(): lax.all_to_all(jnp.broadcast_to(y[None], (nz,) + y.shape), 'z', 0, 0, til...  12.5 us
    all_to_all x1, waiting for transfers between devices, dp_sum(): lax.all_to_all(jnp.broadcast_to(y[None], (nx,) + y.shape), 'x', 0, 0, til...  11.7 us
    ppermute x4, waiting for transfers between devices, shift(): return lax.ppermute(v, 'y', [(i, (i - s) % ny) for i in range(ny)])  10.7 us
    another operation x1, local copies, waits for them, and re-layouts, tensor_gather(): out = jnp.tile(others[0], (1, 2 * ny))  6.28 us
    ppermute x5, starting transfers between devices, tensor_gather(): others = [lax.ppermute(mine, 'core', swap) for mine, _, _ in pieces]  5.96 us
  transfers between devices with their start and end apart: 17, of which 6 were waited for; matrix products, arithmetic and copies ran while one was open for 8% of the time, Pallas kernels for 0%

profile of v12, /device:TPU:1, one launch (start us, length us, event | category | flops | bytes accessed | tf_op | source)
XLA Modules:
  0.0 124.5 jit_solution(15202856473083483810)
XLA Ops:
  0.6 19.9 %all_to_all.20 = f32[4,592,128]{2,1,0:T(8,128)S(1)} all-to-all(f32[4,592,128]{2,1,0:T(8,128)} %bitcast.37), channel_id=1, replica_groups=mesh['z'=8,'x'=4,'y'=4,'core'=2] {'x'}, dimensions={0} | all-to-all | bytes 2424832 | tf_op jit(solution)/shard_map/all_to_all | solution.py:57
  20.7 19.2 %all_to_all.21 = f32[8,80,128]{2,1,0:T(8,128)S(1)} all-to-all(f32[8,80,128]{2,1,0:T(8,128)S(1)} %bitcast.35), channel_id=1, replica_groups=mesh['z'=8,'x'=4,'y'=4,'core'=2] {'z'}, dimensions={0} | all-to-all | bytes 655360 | tf_op jit(solution)/shard_map/all_to_all | solution.py:59
  39.9 12.5 %all_to_all.22 = f32[8,80,128]{2,1,0:T(8,128)S(1)} all-to-all(f32[8,80,128]{2,1,0:T(8,128)S(1)} %broadcast_in_dim.52), channel_id=1, replica_groups=mesh['z'=8,'x'=4,'y'=4,'core'=2] {'z'}, dimensions={0} | all-to-all | bytes 655360 | tf_op jit(solution)/shard_map/all_to_all | solution.py:60
  52.5 1.1 broadcast_in_dim.53
  53.6 3.5 %all-to-all-start.3 = ((f32[4,592,128]{2,1,0:T(8,128)}), f32[4,592,128]{2,1,0:T(8,128)S(1)}, u32[]{:S(2)}, u32[]{:S(2)}) async-start(f32[4,592,128]{2,1,0:T(8,128)} %broadcast_in_dim.53), calls=%async_computation.3 | async-start | bytes 2424832 | tf_op jit(solution)/shard_map/all_to_all | solution.py:62
  57.3 11.7 %all-to-all-done.3 = f32[4,592,128]{2,1,0:T(8,128)S(1)} async-done(((f32[4,592,128]{2,1,0:T(8,128)}), f32[4,592,128]{2,1,0:T(8,128)S(1)}, u32[]{:S(2)}, u32[]{:S(2)}) %all-to-all-start.3) | async-done | bytes 1212448 | tf_op jit(solution)/shard_map/all_to_all | solution.py:62
  69.0 0.2 broadcast_multiply_fusion
  69.2 1.1 copy-done.5
  70.3 0.4 bitcast_add_fusion
  70.7 0.9 copy-done.3
  71.6 1.3 %multiply_reduce_fusion = (f32[2368]{0:T(1024)S(1)}, f32[2368,128]{1,0:T(8,128)S(1)}, f32[2368]{0:T(1024)S(1)}) fusion(f32[2368,128]{1,0:T(8,128)S(1)} %copy-done.3, f32[2368]{0:T(1024)S(1)} %fusion.1, f32[2368,128]{1,0:T(8,128)S(1)} %get-tuple-element.16, f32[2368,128]{1,0:T(8,128)S(1)} %get-tuple-element.17), kind=kLoop, calls=%fused_computation.4 | loop fusion | flops 3026304 | bytes 4878080 | tf_op jit(solution)/shard_map/reduce_sum | solution.py:32
  72.9 0.1 convolution_bitcast_fusion
  73.0 0.2 convolution_bitcast_fusion.1
  73.2 0.1 pad_maximum_fusion
  73.4 5.9 %collective-permute-start = (f32[8]{0:T(128)S(1)}, f32[8]{0:T(128)S(1)}, u32[]{:S(2)}, u32[]{:S(2)}) collective-permute-start(f32[8]{0:T(128)S(1)} %pad_maximum_fusion), channel_id=1, source_target_pairs={{0,7},{1,0},{2,1},{3,2},{4,3},{5,4},{6,5},{7,6},{8,15},{9,8},{10,9... | collective-permute-start | bytes 104 | tf_op jit(solution)/shard_map/ppermute | solution.py:72
  79.2 2.7 %collective-permute-start.1 = (f32[8]{0:T(128)S(1)}, f32[8]{0:T(128)S(1)}, u32[]{:S(2)}, u32[]{:S(2)}) collective-permute-start(f32[8]{0:T(128)S(1)} %pad_maximum_fusion), channel_id=1, source_target_pairs={{0,6},{1,7},{2,0},{3,1},{4,2},{5,3},{6,4},{7,5},{8,14},{9,15},{10,... | collective-permute-start | bytes 104 | tf_op jit(solution)/shard_map/ppermute | solution.py:72
  82.0 0.7 collective-permute-start.2
  82.7 3.2 %collective-permute-start.4 = (f32[8]{0:T(128)S(1)}, f32[8]{0:T(128)S(1)}, u32[]{:S(2)}, u32[]{:S(2)}) collective-permute-start(f32[8]{0:T(128)S(1)} %pad_maximum_fusion), channel_id=1, source_target_pairs={{0,3},{1,4},{2,5},{3,6},{4,7},{5,0},{6,1},{7,2},{8,11},{9,12},{10,... | collective-permute-start | bytes 104 | tf_op jit(solution)/shard_map/ppermute | solution.py:72
  85.9 0.8 collective-permute-start.5
  86.7 0.9 collective-permute-start.6
  87.7 1.8 %collective-permute-done.5 = f32[8]{0:T(128)S(1)} collective-permute-done((f32[8]{0:T(128)S(1)}, f32[8]{0:T(128)S(1)}, u32[]{:S(2)}, u32[]{:S(2)}) %collective-permute-start.5) | collective-permute-done | bytes 64 | tf_op jit(solution)/shard_map/ppermute | solution.py:72
  89.7 0.3 convolution_reduce_fusion
  89.9 1.4 %fusion.3 = (bf16[2368,128]{1,0:T(8,128)(2,1)S(1)}, f32[2368,128]{1,0:T(8,128)}) fusion(f32[2368,128]{1,0:T(8,128)S(1)} %copy-done.3, f32[2368,128]{1,0:T(8,128)S(1)} %get-tuple-element.8, f32[2368]{0:T(1024)S(1)} %broadcast_multiply_fusion.1), kind=kLoop, calls=%fused_computation.34 | loop fusion | flops 909312 | bytes 4252928 | tf_op jit(solution)/shard_map/convert_element_type | solution.py:116
  91.3 0.9 collective-permute-start.7
  92.3 1.2 collective-permute-start.8
  93.4 0.3 collective-permute-start.10
  93.7 0.6 fusion.10
  94.3 6.3 %tile.4 = bf16[2368,8,128]{2,1,0:T(8,128)(2,1)S(1)} broadcast(bf16[2368,128]{1,0:T(8,128)(2,1)S(1)} %collective-permute-done.7), dimensions={0,2} | broadcast | bytes 5455872 | tf_op jit(solution)/shard_map/tile | solution.py:96
  100.6 1.3 %copy.11 = bf16[296,8,8,128]{3,1,2,0:T(8,128)(2,1)S(1)} copy(bf16[296,8,8,128]{3,2,1,0:T(8,128)(2,1)S(1)} %bitcast.33) | data formatting | bytes 9699328
  101.9 5.6 %collective-permute-done.8 = bf16[2368,128]{1,0:T(8,128)(2,1)S(1)} collective-permute-done((bf16[2368,128]{1,0:T(8,128)(2,1)S(1)}, bf16[2368,128]{1,0:T(8,128)(2,1)S(1)}, u32[]{:S(2)}, u32[]{:S(2)}) %collective-permute-start.8) | collective-permute-done | bytes 606240 | tf_op jit(solution)/shard_map/ppermute | solution.py:87
  107.5 2.5 %collective-permute-start.12 = (bf16[1184,128]{1,0:T(8,128)(2,1)S(1)}, bf16[1184,128]{1,0:T(8,128)(2,1)S(1)}, u32[]{:S(2)}, u32[]{:S(2)}) collective-permute-start(bf16[1184,128]{1,0:T(8,128)(2,1)S(1)} %slice.65), channel_id=1, source_target_pairs={{0,6},{2,0},{4,2},{6,4},{1,7},{3,1},{5,3},{7,5},{8,14},{10,8},{12,... | collective-permute-start | bytes 909320 | tf_op jit(solution)/shard_map/ppermute | solution.py:87
  110.1 0.2 constant_dynamic-update-slice_fusion.7
  110.3 1.2 collective-permute-start.9
  111.5 0.1 collective-permute-start.11
  111.6 0.2 constant_dynamic-update-slice_fusion.6
  111.9 0.2 constant_dynamic-update-slice_fusion.5
  112.1 3.6 %collective-permute-done.12 = bf16[1184,128]{1,0:T(8,128)(2,1)S(1)} collective-permute-done((bf16[1184,128]{1,0:T(8,128)(2,1)S(1)}, bf16[1184,128]{1,0:T(8,128)(2,1)S(1)}, u32[]{:S(2)}, u32[]{:S(2)}) %collective-permute-start.12) | collective-permute-done | bytes 303136 | tf_op jit(solution)/shard_map/ppermute | solution.py:87
  115.7 1.7 %collective-permute-start.13 = (bf16[1184,128]{1,0:T(8,128)(2,1)S(1)}, bf16[1184,128]{1,0:T(8,128)(2,1)S(1)}, u32[]{:S(2)}, u32[]{:S(2)}) collective-permute-start(bf16[1184,128]{1,0:T(8,128)(2,1)S(1)} %collective-permute-done.12), channel_id=1, source_target_pairs={{0,1},{1,0},{2,3},{3,2},{4,5},{5,4},{6,7},{7,6},{8,9},{9,8},{10,11... | collective-permute-start | bytes 909320 | tf_op jit(solution)/shard_map/ppermute | solution.py:95
  117.4 1.5 %collective-permute-done.14 = bf16[1184,128]{1,0:T(8,128)(2,1)S(1)} collective-permute-done((bf16[1184,128]{1,0:T(8,128)(2,1)S(1)}, bf16[1184,128]{1,0:T(8,128)(2,1)S(1)}, u32[]{:S(2)}, u32[]{:S(2)}) %collective-permute-start.14) | collective-permute-done | bytes 303136 | tf_op jit(solution)/shard_map/ppermute | solution.py:87
  118.9 2.0 %collective-permute-start.15 = (bf16[1184,128]{1,0:T(8,128)(2,1)S(1)}, bf16[1184,128]{1,0:T(8,128)(2,1)S(1)}, u32[]{:S(2)}, u32[]{:S(2)}) collective-permute-start(bf16[1184,128]{1,0:T(8,128)(2,1)S(1)} %collective-permute-done.14), channel_id=1, source_target_pairs={{0,1},{1,0},{2,3},{3,2},{4,5},{5,4},{6,7},{7,6},{8,9},{9,8},{10,11... | collective-permute-start | bytes 909320 | tf_op jit(solution)/shard_map/ppermute | solution.py:95
  120.9 0.2 constant_dynamic-update-slice_fusion.4
  121.1 0.2 constant_dynamic-update-slice_fusion.3
  121.3 0.2 constant_dynamic-update-slice_fusion.2
  121.6 0.1 constant_dynamic-update-slice_fusion.1
  121.7 0.1 constant_dynamic-update-slice_fusion
  121.8 0.1 constant_dynamic-update-slice_fusion.9
  121.9 0.2 collective-permute-done.15
  122.2 2.2 %copy-done.2 = bf16[2368,1024]{1,0:T(8,128)(2,1)} copy-done((bf16[2368,1024]{1,0:T(8,128)(2,1)}, bf16[2368,1024]{1,0:T(8,128)(2,1)S(1)}, u32[]{:S(2)}) %copy-start.2) | copy-done | bytes 4849688
  (47 shorter events, 0.9 us)
Async XLA Ops:
  53.6 15.5 %all-to-all-start.3 = ((f32[4,592,128]{2,1,0:T(8,128)}), f32[4,592,128]{2,1,0:T(8,128)S(1)}, u32[]{:S(2)}, u32[]{:S(2)}) async-start(f32[4,592,128]{2,1,0:T(8,128)} %broadcast_in_dim.53), calls=%async_computation.3 | async-start | bytes 2424832 | tf_op jit(solution)/shard_map/all_to_all | solution.py:62
  57.3 11.9 %copy-start.4 = (f32[2368,128]{1,0:T(8,128)S(1)}, f32[2368,128]{1,0:T(8,128)}, u32[]{:S(2)}) copy-start(f32[2368,128]{1,0:T(8,128)} %param.7) | copy-start | bytes 3637252
  69.0 1.3 %copy-start.5 = (f32[2368,128]{1,0:T(8,128)S(1)}, f32[2368,128]{1,0:T(8,128)}, u32[]{:S(2)}) copy-start(f32[2368,128]{1,0:T(8,128)} %param.6) | copy-start | bytes 3637252
  70.3 1.3 %copy-start.3 = (f32[2368,128]{1,0:T(8,128)S(1)}, f32[2368,128]{1,0:T(8,128)}, u32[]{:S(2)}) copy-start(f32[2368,128]{1,0:T(8,128)} %param.5) | copy-start | bytes 3637252
  70.7 2.2 %copy-start = (f32[2368,128]{1,0:T(8,128)}, f32[2368,128]{1,0:T(8,128)S(1)}, u32[]{:S(2)}) copy-start(f32[2368,128]{1,0:T(8,128)S(1)} %get-tuple-element.16) | copy-start | bytes 3637252
  70.7 2.2 %copy-start.1 = (f32[2368,128]{1,0:T(8,128)}, f32[2368,128]{1,0:T(8,128)S(1)}, u32[]{:S(2)}) copy-start(f32[2368,128]{1,0:T(8,128)S(1)} %get-tuple-element.17) | copy-start | bytes 3637252
  73.4 12.5 %collective-permute-start = (f32[8]{0:T(128)S(1)}, f32[8]{0:T(128)S(1)}, u32[]{:S(2)}, u32[]{:S(2)}) collective-permute-start(f32[8]{0:T(128)S(1)} %pad_maximum_fusion), channel_id=1, source_target_pairs={{0,7},{1,0},{2,1},{3,2},{4,3},{5,4},{6,5},{7,6},{8,15},{9,8},{10,9... | collective-permute-start | bytes 104 | tf_op jit(solution)/shard_map/ppermute | solution.py:72
  79.2 7.4 %collective-permute-start.1 = (f32[8]{0:T(128)S(1)}, f32[8]{0:T(128)S(1)}, u32[]{:S(2)}, u32[]{:S(2)}) collective-permute-start(f32[8]{0:T(128)S(1)} %pad_maximum_fusion), channel_id=1, source_target_pairs={{0,6},{1,7},{2,0},{3,1},{4,2},{5,3},{6,4},{7,5},{8,14},{9,15},{10,... | collective-permute-start | bytes 104 | tf_op jit(solution)/shard_map/ppermute | solution.py:72
  82.0 5.7 %collective-permute-start.2 = (f32[8]{0:T(128)S(1)}, f32[8]{0:T(128)S(1)}, u32[]{:S(2)}, u32[]{:S(2)}) collective-permute-start(f32[8]{0:T(128)S(1)} %pad_maximum_fusion), channel_id=1, source_target_pairs={{0,5},{1,6},{2,7},{3,0},{4,1},{5,2},{6,3},{7,4},{8,13},{9,14},{10,... | collective-permute-start | bytes 104 | tf_op jit(solution)/shard_map/ppermute | solution.py:72
  82.6 5.0 %collective-permute-start.3 = (f32[8]{0:T(128)S(1)}, f32[8]{0:T(128)S(1)}, u32[]{:S(2)}, u32[]{:S(2)}) collective-permute-start(f32[8]{0:T(128)S(1)} %pad_maximum_fusion), channel_id=1, source_target_pairs={{0,4},{1,5},{2,6},{3,7},{4,0},{5,1},{6,2},{7,3},{8,12},{9,13},{10,... | collective-permute-start | bytes 104 | tf_op jit(solution)/shard_map/ppermute | solution.py:72
  82.7 5.0 %collective-permute-start.4 = (f32[8]{0:T(128)S(1)}, f32[8]{0:T(128)S(1)}, u32[]{:S(2)}, u32[]{:S(2)}) collective-permute-start(f32[8]{0:T(128)S(1)} %pad_maximum_fusion), channel_id=1, source_target_pairs={{0,3},{1,4},{2,5},{3,6},{4,7},{5,0},{6,1},{7,2},{8,11},{9,12},{10,... | collective-permute-start | bytes 104 | tf_op jit(solution)/shard_map/ppermute | solution.py:72
  85.9 3.7 %collective-permute-start.5 = (f32[8]{0:T(128)S(1)}, f32[8]{0:T(128)S(1)}, u32[]{:S(2)}, u32[]{:S(2)}) collective-permute-start(f32[8]{0:T(128)S(1)} %pad_maximum_fusion), channel_id=1, source_target_pairs={{0,2},{1,3},{2,4},{3,5},{4,6},{5,7},{6,0},{7,1},{8,10},{9,11},{10,... | collective-permute-start | bytes 104 | tf_op jit(solution)/shard_map/ppermute | solution.py:72
  86.7 2.9 %collective-permute-start.6 = (f32[8]{0:T(128)S(1)}, f32[8]{0:T(128)S(1)}, u32[]{:S(2)}, u32[]{:S(2)}) collective-permute-start(f32[8]{0:T(128)S(1)} %pad_maximum_fusion), channel_id=1, source_target_pairs={{0,1},{1,2},{2,3},{3,4},{4,5},{5,6},{6,7},{7,0},{8,9},{9,10},{10,1... | collective-permute-start | bytes 104 | tf_op jit(solution)/shard_map/ppermute | solution.py:72
  91.3 3.0 %collective-permute-start.7 = (bf16[2368,128]{1,0:T(8,128)(2,1)S(1)}, bf16[2368,128]{1,0:T(8,128)(2,1)S(1)}, u32[]{:S(2)}, u32[]{:S(2)}) collective-permute-start(bf16[2368,128]{1,0:T(8,128)(2,1)S(1)} %get-tuple-element.5), channel_id=1, source_target_pairs={{0,1},{1,0},{2,3},{3,2},{4,5},{5,4},{6,7},{7,6},{8,9},{9,8},{10,11... | collective-permute-start | bytes 1818632 | tf_op jit(solution)/shard_map/ppermute | solution.py:95
  92.3 15.2 %collective-permute-start.8 = (bf16[2368,128]{1,0:T(8,128)(2,1)S(1)}, bf16[2368,128]{1,0:T(8,128)(2,1)S(1)}, u32[]{:S(2)}, u32[]{:S(2)}) collective-permute-start(bf16[2368,128]{1,0:T(8,128)(2,1)S(1)} %get-tuple-element.5), channel_id=1, source_target_pairs={{0,6},{2,0},{4,2},{6,4},{1,7},{3,1},{5,3},{7,5},{8,14},{10,8},{12,... | collective-permute-start | bytes 1818632 | tf_op jit(solution)/shard_map/ppermute | solution.py:87
  93.4 16.5 %collective-permute-start.10 = (bf16[2368,128]{1,0:T(8,128)(2,1)S(1)}, bf16[2368,128]{1,0:T(8,128)(2,1)S(1)}, u32[]{:S(2)}, u32[]{:S(2)}) collective-permute-start(bf16[2368,128]{1,0:T(8,128)(2,1)S(1)} %get-tuple-element.5), channel_id=1, source_target_pairs={{0,2},{2,4},{4,6},{6,0},{1,3},{3,5},{5,7},{7,1},{8,10},{10,12},{12... | collective-permute-start | bytes 1818632 | tf_op jit(solution)/shard_map/ppermute | solution.py:87
  107.5 8.1 %collective-permute-start.12 = (bf16[1184,128]{1,0:T(8,128)(2,1)S(1)}, bf16[1184,128]{1,0:T(8,128)(2,1)S(1)}, u32[]{:S(2)}, u32[]{:S(2)}) collective-permute-start(bf16[1184,128]{1,0:T(8,128)(2,1)S(1)} %slice.65), channel_id=1, source_target_pairs={{0,6},{2,0},{4,2},{6,4},{1,7},{3,1},{5,3},{7,5},{8,14},{10,8},{12,... | collective-permute-start | bytes 909320 | tf_op jit(solution)/shard_map/ppermute | solution.py:87
  110.0 8.9 %collective-permute-start.14 = (bf16[1184,128]{1,0:T(8,128)(2,1)S(1)}, bf16[1184,128]{1,0:T(8,128)(2,1)S(1)}, u32[]{:S(2)}, u32[]{:S(2)}) collective-permute-start(bf16[1184,128]{1,0:T(8,128)(2,1)S(1)} %slice.66), channel_id=1, source_target_pairs={{0,2},{2,4},{4,6},{6,0},{1,3},{3,5},{5,7},{7,1},{8,10},{10,12},{12... | collective-permute-start | bytes 909320 | tf_op jit(solution)/shard_map/ppermute | solution.py:87
  110.3 10.6 %collective-permute-start.9 = (bf16[2368,128]{1,0:T(8,128)(2,1)S(1)}, bf16[2368,128]{1,0:T(8,128)(2,1)S(1)}, u32[]{:S(2)}, u32[]{:S(2)}) collective-permute-start(bf16[2368,128]{1,0:T(8,128)(2,1)S(1)} %collective-permute-done.8), channel_id=1, source_target_pairs={{0,1},{1,0},{2,3},{3,2},{4,5},{5,4},{6,7},{7,6},{8,9},{9,8},{10,11... | collective-permute-start | bytes 1818632 | tf_op jit(solution)/shard_map/ppermute | solution.py:95
  111.5 9.8 %collective-permute-start.11 = (bf16[2368,128]{1,0:T(8,128)(2,1)S(1)}, bf16[2368,128]{1,0:T(8,128)(2,1)S(1)}, u32[]{:S(2)}, u32[]{:S(2)}) collective-permute-start(bf16[2368,128]{1,0:T(8,128)(2,1)S(1)} %collective-permute-done.10), channel_id=1, source_target_pairs={{0,1},{1,0},{2,3},{3,2},{4,5},{5,4},{6,7},{7,6},{8,9},{9,8},{10,11... | collective-permute-start | bytes 1818632 | tf_op jit(solution)/shard_map/ppermute | solution.py:95
  115.7 6.0 %collective-permute-start.13 = (bf16[1184,128]{1,0:T(8,128)(2,1)S(1)}, bf16[1184,128]{1,0:T(8,128)(2,1)S(1)}, u32[]{:S(2)}, u32[]{:S(2)}) collective-permute-start(bf16[1184,128]{1,0:T(8,128)(2,1)S(1)} %collective-permute-done.12), channel_id=1, source_target_pairs={{0,1},{1,0},{2,3},{3,2},{4,5},{5,4},{6,7},{7,6},{8,9},{9,8},{10,11... | collective-permute-start | bytes 909320 | tf_op jit(solution)/shard_map/ppermute | solution.py:95
  118.9 3.2 %collective-permute-start.15 = (bf16[1184,128]{1,0:T(8,128)(2,1)S(1)}, bf16[1184,128]{1,0:T(8,128)(2,1)S(1)}, u32[]{:S(2)}, u32[]{:S(2)}) collective-permute-start(bf16[1184,128]{1,0:T(8,128)(2,1)S(1)} %collective-permute-done.14), channel_id=1, source_target_pairs={{0,1},{1,0},{2,3},{3,2},{4,5},{5,4},{6,7},{7,6},{8,9},{9,8},{10,11... | collective-permute-start | bytes 909320 | tf_op jit(solution)/shard_map/ppermute | solution.py:95
  122.2 2.2 %copy-start.2 = (bf16[2368,1024]{1,0:T(8,128)(2,1)}, bf16[2368,1024]{1,0:T(8,128)(2,1)S(1)}, u32[]{:S(2)}) copy-start(bf16[2368,1024]{1,0:T(8,128)(2,1)S(1)} %constant_dynamic-update-slice_fusion.8) | copy-start | bytes 14548996

commit v13 on v11

--- a/solution.py
+++ b/solution.py
@@ -71,9 +71,17 @@
     y = lax.axis_index("y")
     slots = jnp.zeros((ny,) + v.shape, v.dtype)
     slots = lax.dynamic_update_index_in_dim(slots, v, y, 0)
-    for s in range(1, ny):
-        got = lax.ppermute(v, "y", [(i, (i - s) % ny) for i in range(ny)])
-        slots = lax.dynamic_update_index_in_dim(slots, got, (y + s) % ny, 0)
+
+    def shift(a, s):
+        return lax.ppermute(a, "y", [(i, (i - s) % ny) for i in range(ny)])
+
+    if ny == 4:
+        plus = shift(v, 1)
+        got = [(plus, 1), (shift(v, -1), 3), (shift(plus, 1), 2)]
+    else:
+        got = [(shift(v, s), s) for s in range(1, ny)]
+    for value, s in got:
+        slots = lax.dynamic_update_index_in_dim(slots, value, (y + s) % ny, 0)
     total = slots[0]
     for k in range(1, ny):
         total = total + slots[k]

time: 122 us -> 126 us (1.033)
  waiting for transfers between devices: 26 us -> 29.4 us
    ppermute x3, waiting for transfers between devices: 2.83 us -> 5.93 us  [shift(): return lax.ppermute(a, 'y', [(i, (i - s) % ny) for i in range(ny)])]
  transfers between devices with their start and end apart: 14 -> 14, of which waited for: 7 -> 9; matrix products, arithmetic and copies ran while one was open for 8% -> 8% of each run, Pallas kernels for 0% -> 0%
where the time goes in v13:
time: 126 us
  blocking collectives  51.6 us (41%)
  waiting for transfers between devices  29.4 us (23%)
  starting transfers between devices  24 us (19%)
  local copies, waits for them, and re-layouts  14.7 us (12%)
  other arithmetic  4.24 us (3%)
    all_to_all x1, blocking collectives, dp_sum(): y = lax.all_to_all(x.reshape(nx, part, cols), 'x', 0, 0, tiled=False).sum(0)  19.9 us
    all_to_all x1, blocking collectives, dp_sum(): lax.all_to_all(y.reshape(nz, padded // nz, cols), 'z', 0, 0, tiled=False)  19.2 us
    all_to_all x1, blocking collectives, dp_sum(): lax.all_to_all(jnp.broadcast_to(y[None], (nz,) + y.shape), 'z', 0, 0, til...  12.5 us
    all_to_all x1, waiting for transfers between devices, dp_sum(): lax.all_to_all(jnp.broadcast_to(y[None], (nx,) + y.shape), 'x', 0, 0, til...  11.7 us
    ppermute x4, waiting for transfers between devices, shift(): return lax.ppermute(v, 'y', [(i, (i - s) % ny) for i in range(ny)])  10.7 us
    ppermute x5, starting transfers between devices, tensor_gather(): others = [lax.ppermute(mine, 'core', swap) for mine, _, _ in pieces]  7.97 us
    another operation x1, local copies, waits for them, and re-layouts, tensor_gather(): out = jnp.tile(others[0], (1, 2 * ny))  6.28 us
    ppermute x3, waiting for transfers between devices, shift(): return lax.ppermute(a, 'y', [(i, (i - s) % ny) for i in range(ny)])  5.93 us
  transfers between devices with their start and end apart: 14, of which 9 were waited for; matrix products, arithmetic and copies ran while one was open for 8% of the time, Pallas kernels for 0%

profile of v13, /device:TPU:1, one launch (start us, length us, event | category | flops | bytes accessed | tf_op | source)
XLA Modules:
  0.0 125.7 jit_solution(10983150365209942507)
XLA Ops:
  0.6 19.9 %all_to_all.20 = f32[4,592,128]{2,1,0:T(8,128)S(1)} all-to-all(f32[4,592,128]{2,1,0:T(8,128)} %bitcast.33), channel_id=1, replica_groups=mesh['z'=8,'x'=4,'y'=4,'core'=2] {'x'}, dimensions={0} | all-to-all | bytes 2424832 | tf_op jit(solution)/shard_map/all_to_all | solution.py:57
  20.7 19.2 %all_to_all.21 = f32[8,80,128]{2,1,0:T(8,128)S(1)} all-to-all(f32[8,80,128]{2,1,0:T(8,128)S(1)} %bitcast.31), channel_id=1, replica_groups=mesh['z'=8,'x'=4,'y'=4,'core'=2] {'z'}, dimensions={0} | all-to-all | bytes 655360 | tf_op jit(solution)/shard_map/all_to_all | solution.py:59
  39.9 12.5 %all_to_all.22 = f32[8,80,128]{2,1,0:T(8,128)S(1)} all-to-all(f32[8,80,128]{2,1,0:T(8,128)S(1)} %broadcast_in_dim.40), channel_id=1, replica_groups=mesh['z'=8,'x'=4,'y'=4,'core'=2] {'z'}, dimensions={0} | all-to-all | bytes 655360 | tf_op jit(solution)/shard_map/all_to_all | solution.py:60
  52.5 1.1 broadcast_in_dim.41
  53.6 3.5 %all-to-all-start.3 = ((f32[4,592,128]{2,1,0:T(8,128)}), f32[4,592,128]{2,1,0:T(8,128)S(1)}, u32[]{:S(2)}, u32[]{:S(2)}) async-start(f32[4,592,128]{2,1,0:T(8,128)} %broadcast_in_dim.41), calls=%async_computation.3 | async-start | bytes 2424832 | tf_op jit(solution)/shard_map/all_to_all | solution.py:62
  57.3 11.7 %all-to-all-done.3 = f32[4,592,128]{2,1,0:T(8,128)S(1)} async-done(((f32[4,592,128]{2,1,0:T(8,128)}), f32[4,592,128]{2,1,0:T(8,128)S(1)}, u32[]{:S(2)}, u32[]{:S(2)}) %all-to-all-start.3) | async-done | bytes 1212448 | tf_op jit(solution)/shard_map/all_to_all | solution.py:62
  69.0 0.2 broadcast_multiply_fusion
  69.2 1.1 copy-done.5
  70.3 0.4 bitcast_add_fusion
  70.7 0.9 copy-done.3
  71.6 1.3 %multiply_reduce_fusion = (f32[2368]{0:T(1024)S(1)}, f32[2368,128]{1,0:T(8,128)S(1)}, f32[2368]{0:T(1024)S(1)}) fusion(f32[2368,128]{1,0:T(8,128)S(1)} %copy-done.3, f32[2368]{0:T(1024)S(1)} %fusion.1, f32[2368,128]{1,0:T(8,128)S(1)} %get-tuple-element.16, f32[2368,128]{1,0:T(8,128)S(1)} %get-tuple-element.17), kind=kLoop, calls=%fused_computation.4 | loop fusion | flops 3026304 | bytes 4878080 | tf_op jit(solution)/shard_map/reduce_sum | solution.py:32
  72.9 0.1 convolution_bitcast_fusion
  73.0 0.2 convolution_bitcast_fusion.1
  73.2 0.1 pad_maximum_fusion
  73.4 5.9 %collective-permute-start = (f32[8]{0:T(128)S(1)}, f32[8]{0:T(128)S(1)}, u32[]{:S(2)}, u32[]{:S(2)}) collective-permute-start(f32[8]{0:T(128)S(1)} %pad_maximum_fusion), channel_id=1, source_target_pairs={{0,1},{1,0},{2,3},{3,2},{4,5},{5,4},{6,7},{7,6},{8,9},{9,8},{10,11... | collective-permute-start | bytes 104 | tf_op jit(solution)/shard_map/ppermute | solution.py:68
  79.2 0.8 collective-permute-done
  80.1 2.7 %collective-permute-start.1 = (f32[8]{0:T(128)S(1)}, f32[8]{0:T(128)S(1)}, u32[]{:S(2)}, u32[]{:S(2)}) collective-permute-start(f32[8]{0:T(128)S(1)} %fusion.11), channel_id=1, source_target_pairs={{0,6},{2,0},{4,2},{6,4},{1,7},{3,1},{5,3},{7,5},{8,14},{10,8},{12,... | collective-permute-start | bytes 104 | tf_op jit(solution)/shard_map/ppermute | solution.py:76
  82.9 0.7 collective-permute-done.1
  83.6 2.9 %collective-permute-done.2 = f32[8]{0:T(128)S(1)} collective-permute-done((f32[8]{0:T(128)S(1)}, f32[8]{0:T(128)S(1)}, u32[]{:S(2)}, u32[]{:S(2)}) %collective-permute-start.2) | collective-permute-done | bytes 64 | tf_op jit(solution)/shard_map/ppermute | solution.py:76
  86.5 0.1 collective-permute-start.3
  86.7 2.4 %collective-permute-done.3 = f32[8]{0:T(128)S(1)} collective-permute-done((f32[8]{0:T(128)S(1)}, f32[8]{0:T(128)S(1)}, u32[]{:S(2)}, u32[]{:S(2)}) %collective-permute-start.3) | collective-permute-done | bytes 64 | tf_op jit(solution)/shard_map/ppermute | solution.py:76
  89.1 0.3 convolution_reduce_fusion
  89.4 1.4 %fusion.3 = (bf16[2368,128]{1,0:T(8,128)(2,1)S(1)}, f32[2368,128]{1,0:T(8,128)}) fusion(f32[2368,128]{1,0:T(8,128)S(1)} %copy-done.3, f32[2368,128]{1,0:T(8,128)S(1)} %get-tuple-element.8, f32[2368]{0:T(1024)S(1)} %broadcast_multiply_fusion.1), kind=kLoop, calls=%fused_computation.34 | loop fusion | flops 909312 | bytes 4252928 | tf_op jit(solution)/shard_map/convert_element_type | solution.py:127
  90.8 2.9 %collective-permute-start.4 = (bf16[2368,128]{1,0:T(8,128)(2,1)S(1)}, bf16[2368,128]{1,0:T(8,128)(2,1)S(1)}, u32[]{:S(2)}, u32[]{:S(2)}) collective-permute-start(bf16[2368,128]{1,0:T(8,128)(2,1)S(1)} %get-tuple-element.5), channel_id=1, source_target_pairs={{0,1},{1,0},{2,3},{3,2},{4,5},{5,4},{6,7},{7,6},{8,9},{9,8},{10,11... | collective-permute-start | bytes 1818632 | tf_op jit(solution)/shard_map/ppermute | solution.py:106
  93.7 1.0 collective-permute-start.5
  94.7 0.5 collective-permute-start.7
  95.2 0.6 fusion.10
  95.7 6.3 %tile.4 = bf16[2368,8,128]{2,1,0:T(8,128)(2,1)S(1)} broadcast(bf16[2368,128]{1,0:T(8,128)(2,1)S(1)} %collective-permute-done.4), dimensions={0,2} | broadcast | bytes 5455872 | tf_op jit(solution)/shard_map/tile | solution.py:107
  102.0 1.3 copy.11
  103.3 5.6 %collective-permute-done.5 = bf16[2368,128]{1,0:T(8,128)(2,1)S(1)} collective-permute-done((bf16[2368,128]{1,0:T(8,128)(2,1)S(1)}, bf16[2368,128]{1,0:T(8,128)(2,1)S(1)}, u32[]{:S(2)}, u32[]{:S(2)}) %collective-permute-start.5) | collective-permute-done | bytes 606240 | tf_op jit(solution)/shard_map/ppermute | solution.py:98
  108.9 2.3 %collective-permute-start.9 = (bf16[1184,128]{1,0:T(8,128)(2,1)S(1)}, bf16[1184,128]{1,0:T(8,128)(2,1)S(1)}, u32[]{:S(2)}, u32[]{:S(2)}) collective-permute-start(bf16[1184,128]{1,0:T(8,128)(2,1)S(1)} %slice.49), channel_id=1, source_target_pairs={{0,6},{2,0},{4,2},{6,4},{1,7},{3,1},{5,3},{7,5},{8,14},{10,8},{12,... | collective-permute-start | bytes 909320 | tf_op jit(solution)/shard_map/ppermute | solution.py:98
  111.3 0.2 constant_dynamic-update-slice_fusion.7
  111.5 1.2 collective-permute-start.6
  112.8 0.1 collective-permute-start.8
  112.9 0.2 constant_dynamic-update-slice_fusion.6
  113.1 0.2 constant_dynamic-update-slice_fusion.5
  113.3 3.6 %collective-permute-done.9 = bf16[1184,128]{1,0:T(8,128)(2,1)S(1)} collective-permute-done((bf16[1184,128]{1,0:T(8,128)(2,1)S(1)}, bf16[1184,128]{1,0:T(8,128)(2,1)S(1)}, u32[]{:S(2)}, u32[]{:S(2)}) %collective-permute-start.9) | collective-permute-done | bytes 303136 | tf_op jit(solution)/shard_map/ppermute | solution.py:98
  116.9 1.7 %collective-permute-start.10 = (bf16[1184,128]{1,0:T(8,128)(2,1)S(1)}, bf16[1184,128]{1,0:T(8,128)(2,1)S(1)}, u32[]{:S(2)}, u32[]{:S(2)}) collective-permute-start(bf16[1184,128]{1,0:T(8,128)(2,1)S(1)} %collective-permute-done.9), channel_id=1, source_target_pairs={{0,1},{1,0},{2,3},{3,2},{4,5},{5,4},{6,7},{7,6},{8,9},{9,8},{10,11... | collective-permute-start | bytes 909320 | tf_op jit(solution)/shard_map/ppermute | solution.py:106
  118.6 1.5 %collective-permute-done.11 = bf16[1184,128]{1,0:T(8,128)(2,1)S(1)} collective-permute-done((bf16[1184,128]{1,0:T(8,128)(2,1)S(1)}, bf16[1184,128]{1,0:T(8,128)(2,1)S(1)}, u32[]{:S(2)}, u32[]{:S(2)}) %collective-permute-start.11) | collective-permute-done | bytes 303136 | tf_op jit(solution)/shard_map/ppermute | solution.py:98
  120.1 2.0 %collective-permute-start.12 = (bf16[1184,128]{1,0:T(8,128)(2,1)S(1)}, bf16[1184,128]{1,0:T(8,128)(2,1)S(1)}, u32[]{:S(2)}, u32[]{:S(2)}) collective-permute-start(bf16[1184,128]{1,0:T(8,128)(2,1)S(1)} %collective-permute-done.11), channel_id=1, source_target_pairs={{0,1},{1,0},{2,3},{3,2},{4,5},{5,4},{6,7},{7,6},{8,9},{9,8},{10,11... | collective-permute-start | bytes 909320 | tf_op jit(solution)/shard_map/ppermute | solution.py:106
  122.1 0.2 constant_dynamic-update-slice_fusion.4
  122.3 0.2 constant_dynamic-update-slice_fusion.3
  122.6 0.2 constant_dynamic-update-slice_fusion.2
  122.8 0.1 constant_dynamic-update-slice_fusion.1
  122.9 0.1 constant_dynamic-update-slice_fusion
  123.0 0.1 constant_dynamic-update-slice_fusion.9
  123.1 0.2 collective-permute-done.12
  123.5 2.2 %copy-done.2 = bf16[2368,1024]{1,0:T(8,128)(2,1)} copy-done((bf16[2368,1024]{1,0:T(8,128)(2,1)}, bf16[2368,1024]{1,0:T(8,128)(2,1)S(1)}, u32[]{:S(2)}) %copy-start.2) | copy-done | bytes 4849688
  (38 shorter events, 0.8 us)
Async XLA Ops:
  53.6 15.5 %all-to-all-start.3 = ((f32[4,592,128]{2,1,0:T(8,128)}), f32[4,592,128]{2,1,0:T(8,128)S(1)}, u32[]{:S(2)}, u32[]{:S(2)}) async-start(f32[4,592,128]{2,1,0:T(8,128)} %broadcast_in_dim.41), calls=%async_computation.3 | async-start | bytes 2424832 | tf_op jit(solution)/shard_map/all_to_all | solution.py:62
  57.3 12.0 %copy-start.4 = (f32[2368,128]{1,0:T(8,128)S(1)}, f32[2368,128]{1,0:T(8,128)}, u32[]{:S(2)}) copy-start(f32[2368,128]{1,0:T(8,128)} %param.7) | copy-start | bytes 3637252
  69.0 1.3 %copy-start.5 = (f32[2368,128]{1,0:T(8,128)S(1)}, f32[2368,128]{1,0:T(8,128)}, u32[]{:S(2)}) copy-start(f32[2368,128]{1,0:T(8,128)} %param.6) | copy-start | bytes 3637252
  70.3 1.3 %copy-start.3 = (f32[2368,128]{1,0:T(8,128)S(1)}, f32[2368,128]{1,0:T(8,128)}, u32[]{:S(2)}) copy-start(f32[2368,128]{1,0:T(8,128)} %param.5) | copy-start | bytes 3637252
  70.7 2.2 %copy-start = (f32[2368,128]{1,0:T(8,128)}, f32[2368,128]{1,0:T(8,128)S(1)}, u32[]{:S(2)}) copy-start(f32[2368,128]{1,0:T(8,128)S(1)} %get-tuple-element.16) | copy-start | bytes 3637252
  70.7 2.2 %copy-start.1 = (f32[2368,128]{1,0:T(8,128)}, f32[2368,128]{1,0:T(8,128)S(1)}, u32[]{:S(2)}) copy-start(f32[2368,128]{1,0:T(8,128)S(1)} %get-tuple-element.17) | copy-start | bytes 3637252
  73.4 6.7 %collective-permute-start = (f32[8]{0:T(128)S(1)}, f32[8]{0:T(128)S(1)}, u32[]{:S(2)}, u32[]{:S(2)}) collective-permute-start(f32[8]{0:T(128)S(1)} %pad_maximum_fusion), channel_id=1, source_target_pairs={{0,1},{1,0},{2,3},{3,2},{4,5},{5,4},{6,7},{7,6},{8,9},{9,8},{10,11... | collective-permute-start | bytes 104 | tf_op jit(solution)/shard_map/ppermute | solution.py:68
  80.1 3.5 %collective-permute-start.1 = (f32[8]{0:T(128)S(1)}, f32[8]{0:T(128)S(1)}, u32[]{:S(2)}, u32[]{:S(2)}) collective-permute-start(f32[8]{0:T(128)S(1)} %fusion.11), channel_id=1, source_target_pairs={{0,6},{2,0},{4,2},{6,4},{1,7},{3,1},{5,3},{7,5},{8,14},{10,8},{12,... | collective-permute-start | bytes 104 | tf_op jit(solution)/shard_map/ppermute | solution.py:76
  82.9 3.6 %collective-permute-start.2 = (f32[8]{0:T(128)S(1)}, f32[8]{0:T(128)S(1)}, u32[]{:S(2)}, u32[]{:S(2)}) collective-permute-start(f32[8]{0:T(128)S(1)} %fusion.11), channel_id=1, source_target_pairs={{0,2},{2,4},{4,6},{6,0},{1,3},{3,5},{5,7},{7,1},{8,10},{10,12},{12... | collective-permute-start | bytes 104 | tf_op jit(solution)/shard_map/ppermute | solution.py:76
  86.5 2.5 %collective-permute-start.3 = (f32[8]{0:T(128)S(1)}, f32[8]{0:T(128)S(1)}, u32[]{:S(2)}, u32[]{:S(2)}) collective-permute-start(f32[8]{0:T(128)S(1)} %collective-permute-done.1), channel_id=1, source_target_pairs={{0,6},{2,0},{4,2},{6,4},{1,7},{3,1},{5,3},{7,5},{8,14},{10,8},{12,... | collective-permute-start | bytes 104 | tf_op jit(solution)/shard_map/ppermute | solution.py:76
  90.8 5.0 %collective-permute-start.4 = (bf16[2368,128]{1,0:T(8,128)(2,1)S(1)}, bf16[2368,128]{1,0:T(8,128)(2,1)S(1)}, u32[]{:S(2)}, u32[]{:S(2)}) collective-permute-start(bf16[2368,128]{1,0:T(8,128)(2,1)S(1)} %get-tuple-element.5), channel_id=1, source_target_pairs={{0,1},{1,0},{2,3},{3,2},{4,5},{5,4},{6,7},{7,6},{8,9},{9,8},{10,11... | collective-permute-start | bytes 1818632 | tf_op jit(solution)/shard_map/ppermute | solution.py:106
  93.7 15.2 %collective-permute-start.5 = (bf16[2368,128]{1,0:T(8,128)(2,1)S(1)}, bf16[2368,128]{1,0:T(8,128)(2,1)S(1)}, u32[]{:S(2)}, u32[]{:S(2)}) collective-permute-start(bf16[2368,128]{1,0:T(8,128)(2,1)S(1)} %get-tuple-element.5), channel_id=1, source_target_pairs={{0,6},{2,0},{4,2},{6,4},{1,7},{3,1},{5,3},{7,5},{8,14},{10,8},{12,... | collective-permute-start | bytes 1818632 | tf_op jit(solution)/shard_map/ppermute | solution.py:98
  94.7 16.5 %collective-permute-start.7 = (bf16[2368,128]{1,0:T(8,128)(2,1)S(1)}, bf16[2368,128]{1,0:T(8,128)(2,1)S(1)}, u32[]{:S(2)}, u32[]{:S(2)}) collective-permute-start(bf16[2368,128]{1,0:T(8,128)(2,1)S(1)} %get-tuple-element.5), channel_id=1, source_target_pairs={{0,2},{2,4},{4,6},{6,0},{1,3},{3,5},{5,7},{7,1},{8,10},{10,12},{12... | collective-permute-start | bytes 1818632 | tf_op jit(solution)/shard_map/ppermute | solution.py:98
  108.9 8.0 %collective-permute-start.9 = (bf16[1184,128]{1,0:T(8,128)(2,1)S(1)}, bf16[1184,128]{1,0:T(8,128)(2,1)S(1)}, u32[]{:S(2)}, u32[]{:S(2)}) collective-permute-start(bf16[1184,128]{1,0:T(8,128)(2,1)S(1)} %slice.49), channel_id=1, source_target_pairs={{0,6},{2,0},{4,2},{6,4},{1,7},{3,1},{5,3},{7,5},{8,14},{10,8},{12,... | collective-permute-start | bytes 909320 | tf_op jit(solution)/shard_map/ppermute | solution.py:98
  111.2 8.9 %collective-permute-start.11 = (bf16[1184,128]{1,0:T(8,128)(2,1)S(1)}, bf16[1184,128]{1,0:T(8,128)(2,1)S(1)}, u32[]{:S(2)}, u32[]{:S(2)}) collective-permute-start(bf16[1184,128]{1,0:T(8,128)(2,1)S(1)} %slice.50), channel_id=1, source_target_pairs={{0,2},{2,4},{4,6},{6,0},{1,3},{3,5},{5,7},{7,1},{8,10},{10,12},{12... | collective-permute-start | bytes 909320 | tf_op jit(solution)/shard_map/ppermute | solution.py:98
  111.5 10.6 %collective-permute-start.6 = (bf16[2368,128]{1,0:T(8,128)(2,1)S(1)}, bf16[2368,128]{1,0:T(8,128)(2,1)S(1)}, u32[]{:S(2)}, u32[]{:S(2)}) collective-permute-start(bf16[2368,128]{1,0:T(8,128)(2,1)S(1)} %collective-permute-done.5), channel_id=1, source_target_pairs={{0,1},{1,0},{2,3},{3,2},{4,5},{5,4},{6,7},{7,6},{8,9},{9,8},{10,11... | collective-permute-start | bytes 1818632 | tf_op jit(solution)/shard_map/ppermute | solution.py:106
  112.8 9.8 %collective-permute-start.8 = (bf16[2368,128]{1,0:T(8,128)(2,1)S(1)}, bf16[2368,128]{1,0:T(8,128)(2,1)S(1)}, u32[]{:S(2)}, u32[]{:S(2)}) collective-permute-start(bf16[2368,128]{1,0:T(8,128)(2,1)S(1)} %collective-permute-done.7), channel_id=1, source_target_pairs={{0,1},{1,0},{2,3},{3,2},{4,5},{5,4},{6,7},{7,6},{8,9},{9,8},{10,11... | collective-permute-start | bytes 1818632 | tf_op jit(solution)/shard_map/ppermute | solution.py:106
  116.9 6.0 %collective-permute-start.10 = (bf16[1184,128]{1,0:T(8,128)(2,1)S(1)}, bf16[1184,128]{1,0:T(8,128)(2,1)S(1)}, u32[]{:S(2)}, u32[]{:S(2)}) collective-permute-start(bf16[1184,128]{1,0:T(8,128)(2,1)S(1)} %collective-permute-done.9), channel_id=1, source_target_pairs={{0,1},{1,0},{2,3},{3,2},{4,5},{5,4},{6,7},{7,6},{8,9},{9,8},{10,11... | collective-permute-start | bytes 909320 | tf_op jit(solution)/shard_map/ppermute | solution.py:106
  120.1 3.2 %collective-permute-start.12 = (bf16[1184,128]{1,0:T(8,128)(2,1)S(1)}, bf16[1184,128]{1,0:T(8,128)(2,1)S(1)}, u32[]{:S(2)}, u32[]{:S(2)}) collective-permute-start(bf16[1184,128]{1,0:T(8,128)(2,1)S(1)} %collective-permute-done.11), channel_id=1, source_target_pairs={{0,1},{1,0},{2,3},{3,2},{4,5},{5,4},{6,7},{7,6},{8,9},{9,8},{10,11... | collective-permute-start | bytes 909320 | tf_op jit(solution)/shard_map/ppermute | solution.py:106
  123.4 2.2 %copy-start.2 = (bf16[2368,1024]{1,0:T(8,128)(2,1)}, bf16[2368,1024]{1,0:T(8,128)(2,1)S(1)}, u32[]{:S(2)}) copy-start(bf16[2368,1024]{1,0:T(8,128)(2,1)S(1)} %constant_dynamic-update-slice_fusion.8) | copy-start | bytes 14548996
